TPU v7x, 256 devices: a whole 4x4x8 slice. The times are simulated.
256 devices in a mesh: wide: 32 (over y, x, core), narrow: 8 (over z).
Axes of the slice: x: 4, y: 4, z: 8, core: 2. Of those that a mesh axis runs over, the one named last changes fastest.
Arguments:
- up_grads: float32 [32, 192, 11008], P('wide', 'narrow'), may hold values from -6 to 6, as said below
- down_grads: float32 [32, 512, 4096], P('wide', 'narrow'), may hold values from -6 to 6, as said below
- gain_grads: float32 [32, 4096], P('wide', 'narrow'), may hold values from -6 to 6
- up_master: float32 [192, 11008], P('narrow', 'wide'), may hold values from -60 to 60, as said below
- down_master: float32 [512, 4096], P('narrow', 'wide'), may hold values from -60 to 60, as said below
- gain_master: float32 [4096], P(('narrow', 'wide')), may hold values from 0.5 to 1.5
- up_first: float32 [192, 11008], P('narrow', 'wide'), may hold values from -1.8 to 1.8, as said below
- down_first: float32 [512, 4096], P('narrow', 'wide'), may hold values from -1.8 to 1.8, as said below
- gain_first: float32 [4096], P(('narrow', 'wide')), may hold values from -4 to 4
- up_second: float32 [192, 11008], P('narrow', 'wide'), may hold values from 0.01 to 1
- down_second: float32 [512, 4096], P('narrow', 'wide'), may hold values from 0.01 to 1
- gain_second: float32 [4096], P(('narrow', 'wide')), may hold values from 0.01 to 1
Outputs:
- up_first_new: float32 [192, 11008], P('narrow', 'wide')
- up_second_new: float32 [192, 11008], P('narrow', 'wide')
- up_master_new: float32 [192, 11008], P('narrow', 'wide')
- up_weights: bfloat16 [192, 11008], replicated
- down_first_new: float32 [512, 4096], P('narrow', 'wide')
- down_second_new: float32 [512, 4096], P('narrow', 'wide')
- down_master_new: float32 [512, 4096], P('narrow', 'wide')
- down_weights: bfloat16 [512, 4096], replicated
- gain_first_new: float32 [4096], P(('narrow', 'wide'))
- gain_second_new: float32 [4096], P(('narrow', 'wide'))
- gain_master_new: float32 [4096], P(('narrow', 'wide'))
- gain_weights: bfloat16 [4096], replicated
Inputs may be any that keep to these rules, and one draw needn't show every extreme that they name: `up_master`: finite real entries. `down_master`: finite real entries. `up_grads`: finite real entries. `down_grads`: finite real entries. `up_first`: finite real entries. `down_first`: finite real entries.
All inputs are finite; a program needn't handle non-finite values.
Results may differ from a plain program's by a relative error of at most 0.001.
Values may be sent and summed in bfloat16 or wider, within the bound.
No kernel may reach another device: no remote copies, remote signals or barrier semaphores. Data moves between devices by JAX's collectives and lax.ppermute only.
A program may use at most 64 MiB of HBM per device.

v0:
```python
import jax
import jax.numpy as jnp
from jax import lax
from jax.sharding import PartitionSpec as P

BETA_ONE = 0.9
BETA_TWO = 0.999
EPSILON = 1e-06
LEARN_RATE = 0.05
DECAY_RATE = 0.01
CORRECT_FIRST = 1.0 - 0.9**10
CORRECT_SECOND = 1.0 - 0.999**10


def moments(grad_sum, master, first, second, decay):
    first_new = BETA_ONE * first + (1.0 - BETA_ONE) * grad_sum
    second_new = BETA_TWO * second + (1.0 - BETA_TWO) * grad_sum * grad_sum
    update = (
        first_new / CORRECT_FIRST / (jnp.sqrt(second_new / CORRECT_SECOND) + EPSILON)
        + decay * master
    )
    return (first_new, second_new, update)


def finish(master, update, weight_sq, update_sq):
    trust = jnp.sqrt(weight_sq) / (jnp.sqrt(update_sq) + EPSILON)
    return master - LEARN_RATE * trust * update


def body(
    up_grads,
    down_grads,
    gain_grads,
    up_master,
    down_master,
    gain_master,
    up_first,
    down_first,
    gain_first,
    up_second,
    down_second,
    gain_second,
):
    weight_sums = lax.psum(
        (
            jnp.sum(up_master * up_master),
            jnp.sum(down_master * down_master),
            jnp.sum(gain_master * gain_master),
        ),
        ("wide", "narrow"),
    )
    up_sum, down_sum, gain_sum = (
        lax.psum_scatter(up_grads[0], "wide", scatter_dimension=1, tiled=True),
        lax.psum_scatter(down_grads[0], "wide", scatter_dimension=1, tiled=True),
        lax.psum_scatter(gain_grads, "wide", scatter_dimension=1, tiled=True),
    )
    gain_sum = gain_sum.reshape(gain_master.shape)
    up_first_new, up_second_new, up_update = moments(
        up_sum, up_master, up_first, up_second, DECAY_RATE
    )
    down_first_new, down_second_new, down_update = moments(
        down_sum, down_master, down_first, down_second, DECAY_RATE
    )
    gain_first_new, gain_second_new, gain_update = moments(
        gain_sum, gain_master, gain_first, gain_second, 0.0
    )
    update_sums = lax.psum(
        (
            jnp.sum(up_update * up_update),
            jnp.sum(down_update * down_update),
            jnp.sum(gain_update * gain_update),
        ),
        ("wide", "narrow"),
    )
    up_master_new = finish(up_master, up_update, weight_sums[0], update_sums[0])
    down_master_new = finish(down_master, down_update, weight_sums[1], update_sums[1])
    gain_master_new = finish(gain_master, gain_update, weight_sums[2], update_sums[2])
    up_low = up_master_new.astype(jnp.bfloat16)
    down_low = down_master_new.astype(jnp.bfloat16)
    gain_low = gain_master_new.astype(jnp.bfloat16).reshape(1, -1)
    rows_up, rows_down, rows_gain = (
        lax.all_gather(up_low, "narrow", axis=0, tiled=True),
        lax.all_gather(down_low, "narrow", axis=0, tiled=True),
        lax.all_gather(gain_low, "narrow", axis=0, tiled=True),
    )
    up_weights, down_weights, gain_whole = (
        lax.all_gather(rows_up, "wide", axis=1, tiled=True),
        lax.all_gather(rows_down, "wide", axis=1, tiled=True),
        lax.all_gather(rows_gain, "wide", axis=1, tiled=True),
    )
    gain_weights = gain_whole.reshape(-1)
    return (
        up_first_new,
        up_second_new,
        up_master_new,
        up_weights,
        down_first_new,
        down_second_new,
        down_master_new,
        down_weights,
        gain_first_new,
        gain_second_new,
        gain_master_new,
        gain_weights,
    )


def solution(mesh):
    return jax.shard_map(
        body,
        mesh=mesh,
        in_specs=(
            P("wide", "narrow", None),
            P("wide", "narrow", None),
            P("wide", "narrow"),
            P("narrow", "wide"),
            P("narrow", "wide"),
            P(("narrow", "wide")),
            P("narrow", "wide"),
            P("narrow", "wide"),
            P(("narrow", "wide")),
            P("narrow", "wide"),
            P("narrow", "wide"),
            P(("narrow", "wide")),
        ),
        out_specs=(
            P("narrow", "wide"),
            P("narrow", "wide"),
            P("narrow", "wide"),
            P(),
            P("narrow", "wide"),
            P("narrow", "wide"),
            P("narrow", "wide"),
            P(),
            P(("narrow", "wide")),
            P(("narrow", "wide")),
            P(("narrow", "wide")),
            P(),
        ),
        check_vma=False,
    )
```

profile of v0, /device:TPU:1, one launch (start us, length us, event | category | flops | bytes accessed | tf_op | source)
XLA Modules:
  0.0 547.5 jit_solution(11987130565649515625)
XLA Ops:
  7.2 0.0 reduce-scatter.8.cloned.1.call-start
  7.2 1.5 copy.32
  8.8 0.0 reduce-scatter.8.cloned.1.call-update
  8.8 0.0 all-reduce.5.cloned.1.call-start
  8.8 0.7 all-reduce.5.cloned.1.call-update
  9.5 0.0 reduce-scatter.6.cloned.1.call-start
  9.6 0.7 reduce-scatter.6.cloned.1.call-update
  10.3 0.0 all-gather.6.cloned.1.call-start
  10.3 1.3 dynamic-slice.1
  12.2 86.8 %reduce-scatter.8.cloned.1.call-done = f32[16,1]{1,0:T(8,128)} async-done(((f32[512,1]{1,0:T(8,128)}), f32[16,1]{1,0:T(8,128)}) %reduce-scatter.8.cloned.1.call-update) | async-done | bytes 80
  99.1 0.8 copy.33
  99.9 1.8 multiply_reduce_fusion.4
  101.7 117.2 %all-reduce.5.cloned.1.call-done = f32[24,11008]{1,0:T(8,128)} async-done(((f32[24,11008]{1,0:T(8,128)}), f32[24,11008]{1,0:T(8,128)}) %all-reduce.5.cloned.1.call-update) | async-done | bytes 1056784
  218.9 1.5 multiply_reduce_fusion
  220.4 0.0 copy-start
  220.5 0.0 copy-start.1
  220.5 86.1 %reduce-scatter.6.cloned.1.call-done = f32[64,128]{1,0:T(8,128)} async-done(((f32[64,4096]{1,0:T(8,128)}), f32[64,128]{1,0:T(8,128)}) %reduce-scatter.6.cloned.1.call-update) | async-done | bytes 32784 | tf_op jit(solution)/shard_map/reduce_scatter | solution.py:54
  306.6 1.5 multiply_reduce_fusion.2
  308.0 0.0 copy-start.2
  308.0 0.0 copy-start.3
  308.0 77.8 %all-reduce.2 = (f32[]{:T(128)}, f32[]{:T(128)}, f32[]{:T(128)}, f32[]{:T(128)}, f32[]{:T(128)}, /*index=5*/f32[]{:T(128)}) all-reduce(f32[]{:T(128)} %get-tuple-element.13, f32[]{:T(128)} %get-tuple-element.12, f32[]{:T(128)} %get-tuple-element.15, f32[]{:T(128)} %get-tuple-element.14, ...), channel_id=1, replica_groups=mesh['wide'=32,'narrow'=8] {'wide','narrow'}, use_global_device_ids=true, to_apply=%region_2.0 | all-reduce | flops 6 | bytes 48 | tf_op jit(solution)/shard_map/psum | solution.py:44
  387.2 1.4 fusion.5
  388.6 20.2 %all_gather.20 = bf16[512,128]{1,0:T(8,128)(2,1)} all-gather(bf16[64,128]{1,0:T(8,128)(2,1)S(1)} %get-tuple-element.24), channel_id=1, replica_groups=mesh['wide'=32,'narrow'=8] {'narrow'}, dimensions={0}, use_global_device_ids=true | all-gather | bytes 147456 | tf_op jit(solution)/shard_map/all_gather | solution.py:83
  408.9 0.0 all-gather.6.cloned.1.call-update
  408.9 0.0 all-gather.8.cloned.1.call-start
  410.4 1.4 fusion.6
  411.8 20.2 %all_gather.18 = bf16[192,344]{1,0:T(8,128)(2,1)} all-gather(bf16[24,344]{1,0:T(8,128)(2,1)S(1)} %get-tuple-element.26), channel_id=1, replica_groups=mesh['wide'=32,'narrow'=8] {'narrow'}, dimensions={0}, use_global_device_ids=true | all-gather | bytes 148608 | tf_op jit(solution)/shard_map/all_gather | solution.py:82
  432.0 0.0 all-gather.8.cloned.1.call-update
  432.0 1.3 dynamic-slice
  435.4 1.2 fusion.4
  436.6 0.2 dynamic-update-slice
  436.7 12.4 %all-reduce = bf16[128]{0:T(256)(128)(2,1)S(1)} all-reduce(bf16[128]{0:T(256)(128)(2,1)S(1)} %dynamic-update-slice), channel_id=2, replica_groups=mesh['wide'=32,'narrow'=8] {'narrow'}, use_global_device_ids=true, to_apply=%add | all-reduce | flops 128 | bytes 512
  449.2 0.1 reshape.36
  449.3 38.6 %all-gather.2 = bf16[32,16,8]{1,2,0:T(8,128)(2,1)S(1)} all-gather(bf16[1,16,8]{1,2,0:T(8,128)(2,1)S(1)} %bitcast.35), channel_id=1, replica_groups=mesh['wide'=32,'narrow'=8] {'wide'}, dimensions={0}, use_global_device_ids=true | all-gather | bytes 8448 | tf_op jit(solution)/shard_map/all_gather | solution.py:89
  487.9 0.1 reshape.43
  488.0 0.6 copy.34
  488.6 0.0 all-gather.6.cloned.1.call-done
  488.6 30.5 %all-gather.8.cloned.1.call-done = bf16[32,344,192]{1,2,0:T(8,128)(2,1)} async-done(((bf16[1,344,192]{1,2,0:T(8,128)(2,1)}), bf16[32,344,192]{1,2,0:T(8,128)(2,1)}) %all-gather.8.cloned.1.call-update) | async-done | bytes 4227088 | tf_op jit(solution)/shard_map/all_gather | solution.py:87
  519.1 7.3 %copy.28 = bf16[32,344,192]{1,0,2:T(8,128)(2,1)} copy(bf16[32,344,192]{1,2,0:T(8,128)(2,1)} %all-gather.8.cloned.1.call-done) | data formatting | bytes 8454144 | tf_op jit(solution)/shard_map/all_gather | solution.py:87
  526.4 0.0 copy-done
  526.4 0.0 copy-done.1
  526.4 0.0 copy-done.2
  526.4 0.0 copy-done.3
  526.4 9.9 %reshape.41 = bf16[11008,192]{0,1:T(8,128)(2,1)} reshape(bf16[32,344,192]{1,0,2:T(8,128)(2,1)} %copy.28) | data formatting | bytes 8454144
  536.3 4.7 copy.39
  (2 shorter events, 0.0 us)
Async XLA Ops:
  7.2 91.9 %reduce-scatter.8.cloned.1.call-start = ((), (), s32[]{:S(2)}) async-start(), calls=%async_computation.5 | async-start | bytes 270336
  8.8 210.1 %all-reduce.5.cloned.1.call-start = ((), (), s32[]{:S(2)}) async-start(), calls=%async_computation.6 | async-start | bytes 2113536
  9.5 297.0 %reduce-scatter.6.cloned.1.call-start = ((), (), s32[]{:S(2)}) async-start(), calls=%async_computation.2 | async-start | bytes 1081344 | tf_op jit(solution)/shard_map/reduce_scatter | solution.py:54
  10.3 478.3 %all-gather.6.cloned.1.call-start = ((), (), s32[]{:S(2)}) async-start(), calls=%async_computation.3 | async-start | bytes 4325376 | tf_op jit(solution)/shard_map/all_gather | solution.py:88
  220.4 306.0 %copy-start = (f32[24,344]{1,0:T(8,128)}, f32[24,344]{1,0:T(8,128)S(1)}, u32[]{:S(2)}) copy-start(f32[24,344]{1,0:T(8,128)S(1)} %get-tuple-element.50) | copy-start | bytes 99076
  220.5 306.0 %copy-start.1 = (f32[24,344]{1,0:T(8,128)}, f32[24,344]{1,0:T(8,128)S(1)}, u32[]{:S(2)}) copy-start(f32[24,344]{1,0:T(8,128)S(1)} %get-tuple-element.49) | copy-start | bytes 99076
  308.0 218.4 %copy-start.2 = (f32[64,128]{1,0:T(8,128)}, f32[64,128]{1,0:T(8,128)S(1)}, u32[]{:S(2)}) copy-start(f32[64,128]{1,0:T(8,128)S(1)} %get-tuple-element.53) | copy-start | bytes 98308
  308.0 218.4 %copy-start.3 = (f32[64,128]{1,0:T(8,128)}, f32[64,128]{1,0:T(8,128)S(1)}, u32[]{:S(2)}) copy-start(f32[64,128]{1,0:T(8,128)S(1)} %get-tuple-element.54) | copy-start | bytes 98308
  408.9 110.2 %all-gather.8.cloned.1.call-start = ((), (), s32[]{:S(2)}) async-start(), calls=%async_computation.4 | async-start | bytes 4866048 | tf_op jit(solution)/shard_map/all_gather | solution.py:87
Sparse Core Ops, SparseCore 0:
  12.3 86.7 reduce-scatter.7
  102.4 116.4 all-reduce.4
  222.7 83.8 reduce-scatter.5
  409.0 56.2 all-gather.5
  467.7 51.3 all-gather.7
where the time goes:
time: 548 us
  waiting for transfers between devices  322 us (59%)
  blocking collectives  169 us (31%)
  local copies, waits for them, and re-layouts  27.7 us (5%)
  between operations  19.4 us (4%)
  other arithmetic  8.79 us (2%)
    unnamed x7, waiting for transfers between devices  206 us
    reduce_scatter x1, waiting for transfers between devices, body(): lax.psum_scatter(down_grads[0], 'wide', scatter_dimension=1, tiled=True)  86.1 us
    psum x1, blocking collectives, body(): lax.psum((jnp.sum(up_master * up_master), jnp.sum(down_master * down_mast...  77.8 us
    all_gather x1, blocking collectives, body(): lax.all_gather(rows_gain, 'wide', axis=1, tiled=True)  38.6 us
    all_gather x1, waiting for transfers between devices, body(): lax.all_gather(rows_up, 'wide', axis=1, tiled=True)  30.5 us
    unnamed x18, local copies, waits for them, and re-layouts  20.4 us
    all_gather x1, blocking collectives, body(): lax.all_gather(up_low, 'narrow', axis=0, tiled=True)  20.2 us
    all_gather x1, blocking collectives, body(): lax.all_gather(down_low, 'narrow', axis=0, tiled=True)  20.2 us
  transfers between devices with their start and end apart: 5, of which 4 were waited for; matrix products, arithmetic and copies ran while one was open for 2% of the time, Pallas kernels for 0%

commit v1 on v0

--- a/solution.py
+++ b/solution.py
@@ -10,6 +10,7 @@
 DECAY_RATE = 0.01
 CORRECT_FIRST = 1.0 - 0.9**10
 CORRECT_SECOND = 1.0 - 0.999**10
+LANES = 128
 
 
 def moments(grad_sum, master, first, second, decay):
@@ -27,6 +28,10 @@
     return master - LEARN_RATE * trust * update
 
 
+def padded(total):
+    return -(-total // LANES) * LANES
+
+
 def body(
     up_grads,
     down_grads,
@@ -41,20 +46,40 @@
     down_second,
     gain_second,
 ):
-    weight_sums = lax.psum(
-        (
-            jnp.sum(up_master * up_master),
-            jnp.sum(down_master * down_master),
-            jnp.sum(gain_master * gain_master),
-        ),
-        ("wide", "narrow"),
+    n_wide = lax.axis_size("wide")
+    n_narrow = lax.axis_size("narrow")
+    up_rows, up_cols = up_master.shape
+    down_rows, down_cols = down_master.shape
+    gain_cols = gain_master.shape[0]
+    up_size = up_rows * up_cols
+    down_size = down_rows * down_cols
+    total = up_size + down_size + gain_cols
+    width = padded(total)
+
+    weight_sums = (
+        jnp.sum(up_master * up_master),
+        jnp.sum(down_master * down_master),
+        jnp.sum(gain_master * gain_master),
     )
-    up_sum, down_sum, gain_sum = (
-        lax.psum_scatter(up_grads[0], "wide", scatter_dimension=1, tiled=True),
-        lax.psum_scatter(down_grads[0], "wide", scatter_dimension=1, tiled=True),
-        lax.psum_scatter(gain_grads, "wide", scatter_dimension=1, tiled=True),
-    )
-    gain_sum = gain_sum.reshape(gain_master.shape)
+
+    up_part = up_grads[0].reshape(up_rows, n_wide, up_cols).transpose(1, 0, 2)
+    down_part = down_grads[0].reshape(down_rows, n_wide, down_cols).transpose(1, 0, 2)
+    gain_part = gain_grads.reshape(n_wide, gain_cols)
+    packed = jnp.concatenate(
+        [
+            up_part.reshape(n_wide, up_size),
+            down_part.reshape(n_wide, down_size),
+            gain_part,
+            jnp.zeros((n_wide, width - total), jnp.float32),
+        ],
+        axis=1,
+    ).reshape(n_wide, width // LANES, LANES)
+    summed = lax.psum_scatter(packed, "wide", scatter_dimension=0, tiled=True)
+    summed = summed.reshape(width)
+    up_sum = summed[:up_size].reshape(up_rows, up_cols)
+    down_sum = summed[up_size : up_size + down_size].reshape(down_rows, down_cols)
+    gain_sum = summed[up_size + down_size : total]
+
     up_first_new, up_second_new, up_update = moments(
         up_sum, up_master, up_first, up_second, DECAY_RATE
     )
@@ -64,31 +89,44 @@
     gain_first_new, gain_second_new, gain_update = moments(
         gain_sum, gain_master, gain_first, gain_second, 0.0
     )
-    update_sums = lax.psum(
+    weight_sums, update_sums = lax.psum(
         (
-            jnp.sum(up_update * up_update),
-            jnp.sum(down_update * down_update),
-            jnp.sum(gain_update * gain_update),
+            weight_sums,
+            (
+                jnp.sum(up_update * up_update),
+                jnp.sum(down_update * down_update),
+                jnp.sum(gain_update * gain_update),
+            ),
         ),
         ("wide", "narrow"),
     )
     up_master_new = finish(up_master, up_update, weight_sums[0], update_sums[0])
     down_master_new = finish(down_master, down_update, weight_sums[1], update_sums[1])
     gain_master_new = finish(gain_master, gain_update, weight_sums[2], update_sums[2])
-    up_low = up_master_new.astype(jnp.bfloat16)
-    down_low = down_master_new.astype(jnp.bfloat16)
-    gain_low = gain_master_new.astype(jnp.bfloat16).reshape(1, -1)
-    rows_up, rows_down, rows_gain = (
-        lax.all_gather(up_low, "narrow", axis=0, tiled=True),
-        lax.all_gather(down_low, "narrow", axis=0, tiled=True),
-        lax.all_gather(gain_low, "narrow", axis=0, tiled=True),
+
+    low = jnp.concatenate(
+        [
+            up_master_new.astype(jnp.bfloat16).reshape(up_size),
+            down_master_new.astype(jnp.bfloat16).reshape(down_size),
+            gain_master_new.astype(jnp.bfloat16),
+            jnp.zeros((width - total,), jnp.bfloat16),
+        ]
+    ).reshape(1, width // LANES, LANES)
+    whole = lax.all_gather(low, ("narrow", "wide"), axis=0, tiled=True)
+    whole = whole.reshape(n_narrow, n_wide, width)
+    up_weights = (
+        whole[:, :, :up_size]
+        .reshape(n_narrow, n_wide, up_rows, up_cols)
+        .transpose(0, 2, 1, 3)
+        .reshape(n_narrow * up_rows, n_wide * up_cols)
     )
-    up_weights, down_weights, gain_whole = (
-        lax.all_gather(rows_up, "wide", axis=1, tiled=True),
-        lax.all_gather(rows_down, "wide", axis=1, tiled=True),
-        lax.all_gather(rows_gain, "wide", axis=1, tiled=True),
+    down_weights = (
+        whole[:, :, up_size : up_size + down_size]
+        .reshape(n_narrow, n_wide, down_rows, down_cols)
+        .transpose(0, 2, 1, 3)
+        .reshape(n_narrow * down_rows, n_wide * down_cols)
     )
-    gain_weights = gain_whole.reshape(-1)
+    gain_weights = whole[:, :, up_size + down_size : total].reshape(-1)
     return (
         up_first_new,
         up_second_new,

time: 548 us -> 380 us (0.69)
  waiting for transfers between devices: 322 us -> 200 us
  blocking collectives: 169 us -> 78 us
  local copies, waits for them, and re-layouts: 27.7 us -> 74.3 us
    unnamed x7 -> x3, waiting for transfers between devices: 206 us -> 85.1 us
    reduce_scatter x1 -> x0, waiting for transfers between devices: 86.1 us -> none  [body(): lax.psum_scatter(down_grads[0], 'wide', scatter_dimension=1, tiled=True)]
    all_gather x2 -> x1, waiting for transfers between devices: 30.5 us -> 115 us  [body(): whole = lax.all_gather(low, ('narrow', 'wide'), axis=0, tiled=True)]
    all_gather x3 -> x0, blocking collectives: 79 us -> none  [the longest x1 38.6 us: body(): lax.all_gather(rows_gain, 'wide', axis=1, tiled=True)]
    reshape x0 -> x8, local copies, waits for them, and re-layouts: none -> 35.9 us  [the longest x2 19.5 us: body(): up_weights = whole[:, :, :up_size].reshape(n_narrow, n_wide, up_rows, up_...]
    unnamed x1 -> x0, blocking collectives: 12.4 us -> none
    slice x0 -> x4, local copies, waits for them, and re-layouts: none -> 10.4 us  [the longest x1 5.99 us: body(): whole[:, :, up_size:up_size + down_size]]
    transpose x0 -> x3, local copies, waits for them, and re-layouts: none -> 9.06 us  [the longest x1 5.3 us: body(): up_weights = whole[:, :, :up_size].reshape(n_narrow, n_wide, up_rows, up_...]
  transfers between devices with their start and end apart: 5 -> 2, of which waited for: 4 -> 2; matrix products, arithmetic and copies ran while one was open for 2% -> 0% of each run, Pallas kernels for 0% -> 0%
where the time goes in v1:
time: 380 us; the launch traced here: 378 us
  waiting for transfers between devices  200 us (53%)
  blocking collectives  78 us (21%)
  local copies, waits for them, and re-layouts  74.3 us (20%)
  between operations  18.5 us (5%)
  other arithmetic  7.16 us (2%)
    all_gather x1, waiting for transfers between devices, body(): whole = lax.all_gather(low, ('narrow', 'wide'), axis=0, tiled=True)  115 us
    unnamed x3, waiting for transfers between devices  85.1 us
    psum x1, blocking collectives, body(): lax.psum((weight_sums, (jnp.sum(up_update * up_update), jnp.sum(down_upda...  78 us
    reshape x2, local copies, waits for them, and re-layouts, body(): up_weights = whole[:, :, :up_size].reshape(n_narrow, n_wide, up_rows, up_...  19.5 us
    reshape x1, local copies, waits for them, and re-layouts, body(): whole = whole.reshape(n_narrow, n_wide, width)  13.5 us
    unnamed x35, local copies, waits for them, and re-layouts  13.1 us
  transfers between devices with their start and end apart: 2, of which 2 were waited for; matrix products, arithmetic and copies ran while one was open for 0% of the time, Pallas kernels for 0%

profile of v1, /device:TPU:1, one launch (start us, length us, event | category | flops | bytes accessed | tf_op | source)
XLA Modules:
  0.0 378.5 jit_solution(11554978971868273810)
XLA Ops:
  7.2 0.0 reduce-scatter.4.cloned.1.call-start
  7.2 0.5 broadcast.49
  7.7 1.3 reduce.3
  9.1 0.1 reshape.74
  9.2 1.4 copy.34
  10.6 0.6 copy.31
  11.2 1.6 copy.43
  12.8 1.3 reshape_squeeze.6
  14.1 0.7 copy.42
  14.8 0.3 reshape.72
  15.1 2.5 concatenate.6
  17.7 0.0 copy-start.12
  17.7 0.0 copy-start.13
  17.7 0.0 copy-start.14
  17.7 0.0 copy-start.5
  17.7 0.0 copy-start.10
  17.7 0.0 copy-start.11
  17.7 0.0 copy-start.2
  17.8 0.0 copy-start.8
  17.8 0.0 copy-start.9
  17.8 1.5 reshape.75
  19.3 0.0 reduce-scatter.4.cloned.1.call-update
  19.3 0.0 all-gather.2.cloned.1.call-start
  19.4 85.1 %reduce-scatter.4.cloned.1.call-done = f32[1,129,128]{2,1,0:T(8,128)} async-done(((f32[32,129,128]{2,1,0:T(8,128)}), f32[1,129,128]{2,1,0:T(8,128)}) %reduce-scatter.4.cloned.1.call-update) | async-done | bytes 66064
  104.5 1.9 multiply_reduce_fusion.4
  106.3 1.5 multiply_reduce_fusion.2
  107.8 1.0 slice.21
  108.9 0.7 multiply_reduce_fusion
  109.5 78.0 %all-reduce.1 = (f32[]{:T(128)}, f32[]{:T(128)}, f32[]{:T(128)}, f32[]{:T(128)}, f32[]{:T(128)}, /*index=5*/f32[]{:T(128)}) all-reduce(f32[]{:T(128)} %get-tuple-element.13, f32[]{:T(128)} %get-tuple-element.12, f32[]{:T(128)} %get-tuple-element.15, f32[]{:T(128)} %get-tuple-element.14, ...), channel_id=1, replica_groups=mesh['wide'=32,'narrow'=8] {'wide','narrow'}, use_global_device_ids=true, to_apply=%region_2.0 | all-reduce | flops 6 | bytes 48 | tf_op jit(solution)/shard_map/psum | solution.py:92
  191.8 0.6 fusion.4
  192.5 0.1 reshape.76
  192.6 0.5 fusion.3
  193.1 0.6 convert_bitcast_fusion
  193.7 0.7 concatenate.7
  194.5 0.0 all-gather.2.cloned.1.call-update
  194.5 115.3 %all-gather.2.cloned.1.call-done = bf16[256,129,128]{2,1,0:T(8,128)(2,1)} async-done(((bf16[1,129,128]{2,1,0:T(8,128)(2,1)}), bf16[256,129,128]{2,1,0:T(8,128)(2,1)}) %all-gather.2.cloned.1.call-update) | async-done | bytes 8454160 | tf_op jit(solution)/shard_map/all_gather | solution.py:115
  309.8 13.5 %reshape.81 = bf16[8,32,16512]{2,1,0:T(8,128)(2,1)} reshape(bf16[256,129,128]{2,1,0:T(8,128)(2,1)} %all-gather.2.cloned.1.call-done) | data formatting | bytes 16908288 | tf_op jit(solution)/shard_map/reshape | solution.py:116
  323.4 1.1 slice.33
  324.4 6.0 %slice.32 = bf16[8,32,8192]{2,1,0:T(8,128)(2,1)} slice(bf16[8,32,16512]{2,1,0:T(8,128)(2,1)} %reshape.81), slice={[0:8], [0:32], [8256:16448]} | slice | bytes 8388608 | tf_op jit(solution)/shard_map/slice | solution.py:124
  330.4 2.3 slice.31
  332.8 0.7 reshape.86
  333.5 3.4 copy.36
  336.9 1.0 bitcast_bitcast_fusion
  337.9 2.7 copy.33
  340.6 6.2 %copy.41 = bf16[64,8,32,128]{3,1,2,0:T(8,128)(2,1)} copy(bf16[64,8,32,128]{3,2,1,0:T(8,128)(2,1)S(1)} %bitcast.43) | data formatting | bytes 8388608
  346.8 9.7 %reshape.82 = bf16[8,32,24,344]{3,2,1,0:T(8,128)(2,1)} reshape(bf16[8,32,8256]{2,1,0:T(8,128)(2,1)} %slice.31) | data formatting | bytes 8454144 | tf_op jit(solution)/shard_map/reshape | solution.py:119
  356.5 5.3 %copy.32 = bf16[8,24,32,344]{3,2,1,0:T(8,128)(2,1)} copy(bf16[8,24,32,344]{3,1,2,0:T(8,128)(2,1)} %bitcast.40) | data formatting | bytes 8454144 | tf_op jit(solution)/shard_map/transpose | solution.py:120
  361.8 9.9 %reshape.83 = bf16[192,11008]{1,0:T(8,128)(2,1)} reshape(bf16[8,24,32,344]{3,2,1,0:T(8,128)(2,1)} %copy.32) | data formatting | bytes 8454144 | tf_op jit(solution)/shard_map/reshape | solution.py:121
  (23 shorter events, 0.0 us)
Async XLA Ops:
  7.2 5.6 %copy-start.1 = (f32[1,24,11008]{2,1,0:T(8,128)S(1)}, f32[1,24,11008]{2,1,0:T(8,128)}, u32[]{:S(2)}) copy-start(f32[1,24,11008]{2,1,0:T(8,128)} %param.12) | copy-start | bytes 3170308
  7.2 97.3 %reduce-scatter.4.cloned.1.call-start = ((), (), s32[]{:S(2)}) async-start(), calls=%async_computation.2 | async-start | bytes 2297856
  17.7 86.8 %copy-start.12 = (f32[16]{0:T(128)S(1)}, f32[16]{0:T(128)}, u32[]{:S(2)}) copy-start(f32[16]{0:T(128)} %param.17) | copy-start | bytes 196
  17.7 86.8 %copy-start.13 = (f32[16]{0:T(128)S(1)}, f32[16]{0:T(128)}, u32[]{:S(2)}) copy-start(f32[16]{0:T(128)} %param.20) | copy-start | bytes 196
  17.7 86.8 %copy-start.14 = (f32[16]{0:T(128)S(1)}, f32[16]{0:T(128)}, u32[]{:S(2)}) copy-start(f32[16]{0:T(128)} %param.23) | copy-start | bytes 196
  17.7 88.6 %copy-start.5 = (f32[64,128]{1,0:T(8,128)S(1)}, f32[64,128]{1,0:T(8,128)}, u32[]{:S(2)}) copy-start(f32[64,128]{1,0:T(8,128)} %param.16) | copy-start | bytes 98308
  17.7 88.6 %copy-start.10 = (f32[64,128]{1,0:T(8,128)S(1)}, f32[64,128]{1,0:T(8,128)}, u32[]{:S(2)}) copy-start(f32[64,128]{1,0:T(8,128)} %param.19) | copy-start | bytes 98308
  17.7 88.6 %copy-start.11 = (f32[64,128]{1,0:T(8,128)S(1)}, f32[64,128]{1,0:T(8,128)}, u32[]{:S(2)}) copy-start(f32[64,128]{1,0:T(8,128)} %param.22) | copy-start | bytes 98308
  17.7 91.1 %copy-start.2 = (f32[24,344]{1,0:T(8,128)S(1)}, f32[24,344]{1,0:T(8,128)}, u32[]{:S(2)}) copy-start(f32[24,344]{1,0:T(8,128)} %param.15) | copy-start | bytes 99076
  17.8 91.1 %copy-start.8 = (f32[24,344]{1,0:T(8,128)S(1)}, f32[24,344]{1,0:T(8,128)}, u32[]{:S(2)}) copy-start(f32[24,344]{1,0:T(8,128)} %param.21) | copy-start | bytes 99076
  17.8 91.1 %copy-start.9 = (f32[24,344]{1,0:T(8,128)S(1)}, f32[24,344]{1,0:T(8,128)}, u32[]{:S(2)}) copy-start(f32[24,344]{1,0:T(8,128)} %param.18) | copy-start | bytes 99076
  19.3 290.4 %all-gather.2.cloned.1.call-start = ((), (), s32[]{:S(2)}) async-start(), calls=%async_computation.1 | async-start | bytes 8947712 | tf_op jit(solution)/shard_map/all_gather | solution.py:115
  107.8 215.5 %copy-start.6 = (f32[64,128]{1,0:T(8,128)}, f32[64,128]{1,0:T(8,128)S(1)}, u32[]{:S(2)}) copy-start(f32[64,128]{1,0:T(8,128)S(1)} %get-tuple-element.32) | copy-start | bytes 98308
  107.8 215.5 %copy-start.7 = (f32[64,128]{1,0:T(8,128)}, f32[64,128]{1,0:T(8,128)S(1)}, u32[]{:S(2)}) copy-start(f32[64,128]{1,0:T(8,128)S(1)} %get-tuple-element.33) | copy-start | bytes 98308
  109.5 213.8 %copy-start.3 = (f32[24,344]{1,0:T(8,128)}, f32[24,344]{1,0:T(8,128)S(1)}, u32[]{:S(2)}) copy-start(f32[24,344]{1,0:T(8,128)S(1)} %get-tuple-element.34) | copy-start | bytes 99076
  109.5 213.8 %copy-start.4 = (f32[24,344]{1,0:T(8,128)}, f32[24,344]{1,0:T(8,128)S(1)}, u32[]{:S(2)}) copy-start(f32[24,344]{1,0:T(8,128)S(1)} %get-tuple-element.35) | copy-start | bytes 99076
  323.4 7.1 %copy-start = (bf16[8,32,16512]{2,1,0:T(8,128)(2,1)S(1)}, bf16[8,32,16512]{2,1,0:T(8,128)(2,1)}, u32[]{:S(2)}) copy-start(bf16[8,32,16512]{2,1,0:T(8,128)(2,1)} %reshape.81) | copy-start | bytes 25362436
Sparse Core Ops, SparseCore 0:
  19.5 84.9 reduce-scatter.3
  194.6 115.1 all-gather.1

commit v2 on v0

--- a/solution.py
+++ b/solution.py
@@ -10,6 +10,7 @@
 DECAY_RATE = 0.01
 CORRECT_FIRST = 1.0 - 0.9**10
 CORRECT_SECOND = 1.0 - 0.999**10
+LANES = 128
 
 
 def moments(grad_sum, master, first, second, decay):
@@ -27,6 +28,16 @@
     return master - LEARN_RATE * trust * update
 
 
+def butterfly_sum(x, n_wide, n_narrow):
+    for axis, size in (("wide", n_wide), ("narrow", n_narrow)):
+        step = 1
+        while step < size:
+            pairs = [(i, i ^ step) for i in range(size)]
+            x = x + lax.ppermute(x, axis, pairs)
+            step *= 2
+    return x
+
+
 def body(
     up_grads,
     down_grads,
@@ -41,20 +52,38 @@
     down_second,
     gain_second,
 ):
-    weight_sums = lax.psum(
-        (
-            jnp.sum(up_master * up_master),
-            jnp.sum(down_master * down_master),
-            jnp.sum(gain_master * gain_master),
-        ),
-        ("wide", "narrow"),
+    n_wide = lax.axis_size("wide")
+    n_narrow = lax.axis_size("narrow")
+    up_rows, up_cols = up_master.shape
+    down_rows, down_cols = down_master.shape
+    gain_cols = gain_master.shape[0]
+    up_tiles = -(-up_cols // LANES)
+    up_pad = up_tiles * LANES
+    up_at = down_rows
+    gain_at = up_at + up_rows * up_tiles
+    height = -(-(gain_at + 1) // 16) * 16
+
+    down_part = down_grads[0].reshape(down_rows, n_wide, down_cols).transpose(1, 0, 2)
+    up_part = up_grads[0].reshape(up_rows, n_wide, up_cols)
+    up_part = jnp.pad(up_part, ((0, 0), (0, 0), (0, up_pad - up_cols)))
+    up_part = up_part.reshape(up_rows, n_wide, up_tiles, LANES).transpose(1, 0, 2, 3)
+    up_part = up_part.reshape(n_wide, up_rows * up_tiles, LANES)
+    gain_part = jnp.pad(gain_grads.reshape(n_wide, 1, gain_cols), ((0, 0), (0, 0), (0, LANES - gain_cols)))
+    packed = jnp.concatenate(
+        [
+            down_part,
+            up_part,
+            gain_part,
+            jnp.zeros((n_wide, height - gain_at - 1, LANES), jnp.float32),
+        ],
+        axis=1,
     )
-    up_sum, down_sum, gain_sum = (
-        lax.psum_scatter(up_grads[0], "wide", scatter_dimension=1, tiled=True),
-        lax.psum_scatter(down_grads[0], "wide", scatter_dimension=1, tiled=True),
-        lax.psum_scatter(gain_grads, "wide", scatter_dimension=1, tiled=True),
-    )
-    gain_sum = gain_sum.reshape(gain_master.shape)
+    received = lax.all_to_all(packed, "wide", 0, 0, tiled=True)
+    summed = jnp.sum(received, axis=0)
+    down_sum = summed[:down_rows]
+    up_sum = summed[up_at:gain_at].reshape(up_rows, up_pad)[:, :up_cols]
+    gain_sum = summed[gain_at, :gain_cols]
+
     up_first_new, up_second_new, up_update = moments(
         up_sum, up_master, up_first, up_second, DECAY_RATE
     )
@@ -64,31 +93,49 @@
     gain_first_new, gain_second_new, gain_update = moments(
         gain_sum, gain_master, gain_first, gain_second, 0.0
     )
-    update_sums = lax.psum(
-        (
+    partial = jnp.stack(
+        [
+            jnp.sum(up_master * up_master),
+            jnp.sum(down_master * down_master),
+            jnp.sum(gain_master * gain_master),
             jnp.sum(up_update * up_update),
             jnp.sum(down_update * down_update),
             jnp.sum(gain_update * gain_update),
-        ),
-        ("wide", "narrow"),
+            jnp.float32(0.0),
+            jnp.float32(0.0),
+        ]
     )
-    up_master_new = finish(up_master, up_update, weight_sums[0], update_sums[0])
-    down_master_new = finish(down_master, down_update, weight_sums[1], update_sums[1])
-    gain_master_new = finish(gain_master, gain_update, weight_sums[2], update_sums[2])
-    up_low = up_master_new.astype(jnp.bfloat16)
-    down_low = down_master_new.astype(jnp.bfloat16)
-    gain_low = gain_master_new.astype(jnp.bfloat16).reshape(1, -1)
-    rows_up, rows_down, rows_gain = (
-        lax.all_gather(up_low, "narrow", axis=0, tiled=True),
-        lax.all_gather(down_low, "narrow", axis=0, tiled=True),
-        lax.all_gather(gain_low, "narrow", axis=0, tiled=True),
+    sums = butterfly_sum(partial, n_wide, n_narrow)
+    up_master_new = finish(up_master, up_update, sums[0], sums[3])
+    down_master_new = finish(down_master, down_update, sums[1], sums[4])
+    gain_master_new = finish(gain_master, gain_update, sums[2], sums[5])
+
+    up_low = jnp.pad(up_master_new.astype(jnp.bfloat16), ((0, 0), (0, up_pad - up_cols)))
+    low = jnp.concatenate(
+        [
+            down_master_new.astype(jnp.bfloat16),
+            up_low.reshape(up_rows * up_tiles, LANES),
+            jnp.pad(gain_master_new.astype(jnp.bfloat16), (0, LANES - gain_cols)).reshape(1, LANES),
+            jnp.zeros((height - gain_at - 1, LANES), jnp.bfloat16),
+        ]
     )
-    up_weights, down_weights, gain_whole = (
-        lax.all_gather(rows_up, "wide", axis=1, tiled=True),
-        lax.all_gather(rows_down, "wide", axis=1, tiled=True),
-        lax.all_gather(rows_gain, "wide", axis=1, tiled=True),
+    rows = lax.all_to_all(
+        jnp.broadcast_to(low[None], (n_narrow, height, LANES)), "narrow", 0, 0, tiled=True
     )
-    gain_weights = gain_whole.reshape(-1)
+    whole = lax.all_gather(rows[None], "wide", axis=0, tiled=True)
+    down_weights = (
+        whole[:, :, :down_rows]
+        .transpose(1, 2, 0, 3)
+        .reshape(n_narrow * down_rows, n_wide * down_cols)
+    )
+    up_weights = (
+        whole[:, :, up_at:gain_at]
+        .reshape(n_wide, n_narrow, up_rows, up_tiles, LANES)
+        .transpose(1, 2, 0, 3, 4)
+        .reshape(n_narrow, up_rows, n_wide, up_pad)[:, :, :, :up_cols]
+        .reshape(n_narrow * up_rows, n_wide * up_cols)
+    )
+    gain_weights = whole[:, :, gain_at, :gain_cols].transpose(1, 0, 2).reshape(-1)
     return (
         up_first_new,
         up_second_new,

time: 548 us -> 241 us (0.44)
  waiting for transfers between devices: 322 us -> 109 us
  blocking collectives: 169 us -> 16.2 us
  local copies, waits for them, and re-layouts: 27.7 us -> 68.3 us
  starting transfers between devices: 0.2 us -> 22 us
    unnamed x7 -> x1, waiting for transfers between devices: 206 us -> 0.02 us
    reduce_scatter x1 -> x0, waiting for transfers between devices: 86.1 us -> none  [body(): lax.psum_scatter(down_grads[0], 'wide', scatter_dimension=1, tiled=True)]
    all_gather x3 -> x0, blocking collectives: 79 us -> none  [the longest x1 38.6 us: body(): lax.all_gather(rows_gain, 'wide', axis=1, tiled=True)]
    psum x1 -> x0, blocking collectives: 77.8 us -> none  [body(): lax.psum((jnp.sum(up_master * up_master), jnp.sum(down_master * down_mast...]
    all_gather x2 -> x1, waiting for transfers between devices: 30.5 us -> 61.9 us  [body(): whole = lax.all_gather(rows[None], 'wide', axis=0, tiled=True)]
    all_to_all x0 -> x1, waiting for transfers between devices: none -> 31.3 us  [body(): received = lax.all_to_all(packed, 'wide', 0, 0, tiled=True)]
    reshape x0 -> x8, local copies, waits for them, and re-layouts: none -> 24.1 us  [the longest x2 22.8 us: body(): up_weights = whole[:, :, up_at:gain_at].reshape(n_wide, n_narrow, up_rows...]
    all_to_all x0 -> x1, blocking collectives: none -> 16.2 us  [body(): lax.all_to_all(jnp.broadcast_to(low[None], (n_narrow, height, LANES)), 'n...]
  transfers between devices with their start and end apart: 5 -> 10, of which waited for: 4 -> 10; matrix products, arithmetic and copies ran while one was open for 2% -> 0% of each run, Pallas kernels for 0% -> 0%
where the time goes in v2:
time: 241 us; the launch traced here: 240 us
  waiting for transfers between devices  109 us (45%)
  local copies, waits for them, and re-layouts  68.3 us (28%)
  starting transfers between devices  22 us (9%)
  between operations  18.6 us (8%)
  blocking collectives  16.2 us (7%)
  other arithmetic  6.01 us (2%)
    all_gather x1, waiting for transfers between devices, body(): whole = lax.all_gather(rows[None], 'wide', axis=0, tiled=True)  61.9 us
    all_to_all x1, waiting for transfers between devices, body(): received = lax.all_to_all(packed, 'wide', 0, 0, tiled=True)  31.3 us
    reshape x2, local copies, waits for them, and re-layouts, body(): up_weights = whole[:, :, up_at:gain_at].reshape(n_wide, n_narrow, up_rows...  22.8 us
    all_to_all x1, blocking collectives, body(): lax.all_to_all(jnp.broadcast_to(low[None], (n_narrow, height, LANES)), 'n...  16.2 us
    ppermute x8, waiting for transfers between devices, butterfly_sum(): x = x + lax.ppermute(x, axis, pairs)  15.6 us
    ppermute x8, starting transfers between devices, butterfly_sum(): x = x + lax.ppermute(x, axis, pairs)  13.4 us
    unnamed x35, local copies, waits for them, and re-layouts  10.3 us
    slice x2, local copies, waits for them, and re-layouts, body(): whole[:, :, up_at:gain_at]  8.84 us
  transfers between devices with their start and end apart: 10, of which 10 were waited for; matrix products, arithmetic and copies ran while one was open for 0% of the time, Pallas kernels for 0%

profile of v2, /device:TPU:1, one launch (start us, length us, event | category | flops | bytes accessed | tf_op | source)
XLA Modules:
  0.0 239.9 jit_solution(16620366658497685970)
XLA Ops:
  7.2 0.5 broadcast.72
  7.7 1.3 reduce.3
  9.0 0.1 reshape.81
  9.1 2.4 copy.44
  11.5 1.3 reshape_squeeze.7
  12.9 0.5 reshape.79
  13.4 0.1 copy.36
  13.7 1.0 copy-done.1
  14.7 0.2 fusion
  14.9 2.8 %copy.37 = f32[32,144,128]{2,1,0:T(8,128)} copy(f32[32,144,128]{2,0,1:T(8,128)S(1)} %fusion) | data formatting | bytes 4718592 | tf_op jit(solution)/shard_map/concatenate | solution.py:72
  17.7 8.6 %all-to-all-start = ((f32[32,144,128]{2,1,0:T(8,128)}), f32[32,144,128]{2,1,0:T(8,128)S(1)}, u32[]{:S(2)}, u32[]{:S(2)}) async-start(f32[32,144,128]{2,1,0:T(8,128)} %copy.37), calls=%async_computation | async-start | bytes 4718592 | tf_op jit(solution)/shard_map/all_to_all | solution.py:81
  26.5 31.3 %all-to-all-done = f32[32,144,128]{2,1,0:T(8,128)S(1)} async-done(((f32[32,144,128]{2,1,0:T(8,128)}), f32[32,144,128]{2,1,0:T(8,128)S(1)}, u32[]{:S(2)}, u32[]{:S(2)}) %all-to-all-start) | async-done | bytes 2359328 | tf_op jit(solution)/shard_map/all_to_all | solution.py:81
  57.7 0.1 reduce_sum.63
  57.9 1.1 multiply_reduce_fusion.4
  59.1 0.6 multiply_reduce_fusion.2
  59.7 0.7 multiply_reduce_fusion
  60.4 4.0 %stack.27 = f32[8]{0:T(128)S(1)} concatenate(f32[1]{0:T(128)} %bitcast.3, f32[1]{0:T(128)} %bitcast.4, f32[1]{0:T(128)} %bitcast.5, f32[1]{0:T(128)} %bitcast.6, f32[1]{0:T(128)} %bitcast.7, f32[1]{0:T(128)} %bitcast.9, f32[2]{0:T(128)S(1)} %broadcast.50), dimensions={0} | concatenate | bytes 64 | tf_op jit(solution)/shard_map/stack | solution.py:96
  64.4 1.9 collective-permute-start
  66.3 0.8 collective-permute-done
  67.1 2.4 %collective-permute-done.1 = f32[8]{0:T(128)S(1)} collective-permute-done((f32[8]{0:T(128)S(1)}, f32[8]{0:T(128)S(1)}, u32[]{:S(2)}, u32[]{:S(2)}) %collective-permute-start.1) | collective-permute-done | bytes 64 | tf_op jit(solution)/shard_map/ppermute | solution.py:36
  69.5 3.9 %collective-permute-done.2 = f32[8]{0:T(128)S(1)} collective-permute-done((f32[8]{0:T(128)S(1)}, f32[8]{0:T(128)S(1)}, u32[]{:S(2)}, u32[]{:S(2)}) %collective-permute-start.2) | collective-permute-done | bytes 64 | tf_op jit(solution)/shard_map/ppermute | solution.py:36
  73.5 2.4 %collective-permute-done.3 = f32[8]{0:T(128)S(1)} collective-permute-done((f32[8]{0:T(128)S(1)}, f32[8]{0:T(128)S(1)}, u32[]{:S(2)}, u32[]{:S(2)}) %collective-permute-start.3) | collective-permute-done | bytes 64 | tf_op jit(solution)/shard_map/ppermute | solution.py:36
  75.9 0.7 collective-permute-start.4
  76.6 3.2 %collective-permute-done.4 = f32[8]{0:T(128)S(1)} collective-permute-done((f32[8]{0:T(128)S(1)}, f32[8]{0:T(128)S(1)}, u32[]{:S(2)}, u32[]{:S(2)}) %collective-permute-start.4) | collective-permute-done | bytes 64 | tf_op jit(solution)/shard_map/ppermute | solution.py:36
  79.8 1.6 collective-permute-start.5
  81.5 1.0 collective-permute-done.5
  82.4 3.0 %collective-permute-start.6 = (f32[8]{0:T(128)S(1)}, f32[8]{0:T(128)S(1)}, u32[]{:S(2)}, u32[]{:S(2)}) collective-permute-start(f32[8]{0:T(128)S(1)} %add.105), channel_id=1, source_target_pairs={{0,2},{1,3},{2,0},{3,1},{4,6},{5,7},{6,4},{7,5},{8,10},{9,11},{10,... | collective-permute-start | bytes 104 | tf_op jit(solution)/shard_map/ppermute | solution.py:36
  85.4 1.0 collective-permute-done.6
  86.4 6.1 %collective-permute-start.7 = (f32[8]{0:T(128)S(1)}, f32[8]{0:T(128)S(1)}, u32[]{:S(2)}, u32[]{:S(2)}) collective-permute-start(f32[8]{0:T(128)S(1)} %add.106), channel_id=1, source_target_pairs={{0,4},{1,5},{2,6},{3,7},{4,0},{5,1},{6,2},{7,3},{8,12},{9,13},{10,... | collective-permute-start | bytes 104 | tf_op jit(solution)/shard_map/ppermute | solution.py:36
  92.5 1.0 collective-permute-done.7
  93.4 0.6 fusion.11
  98.3 0.5 fusion.7
  98.8 0.6 fusion.6
  99.5 0.6 fusion.5
  100.1 0.1 maximum_maximum_fusion
  100.3 16.2 %all_to_all.10 = bf16[8,144,128]{2,1,0:T(8,128)(2,1)} all-to-all(bf16[8,144,128]{2,1,0:T(8,128)(2,1)S(1)} %broadcast_in_dim.17), channel_id=1, replica_groups=mesh['wide'=32,'narrow'=8] {'narrow'}, dimensions={0} | all-to-all | bytes 589824 | tf_op jit(solution)/shard_map/all_to_all | solution.py:122
  116.5 61.9 %all-gather.3.cloned.1.call-done = bf16[256,144,128]{2,1,0:T(8,128)(2,1)} async-done(((bf16[8,144,128]{2,1,0:T(8,128)(2,1)}), bf16[256,144,128]{2,1,0:T(8,128)(2,1)}) %all-gather.3.cloned.1.call-update) | async-done | bytes 9437200 | tf_op jit(solution)/shard_map/all_gather | solution.py:125
  178.4 1.1 slice.63
  179.5 5.8 %slice_bitcast_fusion = bf16[8,64,32,128]{3,1,0,2:T(8,128)(2,1)} fusion(bf16[32,8,144,128]{3,2,1,0:T(8,128)(2,1)} %bitcast.49), kind=kLoop, calls=%fused_computation.1 | loop fusion | bytes 8388608 | tf_op jit(solution)/shard_map/transpose | solution.py:128
  185.4 5.4 %slice.60 = bf16[32,8,72,128]{3,2,1,0:T(8,128)(2,1)} slice(bf16[32,8,144,128]{3,2,1,0:T(8,128)(2,1)} %bitcast.50), slice={[0:32], [0:8], [64:136], [0:128]} | slice | bytes 9437184 | tf_op jit(solution)/shard_map/slice | solution.py:132
  190.8 0.7 reshape.89
  191.5 3.4 %copy.38 = bf16[32,8,72,128]{3,1,2,0:T(8,128)(2,1)S(1)} copy(bf16[32,8,72,128]{3,2,1,0:T(8,128)(2,1)} %slice.60) | data formatting | bytes 9437184 | tf_op jit(solution)/shard_map/slice | solution.py:132
  194.9 0.2 copy-done
  195.1 2.7 %copy.40 = bf16[8,64,32,128]{3,2,1,0:T(8,128)(2,1)S(1)} copy(bf16[8,64,32,128]{3,1,0,2:T(8,128)(2,1)S(1)} %copy-done) | data formatting | bytes 8388608 | tf_op jit(solution)/shard_map/transpose | solution.py:128
  197.8 6.2 %copy.48 = bf16[64,8,32,128]{3,1,2,0:T(8,128)(2,1)} copy(bf16[64,8,32,128]{3,2,1,0:T(8,128)(2,1)S(1)} %bitcast.47) | data formatting | bytes 8388608
  204.0 6.3 %copy.39 = bf16[8,24,32,3,128]{4,3,2,1,0:T(4,128)(2,1)} copy(bf16[8,24,32,3,128]{4,0,3,1,2:T(8,128)(2,1)S(1)} %bitcast.45) | data formatting | bytes 9437184 | tf_op jit(solution)/shard_map/transpose | solution.py:134
  210.3 12.9 %reshape.86 = bf16[8,24,32,384]{3,2,1,0:T(8,128)(2,1)} reshape(bf16[8,24,32,3,128]{4,3,2,1,0:T(4,128)(2,1)} %copy.39) | data formatting | bytes 9437184 | tf_op jit(solution)/shard_map/reshape | solution.py:135
  223.2 9.9 %reshape.87 = bf16[192,11008]{1,0:T(8,128)(2,1)} reshape(bf16[8,24,32,344]{3,2,1,0:T(8,128)(2,1)} %bitcast.46) | data formatting | bytes 8454144 | tf_op jit(solution)/shard_map/reshape | solution.py:136
  (56 shorter events, 0.5 us)
Async XLA Ops:
  7.2 4.3 %copy-start.2 = (f32[1,24,11008]{2,1,0:T(8,128)S(1)}, f32[1,24,11008]{2,1,0:T(8,128)}, u32[]{:S(2)}) copy-start(f32[1,24,11008]{2,1,0:T(8,128)} %param.12) | copy-start | bytes 3170308
  13.4 1.2 copy-start.1
  17.7 40.1 %all-to-all-start = ((f32[32,144,128]{2,1,0:T(8,128)}), f32[32,144,128]{2,1,0:T(8,128)S(1)}, u32[]{:S(2)}, u32[]{:S(2)}) async-start(f32[32,144,128]{2,1,0:T(8,128)} %copy.37), calls=%async_computation | async-start | bytes 4718592 | tf_op jit(solution)/shard_map/all_to_all | solution.py:81
  26.2 31.7 %copy-start.13 = (f32[16]{0:T(128)S(1)}, f32[16]{0:T(128)}, u32[]{:S(2)}) copy-start(f32[16]{0:T(128)} %param.17) | copy-start | bytes 196
  26.3 31.7 %copy-start.14 = (f32[16]{0:T(128)S(1)}, f32[16]{0:T(128)}, u32[]{:S(2)}) copy-start(f32[16]{0:T(128)} %param.20) | copy-start | bytes 196
  26.3 31.7 %copy-start.15 = (f32[16]{0:T(128)S(1)}, f32[16]{0:T(128)}, u32[]{:S(2)}) copy-start(f32[16]{0:T(128)} %param.23) | copy-start | bytes 196
  26.3 32.8 %copy-start.6 = (f32[64,128]{1,0:T(8,128)S(1)}, f32[64,128]{1,0:T(8,128)}, u32[]{:S(2)}) copy-start(f32[64,128]{1,0:T(8,128)} %param.16) | copy-start | bytes 98308
  26.3 32.8 %copy-start.11 = (f32[64,128]{1,0:T(8,128)S(1)}, f32[64,128]{1,0:T(8,128)}, u32[]{:S(2)}) copy-start(f32[64,128]{1,0:T(8,128)} %param.19) | copy-start | bytes 98308
  26.3 32.8 %copy-start.12 = (f32[64,128]{1,0:T(8,128)S(1)}, f32[64,128]{1,0:T(8,128)}, u32[]{:S(2)}) copy-start(f32[64,128]{1,0:T(8,128)} %param.22) | copy-start | bytes 98308
  26.3 33.4 %copy-start.3 = (f32[24,344]{1,0:T(8,128)S(1)}, f32[24,344]{1,0:T(8,128)}, u32[]{:S(2)}) copy-start(f32[24,344]{1,0:T(8,128)} %param.15) | copy-start | bytes 99076
  26.3 33.4 %copy-start.9 = (f32[24,344]{1,0:T(8,128)S(1)}, f32[24,344]{1,0:T(8,128)}, u32[]{:S(2)}) copy-start(f32[24,344]{1,0:T(8,128)} %param.21) | copy-start | bytes 99076
  26.3 33.4 %copy-start.10 = (f32[24,344]{1,0:T(8,128)S(1)}, f32[24,344]{1,0:T(8,128)}, u32[]{:S(2)}) copy-start(f32[24,344]{1,0:T(8,128)} %param.18) | copy-start | bytes 99076
  26.3 152.1 %all-gather.3.cloned.1.call-start = ((), (), s32[]{:S(2)}) async-start(), calls=%async_computation.2 | async-start | bytes 9732096 | tf_op jit(solution)/shard_map/all_gather | solution.py:125
  59.7 125.6 %copy-start.7 = (f32[64,128]{1,0:T(8,128)}, f32[64,128]{1,0:T(8,128)S(1)}, u32[]{:S(2)}) copy-start(f32[64,128]{1,0:T(8,128)S(1)} %get-tuple-element.26) | copy-start | bytes 98308
  59.7 125.6 %copy-start.8 = (f32[64,128]{1,0:T(8,128)}, f32[64,128]{1,0:T(8,128)S(1)}, u32[]{:S(2)}) copy-start(f32[64,128]{1,0:T(8,128)S(1)} %get-tuple-element.27) | copy-start | bytes 98308
  60.4 125.0 %copy-start.4 = (f32[24,344]{1,0:T(8,128)}, f32[24,344]{1,0:T(8,128)S(1)}, u32[]{:S(2)}) copy-start(f32[24,344]{1,0:T(8,128)S(1)} %get-tuple-element.28) | copy-start | bytes 99076
  60.4 125.0 %copy-start.5 = (f32[24,344]{1,0:T(8,128)}, f32[24,344]{1,0:T(8,128)S(1)}, u32[]{:S(2)}) copy-start(f32[24,344]{1,0:T(8,128)S(1)} %get-tuple-element.29) | copy-start | bytes 99076
  64.4 2.7 %collective-permute-start = (f32[8]{0:T(128)S(1)}, f32[8]{0:T(128)S(1)}, u32[]{:S(2)}, u32[]{:S(2)}) collective-permute-start(f32[8]{0:T(128)S(1)} %stack.27), channel_id=1, source_target_pairs={{0,8},{8,0},{16,24},{24,16},{32,40},{40,32},{48,56},{56,48},{64,72... | collective-permute-start | bytes 104 | tf_op jit(solution)/shard_map/ppermute | solution.py:36
  67.1 2.4 %collective-permute-start.1 = (f32[8]{0:T(128)S(1)}, f32[8]{0:T(128)S(1)}, u32[]{:S(2)}, u32[]{:S(2)}) collective-permute-start(f32[8]{0:T(128)S(1)} %add.100), channel_id=1, source_target_pairs={{0,16},{8,24},{16,0},{24,8},{32,48},{40,56},{48,32},{56,40},{64,80... | collective-permute-start | bytes 104 | tf_op jit(solution)/shard_map/ppermute | solution.py:36
  69.5 3.9 %collective-permute-start.2 = (f32[8]{0:T(128)S(1)}, f32[8]{0:T(128)S(1)}, u32[]{:S(2)}, u32[]{:S(2)}) collective-permute-start(f32[8]{0:T(128)S(1)} %add.101), channel_id=1, source_target_pairs={{0,32},{8,40},{16,48},{24,56},{32,0},{40,8},{48,16},{56,24},{64,96... | collective-permute-start | bytes 104 | tf_op jit(solution)/shard_map/ppermute | solution.py:36
  73.5 2.4 %collective-permute-start.3 = (f32[8]{0:T(128)S(1)}, f32[8]{0:T(128)S(1)}, u32[]{:S(2)}, u32[]{:S(2)}) collective-permute-start(f32[8]{0:T(128)S(1)} %add.102), channel_id=1, source_target_pairs={{0,64},{8,72},{16,80},{24,88},{32,96},{40,104},{48,112},{56,120},{... | collective-permute-start | bytes 104 | tf_op jit(solution)/shard_map/ppermute | solution.py:36
  75.9 3.9 %collective-permute-start.4 = (f32[8]{0:T(128)S(1)}, f32[8]{0:T(128)S(1)}, u32[]{:S(2)}, u32[]{:S(2)}) collective-permute-start(f32[8]{0:T(128)S(1)} %add.103), channel_id=1, source_target_pairs={{0,128},{8,136},{16,144},{24,152},{32,160},{40,168},{48,176},{56,1... | collective-permute-start | bytes 104 | tf_op jit(solution)/shard_map/ppermute | solution.py:36
  79.8 2.6 %collective-permute-start.5 = (f32[8]{0:T(128)S(1)}, f32[8]{0:T(128)S(1)}, u32[]{:S(2)}, u32[]{:S(2)}) collective-permute-start(f32[8]{0:T(128)S(1)} %add.104), channel_id=1, source_target_pairs={{0,1},{1,0},{2,3},{3,2},{4,5},{5,4},{6,7},{7,6},{8,9},{9,8},{10,11... | collective-permute-start | bytes 104 | tf_op jit(solution)/shard_map/ppermute | solution.py:36
  82.4 3.9 %collective-permute-start.6 = (f32[8]{0:T(128)S(1)}, f32[8]{0:T(128)S(1)}, u32[]{:S(2)}, u32[]{:S(2)}) collective-permute-start(f32[8]{0:T(128)S(1)} %add.105), channel_id=1, source_target_pairs={{0,2},{1,3},{2,0},{3,1},{4,6},{5,7},{6,4},{7,5},{8,10},{9,11},{10,... | collective-permute-start | bytes 104 | tf_op jit(solution)/shard_map/ppermute | solution.py:36
  86.4 7.1 %collective-permute-start.7 = (f32[8]{0:T(128)S(1)}, f32[8]{0:T(128)S(1)}, u32[]{:S(2)}, u32[]{:S(2)}) collective-permute-start(f32[8]{0:T(128)S(1)} %add.106), channel_id=1, source_target_pairs={{0,4},{1,5},{2,6},{3,7},{4,0},{5,1},{6,2},{7,3},{8,12},{9,13},{10,... | collective-permute-start | bytes 104 | tf_op jit(solution)/shard_map/ppermute | solution.py:36
  191.5 3.6 %copy-start = (bf16[8,64,32,128]{3,1,0,2:T(8,128)(2,1)S(1)}, bf16[8,64,32,128]{3,1,0,2:T(8,128)(2,1)}, u32[]{:S(2)}) copy-start(bf16[8,64,32,128]{3,1,0,2:T(8,128)(2,1)} %slice_bitcast_fusion) | copy-start | bytes 12582916
Sparse Core Ops, SparseCore 0:
  116.7 61.7 all-gather.2

commit v3 on v2

--- a/solution.py
+++ b/solution.py
@@ -111,31 +111,38 @@
     gain_master_new = finish(gain_master, gain_update, sums[2], sums[5])
 
     up_low = jnp.pad(up_master_new.astype(jnp.bfloat16), ((0, 0), (0, up_pad - up_cols)))
-    low = jnp.concatenate(
+    down_low = down_master_new.astype(jnp.bfloat16).reshape(4, 16, LANES)
+    gain_low = jnp.pad(gain_master_new.astype(jnp.bfloat16), (0, LANES - gain_cols))
+    gain_low = jnp.pad(gain_low.reshape(1, LANES), ((0, 15), (0, 0)))
+    down_area = jnp.concatenate(
         [
-            down_master_new.astype(jnp.bfloat16),
-            up_low.reshape(up_rows * up_tiles, LANES),
-            jnp.pad(gain_master_new.astype(jnp.bfloat16), (0, LANES - gain_cols)).reshape(1, LANES),
-            jnp.zeros((height - gain_at - 1, LANES), jnp.bfloat16),
+            jnp.concatenate([down_low[0], down_low[1], down_low[2]], axis=1),
+            jnp.concatenate([down_low[3], gain_low, jnp.zeros((16, LANES), jnp.bfloat16)], axis=1),
         ]
     )
+    low = jnp.concatenate(
+        [up_low, jnp.zeros((32 - up_rows, up_pad), jnp.bfloat16), down_area]
+    )
     rows = lax.all_to_all(
-        jnp.broadcast_to(low[None], (n_narrow, height, LANES)), "narrow", 0, 0, tiled=True
+        jnp.broadcast_to(low[None], (n_narrow,) + low.shape), "narrow", 0, 0, tiled=True
     )
     whole = lax.all_gather(rows[None], "wide", axis=0, tiled=True)
-    down_weights = (
-        whole[:, :, :down_rows]
+    up_weights = (
+        whole[:, :, :up_rows, :up_cols]
         .transpose(1, 2, 0, 3)
-        .reshape(n_narrow * down_rows, n_wide * down_cols)
-    )
-    up_weights = (
-        whole[:, :, up_at:gain_at]
-        .reshape(n_wide, n_narrow, up_rows, up_tiles, LANES)
-        .transpose(1, 2, 0, 3, 4)
-        .reshape(n_narrow, up_rows, n_wide, up_pad)[:, :, :, :up_cols]
         .reshape(n_narrow * up_rows, n_wide * up_cols)
     )
-    gain_weights = whole[:, :, gain_at, :gain_cols].transpose(1, 0, 2).reshape(-1)
+    down_tiles = jnp.concatenate(
+        [
+            whole[:, :, 32:48, 0:128],
+            whole[:, :, 32:48, 128:256],
+            whole[:, :, 32:48, 256:384],
+            whole[:, :, 48:64, 0:128],
+        ],
+        axis=2,
+    )
+    down_weights = down_tiles.transpose(1, 2, 0, 3).reshape(n_narrow * down_rows, n_wide * down_cols)
+    gain_weights = whole[:, :, 48, 128 : 128 + gain_cols].transpose(1, 0, 2).reshape(-1)
     return (
         up_first_new,
         up_second_new,

time: 241 us -> 235 us (0.975)
  local copies, waits for them, and re-layouts: 68.3 us -> 51 us
  waiting for transfers between devices: 109 us -> 117 us
  other arithmetic: 6.01 us -> 9.08 us
    reshape x5 -> x3, local copies, waits for them, and re-layouts: 23.5 us -> 10.6 us  [the longest x1 9.86 us: body(): up_weights = whole[:, :, :up_rows, :up_cols].transpose(1, 2, 0, 3).reshap...]
    all_gather x1, waiting for transfers between devices: 61.9 us -> 69.5 us  [body(): whole = lax.all_gather(rows[None], 'wide', axis=0, tiled=True)]
    slice x3, local copies, waits for them, and re-layouts: 9.96 us -> 5.46 us  [the longest x1 4.34 us: body(): whole[:, :, 32:48, 0:128]]
    unnamed x35 -> x29, local copies, waits for them, and re-layouts: 10.3 us -> 9.13 us
where the time goes in v3:
time: 235 us
  waiting for transfers between devices  117 us (50%)
  local copies, waits for them, and re-layouts  51 us (22%)
  starting transfers between devices  22.1 us (9%)
  between operations  18.5 us (8%)
  blocking collectives  17.3 us (7%)
  other arithmetic  9.08 us (4%)
    all_gather x1, waiting for transfers between devices, body(): whole = lax.all_gather(rows[None], 'wide', axis=0, tiled=True)  69.5 us
    all_to_all x1, waiting for transfers between devices, body(): received = lax.all_to_all(packed, 'wide', 0, 0, tiled=True)  31.4 us
    all_to_all x1, blocking collectives, body(): lax.all_to_all(jnp.broadcast_to(low[None], (n_narrow,) + low.shape), 'nar...  17.3 us
    ppermute x8, waiting for transfers between devices, butterfly_sum(): x = x + lax.ppermute(x, axis, pairs)  15.6 us
    ppermute x8, starting transfers between devices, butterfly_sum(): x = x + lax.ppermute(x, axis, pairs)  13.4 us
    transpose x2, local copies, waits for them, and re-layouts, body(): up_weights = whole[:, :, :up_rows, :up_cols].transpose(1, 2, 0, 3).reshap...  12.2 us
    reshape x1, local copies, waits for them, and re-layouts, body(): up_weights = whole[:, :, :up_rows, :up_cols].transpose(1, 2, 0, 3).reshap...  9.86 us
    unnamed x29, local copies, waits for them, and re-layouts  9.13 us
  transfers between devices with their start and end apart: 10, of which 10 were waited for; matrix products, arithmetic and copies ran while one was open for 0% of the time, Pallas kernels for 0%

profile of v3, /device:TPU:1, one launch (start us, length us, event | category | flops | bytes accessed | tf_op | source)
XLA Modules:
  0.0 234.6 jit_solution(2521033180918019565)
XLA Ops:
  7.2 0.5 broadcast.86
  7.7 1.3 reduce.3
  9.0 0.1 reshape.81
  9.1 2.4 %copy.40 = f32[8,8,32,128]{3,2,1,0:T(8,128)} copy(f32[8,8,32,128]{3,1,2,0:T(8,128)} %bitcast.51) | data formatting | bytes 2097152
  11.5 2.6 %reshape_squeeze.7 = f32[24,32,344]{2,1,0:T(8,128)S(1)} reshape(f32[1,24,11008]{2,1,0:T(8,128)} %param.12) | data formatting | bytes 2113536 | tf_op jit(solution)/shard_map/reshape;squeeze | solution.py:67
  14.1 0.1 pad.20
  14.1 0.5 reshape.79
  14.7 0.1 copy.33
  14.8 0.1 pad.40.clone
  14.9 1.4 fusion
  16.4 2.8 %copy.34 = f32[32,144,128]{2,1,0:T(8,128)} copy(f32[32,144,128]{2,0,1:T(8,128)S(1)} %fusion) | data formatting | bytes 4718592 | tf_op jit(solution)/shard_map/concatenate | solution.py:72
  19.2 8.7 %all-to-all-start = ((f32[32,144,128]{2,1,0:T(8,128)}), f32[32,144,128]{2,1,0:T(8,128)S(1)}, u32[]{:S(2)}, u32[]{:S(2)}) async-start(f32[32,144,128]{2,1,0:T(8,128)} %copy.34), calls=%async_computation | async-start | bytes 4718592 | tf_op jit(solution)/shard_map/all_to_all | solution.py:81
  28.0 0.1 pad.30.clone
  28.1 31.4 %all-to-all-done = f32[32,144,128]{2,1,0:T(8,128)S(1)} async-done(((f32[32,144,128]{2,1,0:T(8,128)}), f32[32,144,128]{2,1,0:T(8,128)S(1)}, u32[]{:S(2)}, u32[]{:S(2)}) %all-to-all-start) | async-done | bytes 2359328 | tf_op jit(solution)/shard_map/all_to_all | solution.py:81
  59.4 0.1 reduce_sum.63
  59.6 1.1 multiply_reduce_fusion.4
  60.8 0.6 multiply_reduce_fusion.2
  61.4 0.7 multiply_reduce_fusion
  62.1 4.0 %stack.27 = f32[8]{0:T(128)S(1)} concatenate(f32[1]{0:T(128)} %bitcast.3, f32[1]{0:T(128)} %bitcast.4, f32[1]{0:T(128)} %bitcast.5, f32[1]{0:T(128)} %bitcast.6, f32[1]{0:T(128)} %bitcast.7, f32[1]{0:T(128)} %bitcast.9, f32[2]{0:T(128)S(1)} %broadcast.52), dimensions={0} | concatenate | bytes 64 | tf_op jit(solution)/shard_map/stack | solution.py:96
  66.1 1.9 collective-permute-start
  68.0 0.8 collective-permute-done
  68.8 2.4 %collective-permute-done.1 = f32[8]{0:T(128)S(1)} collective-permute-done((f32[8]{0:T(128)S(1)}, f32[8]{0:T(128)S(1)}, u32[]{:S(2)}, u32[]{:S(2)}) %collective-permute-start.1) | collective-permute-done | bytes 64 | tf_op jit(solution)/shard_map/ppermute | solution.py:36
  71.2 3.9 %collective-permute-done.2 = f32[8]{0:T(128)S(1)} collective-permute-done((f32[8]{0:T(128)S(1)}, f32[8]{0:T(128)S(1)}, u32[]{:S(2)}, u32[]{:S(2)}) %collective-permute-start.2) | collective-permute-done | bytes 64 | tf_op jit(solution)/shard_map/ppermute | solution.py:36
  75.2 2.4 %collective-permute-done.3 = f32[8]{0:T(128)S(1)} collective-permute-done((f32[8]{0:T(128)S(1)}, f32[8]{0:T(128)S(1)}, u32[]{:S(2)}, u32[]{:S(2)}) %collective-permute-start.3) | collective-permute-done | bytes 64 | tf_op jit(solution)/shard_map/ppermute | solution.py:36
  77.6 0.7 collective-permute-start.4
  78.3 3.2 %collective-permute-done.4 = f32[8]{0:T(128)S(1)} collective-permute-done((f32[8]{0:T(128)S(1)}, f32[8]{0:T(128)S(1)}, u32[]{:S(2)}, u32[]{:S(2)}) %collective-permute-start.4) | collective-permute-done | bytes 64 | tf_op jit(solution)/shard_map/ppermute | solution.py:36
  81.5 1.6 collective-permute-start.5
  83.2 1.0 collective-permute-done.5
  84.1 3.0 %collective-permute-start.6 = (f32[8]{0:T(128)S(1)}, f32[8]{0:T(128)S(1)}, u32[]{:S(2)}, u32[]{:S(2)}) collective-permute-start(f32[8]{0:T(128)S(1)} %add.107), channel_id=1, source_target_pairs={{0,2},{1,3},{2,0},{3,1},{4,6},{5,7},{6,4},{7,5},{8,10},{9,11},{10,... | collective-permute-start | bytes 104 | tf_op jit(solution)/shard_map/ppermute | solution.py:36
  87.1 1.0 collective-permute-done.6
  88.1 6.1 %collective-permute-start.7 = (f32[8]{0:T(128)S(1)}, f32[8]{0:T(128)S(1)}, u32[]{:S(2)}, u32[]{:S(2)}) collective-permute-start(f32[8]{0:T(128)S(1)} %add.108), channel_id=1, source_target_pairs={{0,4},{1,5},{2,6},{3,7},{4,0},{5,1},{6,2},{7,3},{8,12},{9,13},{10,... | collective-permute-start | bytes 104 | tf_op jit(solution)/shard_map/ppermute | solution.py:36
  94.2 1.0 collective-permute-done.7
  95.1 0.6 fusion.23
  100.0 0.5 fusion.17
  100.5 0.6 fusion.15
  101.2 0.6 fusion.16
  101.8 0.1 fusion.9
  101.9 17.3 %all_to_all.10 = bf16[8,64,384]{2,1,0:T(8,128)(2,1)} all-to-all(bf16[8,64,384]{2,1,0:T(8,128)(2,1)S(1)} %broadcast_in_dim.21), channel_id=1, replica_groups=mesh['wide'=32,'narrow'=8] {'narrow'}, dimensions={0} | all-to-all | bytes 786432 | tf_op jit(solution)/shard_map/all_to_all | solution.py:126
  119.2 69.5 %all-gather.3.cloned.1.call-done = bf16[256,64,384]{2,1,0:T(8,128)(2,1)} async-done(((bf16[8,64,384]{2,1,0:T(8,128)(2,1)}), bf16[256,64,384]{2,1,0:T(8,128)(2,1)}) %all-gather.3.cloned.1.call-update) | async-done | bytes 12582928 | tf_op jit(solution)/shard_map/all_gather | solution.py:129
  188.7 1.1 slice.97
  189.9 4.3 %fusion.21 = (bf16[32,8,16,128]{3,2,1,0:T(8,128)(2,1)S(1)}, bf16[32,8,16,128]{3,2,1,0:T(8,128)(2,1)S(1)}, bf16[32,8,16,128]{3,2,1,0:T(8,128)(2,1)S(1)}, bf16[32,8,16,128]{3,2,1,0:T(8,128)(2,1)}) fusion(bf16[32,8,64,384]{3,2,1,0:T(8,128)(2,1)} %bitcast.45), kind=kLoop, calls=%fused_computation.49 | loop fusion | bytes 8388608 | tf_op jit(solution)/shard_map/slice | solution.py:137
  194.2 4.9 %slice_bitcast_fusion = bf16[8,24,32,344]{3,1,0,2:T(8,128)(2,1)} fusion(bf16[32,8,64,384]{3,2,1,0:T(8,128)(2,1)} %bitcast.46), kind=kLoop, calls=%fused_computation | loop fusion | bytes 8454144 | tf_op jit(solution)/shard_map/transpose | solution.py:132
  199.2 0.7 reshape.86
  199.9 7.3 %copy.35 = bf16[8,24,32,344]{3,2,1,0:T(8,128)(2,1)} copy(bf16[8,24,32,344]{3,1,0,2:T(8,128)(2,1)} %slice_bitcast_fusion) | data formatting | bytes 8454144 | tf_op jit(solution)/shard_map/transpose | solution.py:132
  207.1 9.9 %reshape.84 = bf16[192,11008]{1,0:T(8,128)(2,1)} reshape(bf16[8,24,32,344]{3,2,1,0:T(8,128)(2,1)} %copy.35) | data formatting | bytes 8454144 | tf_op jit(solution)/shard_map/reshape | solution.py:133
  217.0 1.8 maximum_bitcast_fusion
  218.9 2.7 %copy.36 = bf16[8,64,32,128]{3,2,1,0:T(8,128)(2,1)S(1)} copy(bf16[8,64,32,128]{3,1,0,2:T(8,128)(2,1)S(1)} %maximum_bitcast_fusion) | data formatting | bytes 8388608 | tf_op jit(solution)/shard_map/transpose | solution.py:144
  221.6 6.2 %copy.44 = bf16[64,8,32,128]{3,1,2,0:T(8,128)(2,1)} copy(bf16[64,8,32,128]{3,2,1,0:T(8,128)(2,1)S(1)} %bitcast.43) | data formatting | bytes 8388608
  (49 shorter events, 0.3 us)
Async XLA Ops:
  19.1 40.5 %copy-start.10 = (f32[16]{0:T(128)S(1)}, f32[16]{0:T(128)}, u32[]{:S(2)}) copy-start(f32[16]{0:T(128)} %param.17) | copy-start | bytes 196
  19.1 40.5 %copy-start.11 = (f32[16]{0:T(128)S(1)}, f32[16]{0:T(128)}, u32[]{:S(2)}) copy-start(f32[16]{0:T(128)} %param.20) | copy-start | bytes 196
  19.1 40.5 %copy-start.12 = (f32[16]{0:T(128)S(1)}, f32[16]{0:T(128)}, u32[]{:S(2)}) copy-start(f32[16]{0:T(128)} %param.23) | copy-start | bytes 196
  19.1 41.6 %copy-start.3 = (f32[64,128]{1,0:T(8,128)S(1)}, f32[64,128]{1,0:T(8,128)}, u32[]{:S(2)}) copy-start(f32[64,128]{1,0:T(8,128)} %param.16) | copy-start | bytes 98308
  19.1 41.6 %copy-start.8 = (f32[64,128]{1,0:T(8,128)S(1)}, f32[64,128]{1,0:T(8,128)}, u32[]{:S(2)}) copy-start(f32[64,128]{1,0:T(8,128)} %param.19) | copy-start | bytes 98308
  19.2 41.6 %copy-start.9 = (f32[64,128]{1,0:T(8,128)S(1)}, f32[64,128]{1,0:T(8,128)}, u32[]{:S(2)}) copy-start(f32[64,128]{1,0:T(8,128)} %param.22) | copy-start | bytes 98308
  19.2 42.2 %copy-start = (f32[24,344]{1,0:T(8,128)S(1)}, f32[24,344]{1,0:T(8,128)}, u32[]{:S(2)}) copy-start(f32[24,344]{1,0:T(8,128)} %param.15) | copy-start | bytes 99076
  19.2 42.2 %copy-start.6 = (f32[24,344]{1,0:T(8,128)S(1)}, f32[24,344]{1,0:T(8,128)}, u32[]{:S(2)}) copy-start(f32[24,344]{1,0:T(8,128)} %param.21) | copy-start | bytes 99076
  19.2 42.2 %copy-start.7 = (f32[24,344]{1,0:T(8,128)S(1)}, f32[24,344]{1,0:T(8,128)}, u32[]{:S(2)}) copy-start(f32[24,344]{1,0:T(8,128)} %param.18) | copy-start | bytes 99076
  19.2 40.2 %all-to-all-start = ((f32[32,144,128]{2,1,0:T(8,128)}), f32[32,144,128]{2,1,0:T(8,128)S(1)}, u32[]{:S(2)}, u32[]{:S(2)}) async-start(f32[32,144,128]{2,1,0:T(8,128)} %copy.34), calls=%async_computation | async-start | bytes 4718592 | tf_op jit(solution)/shard_map/all_to_all | solution.py:81
  27.9 160.8 %all-gather.3.cloned.1.call-start = ((), (), s32[]{:S(2)}) async-start(), calls=%async_computation.2 | async-start | bytes 12976128 | tf_op jit(solution)/shard_map/all_gather | solution.py:129
  61.4 132.8 %copy-start.4 = (f32[64,128]{1,0:T(8,128)}, f32[64,128]{1,0:T(8,128)S(1)}, u32[]{:S(2)}) copy-start(f32[64,128]{1,0:T(8,128)S(1)} %get-tuple-element.26) | copy-start | bytes 98308
  61.4 132.8 %copy-start.5 = (f32[64,128]{1,0:T(8,128)}, f32[64,128]{1,0:T(8,128)S(1)}, u32[]{:S(2)}) copy-start(f32[64,128]{1,0:T(8,128)S(1)} %get-tuple-element.27) | copy-start | bytes 98308
  62.1 132.1 %copy-start.1 = (f32[24,344]{1,0:T(8,128)}, f32[24,344]{1,0:T(8,128)S(1)}, u32[]{:S(2)}) copy-start(f32[24,344]{1,0:T(8,128)S(1)} %get-tuple-element.28) | copy-start | bytes 99076
  62.1 132.1 %copy-start.2 = (f32[24,344]{1,0:T(8,128)}, f32[24,344]{1,0:T(8,128)S(1)}, u32[]{:S(2)}) copy-start(f32[24,344]{1,0:T(8,128)S(1)} %get-tuple-element.29) | copy-start | bytes 99076
  66.1 2.7 %collective-permute-start = (f32[8]{0:T(128)S(1)}, f32[8]{0:T(128)S(1)}, u32[]{:S(2)}, u32[]{:S(2)}) collective-permute-start(f32[8]{0:T(128)S(1)} %stack.27), channel_id=1, source_target_pairs={{0,8},{8,0},{16,24},{24,16},{32,40},{40,32},{48,56},{56,48},{64,72... | collective-permute-start | bytes 104 | tf_op jit(solution)/shard_map/ppermute | solution.py:36
  68.8 2.4 %collective-permute-start.1 = (f32[8]{0:T(128)S(1)}, f32[8]{0:T(128)S(1)}, u32[]{:S(2)}, u32[]{:S(2)}) collective-permute-start(f32[8]{0:T(128)S(1)} %add.102), channel_id=1, source_target_pairs={{0,16},{8,24},{16,0},{24,8},{32,48},{40,56},{48,32},{56,40},{64,80... | collective-permute-start | bytes 104 | tf_op jit(solution)/shard_map/ppermute | solution.py:36
  71.2 3.9 %collective-permute-start.2 = (f32[8]{0:T(128)S(1)}, f32[8]{0:T(128)S(1)}, u32[]{:S(2)}, u32[]{:S(2)}) collective-permute-start(f32[8]{0:T(128)S(1)} %add.103), channel_id=1, source_target_pairs={{0,32},{8,40},{16,48},{24,56},{32,0},{40,8},{48,16},{56,24},{64,96... | collective-permute-start | bytes 104 | tf_op jit(solution)/shard_map/ppermute | solution.py:36
  75.2 2.4 %collective-permute-start.3 = (f32[8]{0:T(128)S(1)}, f32[8]{0:T(128)S(1)}, u32[]{:S(2)}, u32[]{:S(2)}) collective-permute-start(f32[8]{0:T(128)S(1)} %add.104), channel_id=1, source_target_pairs={{0,64},{8,72},{16,80},{24,88},{32,96},{40,104},{48,112},{56,120},{... | collective-permute-start | bytes 104 | tf_op jit(solution)/shard_map/ppermute | solution.py:36
  77.6 3.9 %collective-permute-start.4 = (f32[8]{0:T(128)S(1)}, f32[8]{0:T(128)S(1)}, u32[]{:S(2)}, u32[]{:S(2)}) collective-permute-start(f32[8]{0:T(128)S(1)} %add.105), channel_id=1, source_target_pairs={{0,128},{8,136},{16,144},{24,152},{32,160},{40,168},{48,176},{56,1... | collective-permute-start | bytes 104 | tf_op jit(solution)/shard_map/ppermute | solution.py:36
  81.5 2.6 %collective-permute-start.5 = (f32[8]{0:T(128)S(1)}, f32[8]{0:T(128)S(1)}, u32[]{:S(2)}, u32[]{:S(2)}) collective-permute-start(f32[8]{0:T(128)S(1)} %add.106), channel_id=1, source_target_pairs={{0,1},{1,0},{2,3},{3,2},{4,5},{5,4},{6,7},{7,6},{8,9},{9,8},{10,11... | collective-permute-start | bytes 104 | tf_op jit(solution)/shard_map/ppermute | solution.py:36
  84.1 3.9 %collective-permute-start.6 = (f32[8]{0:T(128)S(1)}, f32[8]{0:T(128)S(1)}, u32[]{:S(2)}, u32[]{:S(2)}) collective-permute-start(f32[8]{0:T(128)S(1)} %add.107), channel_id=1, source_target_pairs={{0,2},{1,3},{2,0},{3,1},{4,6},{5,7},{6,4},{7,5},{8,10},{9,11},{10,... | collective-permute-start | bytes 104 | tf_op jit(solution)/shard_map/ppermute | solution.py:36
  88.1 7.1 %collective-permute-start.7 = (f32[8]{0:T(128)S(1)}, f32[8]{0:T(128)S(1)}, u32[]{:S(2)}, u32[]{:S(2)}) collective-permute-start(f32[8]{0:T(128)S(1)} %add.108), channel_id=1, source_target_pairs={{0,4},{1,5},{2,6},{3,7},{4,0},{5,1},{6,2},{7,3},{8,12},{9,13},{10,... | collective-permute-start | bytes 104 | tf_op jit(solution)/shard_map/ppermute | solution.py:36
Sparse Core Ops, SparseCore 0:
  119.4 69.3 all-gather.2

commit v4 on v3

--- a/solution.py
+++ b/solution.py
@@ -28,14 +28,19 @@
     return master - LEARN_RATE * trust * update
 
 
-def butterfly_sum(x, n_wide, n_narrow):
-    for axis, size in (("wide", n_wide), ("narrow", n_narrow)):
-        step = 1
-        while step < size:
-            pairs = [(i, i ^ step) for i in range(size)]
-            x = x + lax.ppermute(x, axis, pairs)
-            step *= 2
-    return x
+def group_sum(x, axis, masks):
+    size = lax.axis_size(axis)
+    got = [lax.ppermute(x, axis, [(i, i ^ m) for i in range(size)]) for m in masks]
+    while len(got) > 1:
+        got = [got[i] + got[i + 1] if i + 1 < len(got) else got[i] for i in range(0, len(got), 2)]
+    return x + got[0]
+
+
+def mesh_sum(x):
+    x = group_sum(x, "wide", (1,))
+    x = group_sum(x, "wide", (2, 4, 6))
+    x = group_sum(x, "wide", (8, 16, 24))
+    return group_sum(x, "narrow", tuple(range(1, lax.axis_size("narrow"))))
 
 
 def body(
@@ -105,7 +110,7 @@
             jnp.float32(0.0),
         ]
     )
-    sums = butterfly_sum(partial, n_wide, n_narrow)
+    sums = mesh_sum(partial)
     up_master_new = finish(up_master, up_update, sums[0], sums[3])
     down_master_new = finish(down_master, down_update, sums[1], sums[4])
     gain_master_new = finish(gain_master, gain_update, sums[2], sums[5])

time: 235 us -> 234 us (level)
  waiting for transfers between devices: 117 us -> 106 us
  starting transfers between devices: 22.1 us -> 32.2 us
    ppermute x8 -> x14, waiting for transfers between devices: 15.6 us -> 5.08 us  [group_sum(): lax.ppermute(x, axis, [(i, i ^ m) for i in range(size)])]
    ppermute x8 -> x14, starting transfers between devices: 13.4 us -> 23.4 us  [group_sum(): lax.ppermute(x, axis, [(i, i ^ m) for i in range(size)])]
  transfers between devices with their start and end apart: 10 -> 16, of which waited for: 10 -> 10; matrix products, arithmetic and copies ran while one was open for 0% -> 0% of each run, Pallas kernels for 0% -> 0%
where the time goes in v4:
time: 234 us; the launch traced here: 233 us
  waiting for transfers between devices  106 us (45%)
  local copies, waits for them, and re-layouts  51 us (22%)
  starting transfers between devices  32.2 us (14%)
  between operations  18.5 us (8%)
  blocking collectives  15.9 us (7%)
  other arithmetic  9.08 us (4%)
    all_gather x1, waiting for transfers between devices, body(): whole = lax.all_gather(rows[None], 'wide', axis=0, tiled=True)  69.7 us
    all_to_all x1, waiting for transfers between devices, body(): received = lax.all_to_all(packed, 'wide', 0, 0, tiled=True)  31.4 us
    ppermute x14, starting transfers between devices, group_sum(): lax.ppermute(x, axis, [(i, i ^ m) for i in range(size)])  23.4 us
    all_to_all x1, blocking collectives, body(): lax.all_to_all(jnp.broadcast_to(low[None], (n_narrow,) + low.shape), 'nar...  15.9 us
    transpose x2, local copies, waits for them, and re-layouts, body(): up_weights = whole[:, :, :up_rows, :up_cols].transpose(1, 2, 0, 3).reshap...  12.2 us
    reshape x1, local copies, waits for them, and re-layouts, body(): up_weights = whole[:, :, :up_rows, :up_cols].transpose(1, 2, 0, 3).reshap...  9.86 us
    unnamed x29, local copies, waits for them, and re-layouts  9.13 us
    all_to_all x1, starting transfers between devices, body(): received = lax.all_to_all(packed, 'wide', 0, 0, tiled=True)  8.72 us
  transfers between devices with their start and end apart: 16, of which 10 were waited for; matrix products, arithmetic and copies ran while one was open for 0% of the time, Pallas kernels for 0%

profile of v4, /device:TPU:1, one launch (start us, length us, event | category | flops | bytes accessed | tf_op | source)
XLA Modules:
  0.0 232.9 jit_solution(4109912664594950240)
XLA Ops:
  7.2 0.5 broadcast.86
  7.7 1.3 reduce.3
  9.1 2.4 %copy.40 = f32[8,8,32,128]{3,2,1,0:T(8,128)} copy(f32[8,8,32,128]{3,1,2,0:T(8,128)} %bitcast.51) | data formatting | bytes 2097152
  11.5 2.6 %reshape_squeeze.7 = f32[24,32,344]{2,1,0:T(8,128)S(1)} reshape(f32[1,24,11008]{2,1,0:T(8,128)} %param.12) | data formatting | bytes 2113536 | tf_op jit(solution)/shard_map/reshape;squeeze | solution.py:72
  14.1 0.5 reshape.79
  14.9 1.4 fusion
  16.4 2.8 %copy.34 = f32[32,144,128]{2,1,0:T(8,128)} copy(f32[32,144,128]{2,0,1:T(8,128)S(1)} %fusion) | data formatting | bytes 4718592 | tf_op jit(solution)/shard_map/concatenate | solution.py:77
  19.2 8.7 %all-to-all-start = ((f32[32,144,128]{2,1,0:T(8,128)}), f32[32,144,128]{2,1,0:T(8,128)S(1)}, u32[]{:S(2)}, u32[]{:S(2)}) async-start(f32[32,144,128]{2,1,0:T(8,128)} %copy.34), calls=%async_computation | async-start | bytes 4718592 | tf_op jit(solution)/shard_map/all_to_all | solution.py:86
  28.1 31.4 %all-to-all-done = f32[32,144,128]{2,1,0:T(8,128)S(1)} async-done(((f32[32,144,128]{2,1,0:T(8,128)}), f32[32,144,128]{2,1,0:T(8,128)S(1)}, u32[]{:S(2)}, u32[]{:S(2)}) %all-to-all-start) | async-done | bytes 2359328 | tf_op jit(solution)/shard_map/all_to_all | solution.py:86
  59.6 1.1 multiply_reduce_fusion.4
  60.8 0.6 multiply_reduce_fusion.2
  61.4 0.7 multiply_reduce_fusion
  62.1 4.0 %stack.27 = f32[8]{0:T(128)S(1)} concatenate(f32[1]{0:T(128)} %bitcast.3, f32[1]{0:T(128)} %bitcast.4, f32[1]{0:T(128)} %bitcast.5, f32[1]{0:T(128)} %bitcast.6, f32[1]{0:T(128)} %bitcast.7, f32[1]{0:T(128)} %bitcast.9, f32[2]{0:T(128)S(1)} %broadcast.52), dimensions={0} | concatenate | bytes 64 | tf_op jit(solution)/shard_map/stack | solution.py:101
  66.1 1.9 collective-permute-start
  68.0 0.8 collective-permute-done
  68.8 1.0 collective-permute-start.2
  69.8 2.2 collective-permute-start.1
  72.1 0.4 collective-permute-done.3
  72.4 0.3 collective-permute-done.2
  72.7 0.3 collective-permute-done.1
  73.0 1.2 collective-permute-start.6
  74.3 1.2 collective-permute-start.5
  75.5 0.8 collective-permute-start.4
  76.3 0.4 collective-permute-done.6
  76.7 1.5 collective-permute-done.5
  78.2 5.7 %collective-permute-start.13 = (f32[8]{0:T(128)S(1)}, f32[8]{0:T(128)S(1)}, u32[]{:S(2)}, u32[]{:S(2)}) collective-permute-start(f32[8]{0:T(128)S(1)} %add_add_fusion.1), channel_id=1, source_target_pairs={{0,7},{1,6},{2,5},{3,4},{4,3},{5,2},{6,1},{7,0},{8,15},{9,14},{10,... | collective-permute-start | bytes 104 | tf_op jit(solution)/shard_map/ppermute | solution.py:33
  83.9 0.5 collective-permute-start.12
  84.4 3.5 %collective-permute-start.11 = (f32[8]{0:T(128)S(1)}, f32[8]{0:T(128)S(1)}, u32[]{:S(2)}, u32[]{:S(2)}) collective-permute-start(f32[8]{0:T(128)S(1)} %add_add_fusion.1), channel_id=1, source_target_pairs={{0,5},{1,4},{2,7},{3,6},{4,1},{5,0},{6,3},{7,2},{8,13},{9,12},{10,... | collective-permute-start | bytes 104 | tf_op jit(solution)/shard_map/ppermute | solution.py:33
  87.9 1.8 collective-permute-start.10
  89.7 1.6 collective-permute-start.9
  91.3 1.9 collective-permute-start.7
  93.2 1.0 collective-permute-done.10
  94.2 0.4 collective-permute-done.8
  94.6 0.6 fusion.23
  99.5 0.5 fusion.17
  100.0 0.6 fusion.15
  100.7 0.6 fusion.16
  101.4 15.9 %all_to_all.10 = bf16[8,64,384]{2,1,0:T(8,128)(2,1)} all-to-all(bf16[8,64,384]{2,1,0:T(8,128)(2,1)S(1)} %broadcast_in_dim.21), channel_id=1, replica_groups=mesh['wide'=32,'narrow'=8] {'narrow'}, dimensions={0} | all-to-all | bytes 786432 | tf_op jit(solution)/shard_map/all_to_all | solution.py:131
  117.3 69.7 %all-gather.3.cloned.1.call-done = bf16[256,64,384]{2,1,0:T(8,128)(2,1)} async-done(((bf16[8,64,384]{2,1,0:T(8,128)(2,1)}), bf16[256,64,384]{2,1,0:T(8,128)(2,1)}) %all-gather.3.cloned.1.call-update) | async-done | bytes 12582928 | tf_op jit(solution)/shard_map/all_gather | solution.py:134
  187.0 1.1 slice.97
  188.2 4.3 %fusion.21 = (bf16[32,8,16,128]{3,2,1,0:T(8,128)(2,1)S(1)}, bf16[32,8,16,128]{3,2,1,0:T(8,128)(2,1)S(1)}, bf16[32,8,16,128]{3,2,1,0:T(8,128)(2,1)S(1)}, bf16[32,8,16,128]{3,2,1,0:T(8,128)(2,1)}) fusion(bf16[32,8,64,384]{3,2,1,0:T(8,128)(2,1)} %bitcast.45), kind=kLoop, calls=%fused_computation.52 | loop fusion | bytes 8388608 | tf_op jit(solution)/shard_map/slice | solution.py:142
  192.5 4.9 %slice_bitcast_fusion = bf16[8,24,32,344]{3,1,0,2:T(8,128)(2,1)} fusion(bf16[32,8,64,384]{3,2,1,0:T(8,128)(2,1)} %bitcast.46), kind=kLoop, calls=%fused_computation | loop fusion | bytes 8454144 | tf_op jit(solution)/shard_map/transpose | solution.py:137
  197.5 0.7 reshape.86
  198.2 7.2 %copy.35 = bf16[8,24,32,344]{3,2,1,0:T(8,128)(2,1)} copy(bf16[8,24,32,344]{3,1,0,2:T(8,128)(2,1)} %slice_bitcast_fusion) | data formatting | bytes 8454144 | tf_op jit(solution)/shard_map/transpose | solution.py:137
  205.4 9.9 %reshape.84 = bf16[192,11008]{1,0:T(8,128)(2,1)} reshape(bf16[8,24,32,344]{3,2,1,0:T(8,128)(2,1)} %copy.35) | data formatting | bytes 8454144 | tf_op jit(solution)/shard_map/reshape | solution.py:138
  215.3 1.8 maximum_bitcast_fusion
  217.2 2.7 %copy.36 = bf16[8,64,32,128]{3,2,1,0:T(8,128)(2,1)S(1)} copy(bf16[8,64,32,128]{3,1,0,2:T(8,128)(2,1)S(1)} %maximum_bitcast_fusion) | data formatting | bytes 8388608 | tf_op jit(solution)/shard_map/transpose | solution.py:149
  219.9 6.2 %copy.44 = bf16[64,8,32,128]{3,1,2,0:T(8,128)(2,1)} copy(bf16[64,8,32,128]{3,2,1,0:T(8,128)(2,1)S(1)} %bitcast.43) | data formatting | bytes 8388608
  (57 shorter events, 0.9 us)
Async XLA Ops:
  19.1 40.5 %copy-start.10 = (f32[16]{0:T(128)S(1)}, f32[16]{0:T(128)}, u32[]{:S(2)}) copy-start(f32[16]{0:T(128)} %param.17) | copy-start | bytes 196
  19.1 40.5 %copy-start.11 = (f32[16]{0:T(128)S(1)}, f32[16]{0:T(128)}, u32[]{:S(2)}) copy-start(f32[16]{0:T(128)} %param.20) | copy-start | bytes 196
  19.1 40.5 %copy-start.12 = (f32[16]{0:T(128)S(1)}, f32[16]{0:T(128)}, u32[]{:S(2)}) copy-start(f32[16]{0:T(128)} %param.23) | copy-start | bytes 196
  19.1 41.6 %copy-start.3 = (f32[64,128]{1,0:T(8,128)S(1)}, f32[64,128]{1,0:T(8,128)}, u32[]{:S(2)}) copy-start(f32[64,128]{1,0:T(8,128)} %param.16) | copy-start | bytes 98308
  19.1 41.6 %copy-start.8 = (f32[64,128]{1,0:T(8,128)S(1)}, f32[64,128]{1,0:T(8,128)}, u32[]{:S(2)}) copy-start(f32[64,128]{1,0:T(8,128)} %param.19) | copy-start | bytes 98308
  19.2 41.6 %copy-start.9 = (f32[64,128]{1,0:T(8,128)S(1)}, f32[64,128]{1,0:T(8,128)}, u32[]{:S(2)}) copy-start(f32[64,128]{1,0:T(8,128)} %param.22) | copy-start | bytes 98308
  19.2 42.2 %copy-start = (f32[24,344]{1,0:T(8,128)S(1)}, f32[24,344]{1,0:T(8,128)}, u32[]{:S(2)}) copy-start(f32[24,344]{1,0:T(8,128)} %param.15) | copy-start | bytes 99076
  19.2 42.2 %copy-start.6 = (f32[24,344]{1,0:T(8,128)S(1)}, f32[24,344]{1,0:T(8,128)}, u32[]{:S(2)}) copy-start(f32[24,344]{1,0:T(8,128)} %param.21) | copy-start | bytes 99076
  19.2 42.2 %copy-start.7 = (f32[24,344]{1,0:T(8,128)S(1)}, f32[24,344]{1,0:T(8,128)}, u32[]{:S(2)}) copy-start(f32[24,344]{1,0:T(8,128)} %param.18) | copy-start | bytes 99076
  19.2 40.2 %all-to-all-start = ((f32[32,144,128]{2,1,0:T(8,128)}), f32[32,144,128]{2,1,0:T(8,128)S(1)}, u32[]{:S(2)}, u32[]{:S(2)}) async-start(f32[32,144,128]{2,1,0:T(8,128)} %copy.34), calls=%async_computation | async-start | bytes 4718592 | tf_op jit(solution)/shard_map/all_to_all | solution.py:86
  27.9 159.1 %all-gather.3.cloned.1.call-start = ((), (), s32[]{:S(2)}) async-start(), calls=%async_computation.2 | async-start | bytes 12976128 | tf_op jit(solution)/shard_map/all_gather | solution.py:134
  61.4 131.1 %copy-start.4 = (f32[64,128]{1,0:T(8,128)}, f32[64,128]{1,0:T(8,128)S(1)}, u32[]{:S(2)}) copy-start(f32[64,128]{1,0:T(8,128)S(1)} %get-tuple-element.26) | copy-start | bytes 98308
  61.4 131.1 %copy-start.5 = (f32[64,128]{1,0:T(8,128)}, f32[64,128]{1,0:T(8,128)S(1)}, u32[]{:S(2)}) copy-start(f32[64,128]{1,0:T(8,128)S(1)} %get-tuple-element.27) | copy-start | bytes 98308
  62.1 130.4 %copy-start.1 = (f32[24,344]{1,0:T(8,128)}, f32[24,344]{1,0:T(8,128)S(1)}, u32[]{:S(2)}) copy-start(f32[24,344]{1,0:T(8,128)S(1)} %get-tuple-element.28) | copy-start | bytes 99076
  62.1 130.4 %copy-start.2 = (f32[24,344]{1,0:T(8,128)}, f32[24,344]{1,0:T(8,128)S(1)}, u32[]{:S(2)}) copy-start(f32[24,344]{1,0:T(8,128)S(1)} %get-tuple-element.29) | copy-start | bytes 99076
  66.1 2.7 %collective-permute-start = (f32[8]{0:T(128)S(1)}, f32[8]{0:T(128)S(1)}, u32[]{:S(2)}, u32[]{:S(2)}) collective-permute-start(f32[8]{0:T(128)S(1)} %stack.27), channel_id=1, source_target_pairs={{0,8},{8,0},{16,24},{24,16},{32,40},{40,32},{48,56},{56,48},{64,72... | collective-permute-start | bytes 104 | tf_op jit(solution)/shard_map/ppermute | solution.py:33
  68.8 3.6 %collective-permute-start.3 = (f32[8]{0:T(128)S(1)}, f32[8]{0:T(128)S(1)}, u32[]{:S(2)}, u32[]{:S(2)}) collective-permute-start(f32[8]{0:T(128)S(1)} %add.120), channel_id=1, source_target_pairs={{0,48},{8,56},{16,32},{24,40},{32,16},{40,24},{48,0},{56,8},{64,11... | collective-permute-start | bytes 104 | tf_op jit(solution)/shard_map/ppermute | solution.py:33
  68.8 3.9 %collective-permute-start.2 = (f32[8]{0:T(128)S(1)}, f32[8]{0:T(128)S(1)}, u32[]{:S(2)}, u32[]{:S(2)}) collective-permute-start(f32[8]{0:T(128)S(1)} %add.120), channel_id=1, source_target_pairs={{0,32},{8,40},{16,48},{24,56},{32,0},{40,8},{48,16},{56,24},{64,96... | collective-permute-start | bytes 104 | tf_op jit(solution)/shard_map/ppermute | solution.py:33
  69.8 3.2 %collective-permute-start.1 = (f32[8]{0:T(128)S(1)}, f32[8]{0:T(128)S(1)}, u32[]{:S(2)}, u32[]{:S(2)}) collective-permute-start(f32[8]{0:T(128)S(1)} %add.120), channel_id=1, source_target_pairs={{0,16},{8,24},{16,0},{24,8},{32,48},{40,56},{48,32},{56,40},{64,80... | collective-permute-start | bytes 104 | tf_op jit(solution)/shard_map/ppermute | solution.py:33
  73.0 3.6 %collective-permute-start.6 = (f32[8]{0:T(128)S(1)}, f32[8]{0:T(128)S(1)}, u32[]{:S(2)}, u32[]{:S(2)}) collective-permute-start(f32[8]{0:T(128)S(1)} %add_add_fusion.2), channel_id=1, source_target_pairs={{0,192},{8,200},{16,208},{24,216},{32,224},{40,232},{48,240},{56,2... | collective-permute-start | bytes 104 | tf_op jit(solution)/shard_map/ppermute | solution.py:33
  74.3 3.9 %collective-permute-start.5 = (f32[8]{0:T(128)S(1)}, f32[8]{0:T(128)S(1)}, u32[]{:S(2)}, u32[]{:S(2)}) collective-permute-start(f32[8]{0:T(128)S(1)} %add_add_fusion.2), channel_id=1, source_target_pairs={{0,128},{8,136},{16,144},{24,152},{32,160},{40,168},{48,176},{56,1... | collective-permute-start | bytes 104 | tf_op jit(solution)/shard_map/ppermute | solution.py:33
  75.5 2.7 %collective-permute-start.4 = (f32[8]{0:T(128)S(1)}, f32[8]{0:T(128)S(1)}, u32[]{:S(2)}, u32[]{:S(2)}) collective-permute-start(f32[8]{0:T(128)S(1)} %add_add_fusion.2), channel_id=1, source_target_pairs={{0,64},{8,72},{16,80},{24,88},{32,96},{40,104},{48,112},{56,120},{... | collective-permute-start | bytes 104 | tf_op jit(solution)/shard_map/ppermute | solution.py:33
  78.2 13.1 %collective-permute-start.13 = (f32[8]{0:T(128)S(1)}, f32[8]{0:T(128)S(1)}, u32[]{:S(2)}, u32[]{:S(2)}) collective-permute-start(f32[8]{0:T(128)S(1)} %add_add_fusion.1), channel_id=1, source_target_pairs={{0,7},{1,6},{2,5},{3,4},{4,3},{5,2},{6,1},{7,0},{8,15},{9,14},{10,... | collective-permute-start | bytes 104 | tf_op jit(solution)/shard_map/ppermute | solution.py:33
  83.9 7.5 %collective-permute-start.12 = (f32[8]{0:T(128)S(1)}, f32[8]{0:T(128)S(1)}, u32[]{:S(2)}, u32[]{:S(2)}) collective-permute-start(f32[8]{0:T(128)S(1)} %add_add_fusion.1), channel_id=1, source_target_pairs={{0,6},{1,7},{2,4},{3,5},{4,2},{5,3},{6,0},{7,1},{8,14},{9,15},{10,... | collective-permute-start | bytes 104 | tf_op jit(solution)/shard_map/ppermute | solution.py:33
  84.4 8.8 %collective-permute-start.11 = (f32[8]{0:T(128)S(1)}, f32[8]{0:T(128)S(1)}, u32[]{:S(2)}, u32[]{:S(2)}) collective-permute-start(f32[8]{0:T(128)S(1)} %add_add_fusion.1), channel_id=1, source_target_pairs={{0,5},{1,4},{2,7},{3,6},{4,1},{5,0},{6,3},{7,2},{8,13},{9,12},{10,... | collective-permute-start | bytes 104 | tf_op jit(solution)/shard_map/ppermute | solution.py:33
  87.9 6.3 %collective-permute-start.10 = (f32[8]{0:T(128)S(1)}, f32[8]{0:T(128)S(1)}, u32[]{:S(2)}, u32[]{:S(2)}) collective-permute-start(f32[8]{0:T(128)S(1)} %add_add_fusion.1), channel_id=1, source_target_pairs={{0,4},{1,5},{2,6},{3,7},{4,0},{5,1},{6,2},{7,3},{8,12},{9,13},{10,... | collective-permute-start | bytes 104 | tf_op jit(solution)/shard_map/ppermute | solution.py:33
  89.7 4.5 %collective-permute-start.9 = (f32[8]{0:T(128)S(1)}, f32[8]{0:T(128)S(1)}, u32[]{:S(2)}, u32[]{:S(2)}) collective-permute-start(f32[8]{0:T(128)S(1)} %add_add_fusion.1), channel_id=1, source_target_pairs={{0,3},{1,2},{2,1},{3,0},{4,7},{5,6},{6,5},{7,4},{8,11},{9,10},{10,... | collective-permute-start | bytes 104 | tf_op jit(solution)/shard_map/ppermute | solution.py:33
  91.3 3.3 %collective-permute-start.8 = (f32[8]{0:T(128)S(1)}, f32[8]{0:T(128)S(1)}, u32[]{:S(2)}, u32[]{:S(2)}) collective-permute-start(f32[8]{0:T(128)S(1)} %add_add_fusion.1), channel_id=1, source_target_pairs={{0,2},{1,3},{2,0},{3,1},{4,6},{5,7},{6,4},{7,5},{8,10},{9,11},{10,... | collective-permute-start | bytes 104 | tf_op jit(solution)/shard_map/ppermute | solution.py:33
  91.3 3.3 %collective-permute-start.7 = (f32[8]{0:T(128)S(1)}, f32[8]{0:T(128)S(1)}, u32[]{:S(2)}, u32[]{:S(2)}) collective-permute-start(f32[8]{0:T(128)S(1)} %add_add_fusion.1), channel_id=1, source_target_pairs={{0,1},{1,0},{2,3},{3,2},{4,5},{5,4},{6,7},{7,6},{8,9},{9,8},{10,11... | collective-permute-start | bytes 104 | tf_op jit(solution)/shard_map/ppermute | solution.py:33
Sparse Core Ops, SparseCore 0:
  117.5 69.5 all-gather.2

commit v5 on v4

--- a/solution.py
+++ b/solution.py
@@ -2,6 +2,8 @@
 import jax.numpy as jnp
 from jax import lax
 from jax.sharding import PartitionSpec as P
+from jax.experimental import pallas as pl
+from jax.experimental.pallas import tpu as pltpu
 
 BETA_ONE = 0.9
 BETA_TWO = 0.999
@@ -40,7 +42,48 @@
     x = group_sum(x, "wide", (1,))
     x = group_sum(x, "wide", (2, 4, 6))
     x = group_sum(x, "wide", (8, 16, 24))
-    return group_sum(x, "narrow", tuple(range(1, lax.axis_size("narrow"))))
+    step = 1
+    while step < lax.axis_size("narrow"):
+        x = group_sum(x, "narrow", (step,))
+        step *= 2
+    return x
+
+
+def unpack(whole, up_shape, down_shape):
+    n_wide, n_narrow, height, width = whole.shape
+    up_rows, up_cols = up_shape
+    down_rows, down_cols = down_shape
+    per = 2
+
+    def kernel(in_ref, up_ref, down_ref):
+        for j in range(per):
+            for w in range(n_wide):
+                up_ref[up_rows * j : up_rows * (j + 1), up_cols * w : up_cols * (w + 1)] = in_ref[
+                    w, j, :up_rows, :up_cols
+                ]
+                for t in range(down_rows // 16):
+                    row = 32 + 16 * (t // 3)
+                    lane = LANES * (t % 3)
+                    down_ref[
+                        down_rows * j + 16 * t : down_rows * j + 16 * (t + 1),
+                        down_cols * w : down_cols * (w + 1),
+                    ] = in_ref[w, j, row : row + 16, lane : lane + LANES]
+
+    moved = whole.size * 2 + (up_rows * up_cols + down_rows * down_cols) * n_wide * n_narrow * 2
+    return pl.pallas_call(
+        kernel,
+        grid=(n_narrow // per,),
+        in_specs=[pl.BlockSpec((n_wide, per, height, width), lambda i: (0, i, 0, 0))],
+        out_specs=[
+            pl.BlockSpec((per * up_rows, n_wide * up_cols), lambda i: (i, 0)),
+            pl.BlockSpec((per * down_rows, n_wide * down_cols), lambda i: (i, 0)),
+        ],
+        out_shape=[
+            jax.ShapeDtypeStruct((n_narrow * up_rows, n_wide * up_cols), jnp.bfloat16),
+            jax.ShapeDtypeStruct((n_narrow * down_rows, n_wide * down_cols), jnp.bfloat16),
+        ],
+        cost_estimate=pl.CostEstimate(flops=0, transcendentals=0, bytes_accessed=moved),
+    )(whole)
 
 
 def body(
@@ -132,21 +175,7 @@
         jnp.broadcast_to(low[None], (n_narrow,) + low.shape), "narrow", 0, 0, tiled=True
     )
     whole = lax.all_gather(rows[None], "wide", axis=0, tiled=True)
-    up_weights = (
-        whole[:, :, :up_rows, :up_cols]
-        .transpose(1, 2, 0, 3)
-        .reshape(n_narrow * up_rows, n_wide * up_cols)
-    )
-    down_tiles = jnp.concatenate(
-        [
-            whole[:, :, 32:48, 0:128],
-            whole[:, :, 32:48, 128:256],
-            whole[:, :, 32:48, 256:384],
-            whole[:, :, 48:64, 0:128],
-        ],
-        axis=2,
-    )
-    down_weights = down_tiles.transpose(1, 2, 0, 3).reshape(n_narrow * down_rows, n_wide * down_cols)
+    up_weights, down_weights = unpack(whole, up_master.shape, down_master.shape)
     gain_weights = whole[:, :, 48, 128 : 128 + gain_cols].transpose(1, 0, 2).reshape(-1)
     return (
         up_first_new,

time: 234 us -> 204 us (0.87)
  local copies, waits for them, and re-layouts: 51 us -> 14.7 us
  Pallas kernels: 0 us -> 8.59 us
  waiting for transfers between devices: 106 us -> 110 us
  starting transfers between devices: 32.2 us -> 29 us
  other arithmetic: 9.08 us -> 6.01 us
    transpose x3 -> x0, local copies, waits for them, and re-layouts: 14.9 us -> none  [the longest x2 12.2 us: body(): up_weights = whole[:, :, :up_rows, :up_cols].transpose(1, 2, 0, 3).reshap...]
    reshape x1 -> x0, local copies, waits for them, and re-layouts: 9.86 us -> none  [body(): up_weights = whole[:, :, :up_rows, :up_cols].transpose(1, 2, 0, 3).reshap...]
    pallas_call x0 -> x1, Pallas kernels: none -> 8.59 us  [unpack(): pl.pallas_call(kernel, grid=(n_narrow // per,), in_specs=[pl.BlockSpec((n...]
    unnamed x29 -> x30, local copies, waits for them, and re-layouts: 9.13 us -> 1.85 us
    slice x1 -> x0, local copies, waits for them, and re-layouts: 4.34 us -> none  [body(): whole[:, :, 32:48, 0:128]]
    all_gather x1, waiting for transfers between devices: 69.7 us -> 73 us  [body(): whole = lax.all_gather(rows[None], 'wide', axis=0, tiled=True)]
    ppermute x14 -> x10, starting transfers between devices: 23.4 us -> 20.4 us  [group_sum(): lax.ppermute(x, axis, [(i, i ^ m) for i in range(size)])]
    ppermute x14 -> x10, waiting for transfers between devices: 5.08 us -> 5.6 us  [group_sum(): lax.ppermute(x, axis, [(i, i ^ m) for i in range(size)])]
  transfers between devices with their start and end apart: 16 -> 12, of which waited for: 10 -> 8; matrix products, arithmetic and copies ran while one was open for 0% -> 0% of each run, Pallas kernels for 0% -> 0%
where the time goes in v5:
time: 204 us
  waiting for transfers between devices  110 us (54%)
  starting transfers between devices  29 us (14%)
  between operations  18.6 us (9%)
  blocking collectives  17.3 us (8%)
  local copies, waits for them, and re-layouts  14.7 us (7%)
  Pallas kernels  8.59 us (4%)
  other arithmetic  6.01 us (3%)
    all_gather x1, waiting for transfers between devices, body(): whole = lax.all_gather(rows[None], 'wide', axis=0, tiled=True)  73 us
    all_to_all x1, waiting for transfers between devices, body(): received = lax.all_to_all(packed, 'wide', 0, 0, tiled=True)  31.3 us
    ppermute x10, starting transfers between devices, group_sum(): lax.ppermute(x, axis, [(i, i ^ m) for i in range(size)])  20.4 us
    all_to_all x1, blocking collectives, body(): lax.all_to_all(jnp.broadcast_to(low[None], (n_narrow,) + low.shape), 'nar...  17.3 us
    pallas_call x1, Pallas kernels, unpack(): pl.pallas_call(kernel, grid=(n_narrow // per,), in_specs=[pl.BlockSpec((n...  8.59 us
    all_to_all x1, starting transfers between devices, body(): received = lax.all_to_all(packed, 'wide', 0, 0, tiled=True)  8.58 us
    ppermute x10, waiting for transfers between devices, group_sum(): lax.ppermute(x, axis, [(i, i ^ m) for i in range(size)])  5.6 us
  transfers between devices with their start and end apart: 12, of which 8 were waited for; matrix products, arithmetic and copies ran while one was open for 0% of the time, Pallas kernels for 0%

profile of v5, /device:TPU:1, one launch (start us, length us, event | category | flops | bytes accessed | tf_op | source)
XLA Modules:
  0.0 204.0 jit_solution(11110665861281665478)
XLA Ops:
  7.2 0.5 broadcast.86
  7.7 1.3 reduce.3
  9.0 0.1 reshape.75
  9.1 2.6 %reshape_squeeze.7 = f32[24,32,344]{2,1,0:T(8,128)S(1)} reshape(f32[1,24,11008]{2,1,0:T(8,128)} %param.12) | data formatting | bytes 2113536 | tf_op jit(solution)/shard_map/reshape;squeeze | solution.py:115
  11.7 0.1 pad.20
  11.8 0.5 reshape.73
  12.3 0.1 copy.29
  12.5 1.1 copy-done
  13.5 0.2 copy.34
  13.7 0.1 pad.36.clone
  13.8 0.2 fusion
  14.0 2.8 %copy.30 = f32[32,144,128]{2,1,0:T(8,128)} copy(f32[32,144,128]{2,0,1:T(8,128)S(1)} %fusion) | data formatting | bytes 4718592 | tf_op jit(solution)/shard_map/concatenate | solution.py:120
  16.8 8.6 %all-to-all-start = ((f32[32,144,128]{2,1,0:T(8,128)}), f32[32,144,128]{2,1,0:T(8,128)S(1)}, u32[]{:S(2)}, u32[]{:S(2)}) async-start(f32[32,144,128]{2,1,0:T(8,128)} %copy.30), calls=%async_computation | async-start | bytes 4718592 | tf_op jit(solution)/shard_map/all_to_all | solution.py:129
  25.4 0.0 copy-start.4
  25.4 0.0 copy-start.9
  25.5 0.0 all-gather.3.cloned.1.call-start
  25.6 0.1 pad.26.clone
  25.6 31.3 %all-to-all-done = f32[32,144,128]{2,1,0:T(8,128)S(1)} async-done(((f32[32,144,128]{2,1,0:T(8,128)}), f32[32,144,128]{2,1,0:T(8,128)S(1)}, u32[]{:S(2)}, u32[]{:S(2)}) %all-to-all-start) | async-done | bytes 2359328 | tf_op jit(solution)/shard_map/all_to_all | solution.py:129
  56.9 0.1 reduce_sum.63
  57.1 0.6 multiply_reduce_fusion.2
  57.7 0.0 copy-start.6
  57.7 1.1 multiply_reduce_fusion.4
  58.9 0.6 multiply_reduce_fusion
  59.5 4.0 %stack.27 = f32[8]{0:T(128)S(1)} concatenate(f32[1]{0:T(128)} %bitcast.3, f32[1]{0:T(128)} %bitcast.4, f32[1]{0:T(128)} %bitcast.5, f32[1]{0:T(128)} %bitcast.6, f32[1]{0:T(128)} %bitcast.7, f32[1]{0:T(128)} %bitcast.9, f32[2]{0:T(128)S(1)} %broadcast.52), dimensions={0} | concatenate | bytes 64 | tf_op jit(solution)/shard_map/stack | solution.py:144
  63.5 1.9 collective-permute-start
  65.4 0.8 collective-permute-done
  66.3 3.9 %collective-permute-start.2 = (f32[8]{0:T(128)S(1)}, f32[8]{0:T(128)S(1)}, u32[]{:S(2)}, u32[]{:S(2)}) collective-permute-start(f32[8]{0:T(128)S(1)} %add.108), channel_id=1, source_target_pairs={{0,32},{8,40},{16,48},{24,56},{32,0},{40,8},{48,16},{56,24},{64,96... | collective-permute-start | bytes 104 | tf_op jit(solution)/shard_map/ppermute | solution.py:35
  70.1 1.0 collective-permute-done.2
  71.1 0.5 collective-permute-start.6
  71.6 3.3 %collective-permute-start.5 = (f32[8]{0:T(128)S(1)}, f32[8]{0:T(128)S(1)}, u32[]{:S(2)}, u32[]{:S(2)}) collective-permute-start(f32[8]{0:T(128)S(1)} %add_add_fusion.1), channel_id=1, source_target_pairs={{0,128},{8,136},{16,144},{24,152},{32,160},{40,168},{48,176},{56,1... | collective-permute-start | bytes 104 | tf_op jit(solution)/shard_map/ppermute | solution.py:35
  75.0 1.0 collective-permute-done.5
  75.9 1.6 collective-permute-start.7
  77.5 1.0 collective-permute-done.7
  78.5 3.0 %collective-permute-start.8 = (f32[8]{0:T(128)S(1)}, f32[8]{0:T(128)S(1)}, u32[]{:S(2)}, u32[]{:S(2)}) collective-permute-start(f32[8]{0:T(128)S(1)} %add.115), channel_id=1, source_target_pairs={{0,2},{1,3},{2,0},{3,1},{4,6},{5,7},{6,4},{7,5},{8,10},{9,11},{10,... | collective-permute-start | bytes 104 | tf_op jit(solution)/shard_map/ppermute | solution.py:35
  81.5 1.0 collective-permute-done.8
  82.5 6.1 %collective-permute-start.9 = (f32[8]{0:T(128)S(1)}, f32[8]{0:T(128)S(1)}, u32[]{:S(2)}, u32[]{:S(2)}) collective-permute-start(f32[8]{0:T(128)S(1)} %add.116), channel_id=1, source_target_pairs={{0,4},{1,5},{2,6},{3,7},{4,0},{5,1},{6,2},{7,3},{8,12},{9,13},{10,... | collective-permute-start | bytes 104 | tf_op jit(solution)/shard_map/ppermute | solution.py:35
  88.6 1.0 collective-permute-done.9
  89.5 0.6 fusion.22
  93.0 0.5 fusion.17
  94.9 0.6 fusion.15
  95.6 0.6 fusion.16
  96.2 0.1 fusion.9
  96.3 17.3 %all_to_all.10 = bf16[8,64,384]{2,1,0:T(8,128)(2,1)} all-to-all(bf16[8,64,384]{2,1,0:T(8,128)(2,1)S(1)} %broadcast_in_dim.21), channel_id=1, replica_groups=mesh['wide'=32,'narrow'=8] {'narrow'}, dimensions={0} | all-to-all | bytes 786432 | tf_op jit(solution)/shard_map/all_to_all | solution.py:174
  113.6 0.0 all-gather.3.cloned.1.call-update
  113.6 73.0 %all-gather.3.cloned.1.call-done = bf16[256,64,384]{2,1,0:T(8,128)(2,1)} async-done(((bf16[8,64,384]{2,1,0:T(8,128)(2,1)}), bf16[256,64,384]{2,1,0:T(8,128)(2,1)}) %all-gather.3.cloned.1.call-update) | async-done | bytes 12582928 | tf_op jit(solution)/shard_map/all_gather | solution.py:177
  186.6 8.6 %shard_map.211 = (bf16[192,11008]{1,0:T(8,128)(2,1)}, bf16[512,4096]{1,0:T(8,128)(2,1)}) custom-call(bf16[32,8,64,384]{3,2,1,0:T(8,128)(2,1)} %bitcast.32), custom_call_target="tpu_custom_call" | custom-call | bytes 21004288 | tf_op jit(solution)/shard_map/pallas_call | solution.py:73
  195.2 1.1 slice.72
  196.4 0.7 reshape.78
  (47 shorter events, 0.2 us)
Async XLA Ops:
  12.3 1.2 copy-start
  16.8 40.1 %all-to-all-start = ((f32[32,144,128]{2,1,0:T(8,128)}), f32[32,144,128]{2,1,0:T(8,128)S(1)}, u32[]{:S(2)}, u32[]{:S(2)}) async-start(f32[32,144,128]{2,1,0:T(8,128)} %copy.30), calls=%async_computation | async-start | bytes 4718592 | tf_op jit(solution)/shard_map/all_to_all | solution.py:129
  25.4 31.7 %copy-start.4 = (f32[64,128]{1,0:T(8,128)S(1)}, f32[64,128]{1,0:T(8,128)}, u32[]{:S(2)}) copy-start(f32[64,128]{1,0:T(8,128)} %param.16) | copy-start | bytes 98308
  25.4 31.7 %copy-start.9 = (f32[64,128]{1,0:T(8,128)S(1)}, f32[64,128]{1,0:T(8,128)}, u32[]{:S(2)}) copy-start(f32[64,128]{1,0:T(8,128)} %param.19) | copy-start | bytes 98308
  25.4 31.7 %copy-start.10 = (f32[64,128]{1,0:T(8,128)S(1)}, f32[64,128]{1,0:T(8,128)}, u32[]{:S(2)}) copy-start(f32[64,128]{1,0:T(8,128)} %param.22) | copy-start | bytes 98308
  25.4 32.3 %copy-start.11 = (f32[16]{0:T(128)S(1)}, f32[16]{0:T(128)}, u32[]{:S(2)}) copy-start(f32[16]{0:T(128)} %param.17) | copy-start | bytes 196
  25.4 32.3 %copy-start.12 = (f32[16]{0:T(128)S(1)}, f32[16]{0:T(128)}, u32[]{:S(2)}) copy-start(f32[16]{0:T(128)} %param.20) | copy-start | bytes 196
  25.4 32.3 %copy-start.13 = (f32[16]{0:T(128)S(1)}, f32[16]{0:T(128)}, u32[]{:S(2)}) copy-start(f32[16]{0:T(128)} %param.23) | copy-start | bytes 196
  25.5 33.4 %copy-start.1 = (f32[24,344]{1,0:T(8,128)S(1)}, f32[24,344]{1,0:T(8,128)}, u32[]{:S(2)}) copy-start(f32[24,344]{1,0:T(8,128)} %param.15) | copy-start | bytes 99076
  25.5 33.4 %copy-start.7 = (f32[24,344]{1,0:T(8,128)S(1)}, f32[24,344]{1,0:T(8,128)}, u32[]{:S(2)}) copy-start(f32[24,344]{1,0:T(8,128)} %param.21) | copy-start | bytes 99076
  25.5 33.4 %copy-start.8 = (f32[24,344]{1,0:T(8,128)S(1)}, f32[24,344]{1,0:T(8,128)}, u32[]{:S(2)}) copy-start(f32[24,344]{1,0:T(8,128)} %param.18) | copy-start | bytes 99076
  25.5 161.1 %all-gather.3.cloned.1.call-start = ((), (), s32[]{:S(2)}) async-start(), calls=%async_computation.2 | async-start | bytes 12976128 | tf_op jit(solution)/shard_map/all_gather | solution.py:177
  57.7 137.5 %copy-start.5 = (f32[64,128]{1,0:T(8,128)}, f32[64,128]{1,0:T(8,128)S(1)}, u32[]{:S(2)}) copy-start(f32[64,128]{1,0:T(8,128)S(1)} %get-tuple-element.30) | copy-start | bytes 98308
  57.7 137.5 %copy-start.6 = (f32[64,128]{1,0:T(8,128)}, f32[64,128]{1,0:T(8,128)S(1)}, u32[]{:S(2)}) copy-start(f32[64,128]{1,0:T(8,128)S(1)} %get-tuple-element.31) | copy-start | bytes 98308
  59.5 135.7 %copy-start.2 = (f32[24,344]{1,0:T(8,128)}, f32[24,344]{1,0:T(8,128)S(1)}, u32[]{:S(2)}) copy-start(f32[24,344]{1,0:T(8,128)S(1)} %get-tuple-element.32) | copy-start | bytes 99076
  59.5 135.7 %copy-start.3 = (f32[24,344]{1,0:T(8,128)}, f32[24,344]{1,0:T(8,128)S(1)}, u32[]{:S(2)}) copy-start(f32[24,344]{1,0:T(8,128)S(1)} %get-tuple-element.33) | copy-start | bytes 99076
  63.5 2.7 %collective-permute-start = (f32[8]{0:T(128)S(1)}, f32[8]{0:T(128)S(1)}, u32[]{:S(2)}, u32[]{:S(2)}) collective-permute-start(f32[8]{0:T(128)S(1)} %stack.27), channel_id=1, source_target_pairs={{0,8},{8,0},{16,24},{24,16},{32,40},{40,32},{48,56},{56,48},{64,72... | collective-permute-start | bytes 104 | tf_op jit(solution)/shard_map/ppermute | solution.py:35
  66.3 3.9 %collective-permute-start.3 = (f32[8]{0:T(128)S(1)}, f32[8]{0:T(128)S(1)}, u32[]{:S(2)}, u32[]{:S(2)}) collective-permute-start(f32[8]{0:T(128)S(1)} %add.108), channel_id=1, source_target_pairs={{0,48},{8,56},{16,32},{24,40},{32,16},{40,24},{48,0},{56,8},{64,11... | collective-permute-start | bytes 104 | tf_op jit(solution)/shard_map/ppermute | solution.py:35
  66.3 3.9 %collective-permute-start.1 = (f32[8]{0:T(128)S(1)}, f32[8]{0:T(128)S(1)}, u32[]{:S(2)}, u32[]{:S(2)}) collective-permute-start(f32[8]{0:T(128)S(1)} %add.108), channel_id=1, source_target_pairs={{0,16},{8,24},{16,0},{24,8},{32,48},{40,56},{48,32},{56,40},{64,80... | collective-permute-start | bytes 104 | tf_op jit(solution)/shard_map/ppermute | solution.py:35
  66.3 4.8 %collective-permute-start.2 = (f32[8]{0:T(128)S(1)}, f32[8]{0:T(128)S(1)}, u32[]{:S(2)}, u32[]{:S(2)}) collective-permute-start(f32[8]{0:T(128)S(1)} %add.108), channel_id=1, source_target_pairs={{0,32},{8,40},{16,48},{24,56},{32,0},{40,8},{48,16},{56,24},{64,96... | collective-permute-start | bytes 104 | tf_op jit(solution)/shard_map/ppermute | solution.py:35
  71.1 3.9 %collective-permute-start.6 = (f32[8]{0:T(128)S(1)}, f32[8]{0:T(128)S(1)}, u32[]{:S(2)}, u32[]{:S(2)}) collective-permute-start(f32[8]{0:T(128)S(1)} %add_add_fusion.1), channel_id=1, source_target_pairs={{0,192},{8,200},{16,208},{24,216},{32,224},{40,232},{48,240},{56,2... | collective-permute-start | bytes 104 | tf_op jit(solution)/shard_map/ppermute | solution.py:35
  71.6 3.3 %collective-permute-start.4 = (f32[8]{0:T(128)S(1)}, f32[8]{0:T(128)S(1)}, u32[]{:S(2)}, u32[]{:S(2)}) collective-permute-start(f32[8]{0:T(128)S(1)} %add_add_fusion.1), channel_id=1, source_target_pairs={{0,64},{8,72},{16,80},{24,88},{32,96},{40,104},{48,112},{56,120},{... | collective-permute-start | bytes 104 | tf_op jit(solution)/shard_map/ppermute | solution.py:35
  71.6 4.3 %collective-permute-start.5 = (f32[8]{0:T(128)S(1)}, f32[8]{0:T(128)S(1)}, u32[]{:S(2)}, u32[]{:S(2)}) collective-permute-start(f32[8]{0:T(128)S(1)} %add_add_fusion.1), channel_id=1, source_target_pairs={{0,128},{8,136},{16,144},{24,152},{32,160},{40,168},{48,176},{56,1... | collective-permute-start | bytes 104 | tf_op jit(solution)/shard_map/ppermute | solution.py:35
  75.9 2.6 %collective-permute-start.7 = (f32[8]{0:T(128)S(1)}, f32[8]{0:T(128)S(1)}, u32[]{:S(2)}, u32[]{:S(2)}) collective-permute-start(f32[8]{0:T(128)S(1)} %add_add_fusion), channel_id=1, source_target_pairs={{0,1},{1,0},{2,3},{3,2},{4,5},{5,4},{6,7},{7,6},{8,9},{9,8},{10,11... | collective-permute-start | bytes 104 | tf_op jit(solution)/shard_map/ppermute | solution.py:35
  78.5 3.9 %collective-permute-start.8 = (f32[8]{0:T(128)S(1)}, f32[8]{0:T(128)S(1)}, u32[]{:S(2)}, u32[]{:S(2)}) collective-permute-start(f32[8]{0:T(128)S(1)} %add.115), channel_id=1, source_target_pairs={{0,2},{1,3},{2,0},{3,1},{4,6},{5,7},{6,4},{7,5},{8,10},{9,11},{10,... | collective-permute-start | bytes 104 | tf_op jit(solution)/shard_map/ppermute | solution.py:35
  82.5 7.1 %collective-permute-start.9 = (f32[8]{0:T(128)S(1)}, f32[8]{0:T(128)S(1)}, u32[]{:S(2)}, u32[]{:S(2)}) collective-permute-start(f32[8]{0:T(128)S(1)} %add.116), channel_id=1, source_target_pairs={{0,4},{1,5},{2,6},{3,7},{4,0},{5,1},{6,2},{7,3},{8,12},{9,13},{10,... | collective-permute-start | bytes 104 | tf_op jit(solution)/shard_map/ppermute | solution.py:35
Sparse Core Ops, SparseCore 0:
  113.8 72.8 all-gather.2

commit v6 on v5

--- a/solution.py
+++ b/solution.py
@@ -61,13 +61,16 @@
                 up_ref[up_rows * j : up_rows * (j + 1), up_cols * w : up_cols * (w + 1)] = in_ref[
                     w, j, :up_rows, :up_cols
                 ]
-                for t in range(down_rows // 16):
-                    row = 32 + 16 * (t // 3)
-                    lane = LANES * (t % 3)
+                for t in range(3):
                     down_ref[
                         down_rows * j + 16 * t : down_rows * j + 16 * (t + 1),
                         down_cols * w : down_cols * (w + 1),
-                    ] = in_ref[w, j, row : row + 16, lane : lane + LANES]
+                    ] = in_ref[w, j, up_rows : up_rows + 16, LANES * t : LANES * (t + 1)]
+                for t in range(2):
+                    down_ref[
+                        down_rows * j + 48 + 8 * t : down_rows * j + 56 + 8 * t,
+                        down_cols * w : down_cols * (w + 1),
+                    ] = in_ref[w, j, up_rows + 16 : up_rows + 24, LANES * t : LANES * (t + 1)]
 
     moved = whole.size * 2 + (up_rows * up_cols + down_rows * down_cols) * n_wide * n_narrow * 2
     return pl.pallas_call(
@@ -159,24 +162,22 @@
     gain_master_new = finish(gain_master, gain_update, sums[2], sums[5])
 
     up_low = jnp.pad(up_master_new.astype(jnp.bfloat16), ((0, 0), (0, up_pad - up_cols)))
-    down_low = down_master_new.astype(jnp.bfloat16).reshape(4, 16, LANES)
+    down_low = down_master_new.astype(jnp.bfloat16)
     gain_low = jnp.pad(gain_master_new.astype(jnp.bfloat16), (0, LANES - gain_cols))
-    gain_low = jnp.pad(gain_low.reshape(1, LANES), ((0, 15), (0, 0)))
-    down_area = jnp.concatenate(
+    gain_low = jnp.pad(gain_low.reshape(1, LANES), ((0, 7), (0, 0)))
+    low = jnp.concatenate(
         [
-            jnp.concatenate([down_low[0], down_low[1], down_low[2]], axis=1),
-            jnp.concatenate([down_low[3], gain_low, jnp.zeros((16, LANES), jnp.bfloat16)], axis=1),
+            up_low,
+            jnp.concatenate([down_low[0:16], down_low[16:32], down_low[32:48]], axis=1),
+            jnp.concatenate([down_low[48:56], down_low[56:64], gain_low], axis=1),
         ]
-    )
-    low = jnp.concatenate(
-        [up_low, jnp.zeros((32 - up_rows, up_pad), jnp.bfloat16), down_area]
     )
     rows = lax.all_to_all(
         jnp.broadcast_to(low[None], (n_narrow,) + low.shape), "narrow", 0, 0, tiled=True
     )
     whole = lax.all_gather(rows[None], "wide", axis=0, tiled=True)
     up_weights, down_weights = unpack(whole, up_master.shape, down_master.shape)
-    gain_weights = whole[:, :, 48, 128 : 128 + gain_cols].transpose(1, 0, 2).reshape(-1)
+    gain_weights = whole[:, :, up_rows + 16, 2 * LANES : 2 * LANES + gain_cols].transpose(1, 0, 2).reshape(-1)
     return (
         up_first_new,
         up_second_new,

time: 204 us -> 192 us (0.941)
  waiting for transfers between devices: 110 us -> 71 us
  blocking collectives: 17.3 us -> 56 us
  starting transfers between devices: 29 us -> 18.7 us
    all_to_all x0 -> x1, blocking collectives: none -> 39.7 us  [body(): received = lax.all_to_all(packed, 'wide', 0, 0, tiled=True)]
    all_to_all x1 -> x0, waiting for transfers between devices: 31.3 us -> none  [body(): received = lax.all_to_all(packed, 'wide', 0, 0, tiled=True)]
    all_to_all x1 -> x0, starting transfers between devices: 8.58 us -> none  [body(): received = lax.all_to_all(packed, 'wide', 0, 0, tiled=True)]
    all_gather x1, waiting for transfers between devices: 73 us -> 64.9 us  [body(): whole = lax.all_gather(rows[None], 'wide', axis=0, tiled=True)]
  transfers between devices with their start and end apart: 12 -> 11, of which waited for: 8 -> 7; matrix products, arithmetic and copies ran while one was open for 0% -> 0% of each run, Pallas kernels for 0% -> 0%
where the time goes in v6:
time: 192 us
  waiting for transfers between devices  71 us (37%)
  blocking collectives  56 us (29%)
  starting transfers between devices  18.7 us (10%)
  between operations  18.5 us (10%)
  local copies, waits for them, and re-layouts  13.7 us (7%)
  Pallas kernels  7.96 us (4%)
  other arithmetic  5.94 us (3%)
    all_gather x1, waiting for transfers between devices, body(): whole = lax.all_gather(rows[None], 'wide', axis=0, tiled=True)  64.9 us
    all_to_all x1, blocking collectives, body(): received = lax.all_to_all(packed, 'wide', 0, 0, tiled=True)  39.7 us
    ppermute x10, starting transfers between devices, group_sum(): lax.ppermute(x, axis, [(i, i ^ m) for i in range(size)])  18.6 us
    all_to_all x1, blocking collectives, body(): lax.all_to_all(jnp.broadcast_to(low[None], (n_narrow,) + low.shape), 'nar...  16.2 us
    pallas_call x1, Pallas kernels, unpack(): pl.pallas_call(kernel, grid=(n_narrow // per,), in_specs=[pl.BlockSpec((n...  7.96 us
    ppermute x10, waiting for transfers between devices, group_sum(): lax.ppermute(x, axis, [(i, i ^ m) for i in range(size)])  6.05 us
    another operation x1, local copies, waits for them, and re-layouts, body(): jnp.stack([jnp.sum(up_master * up_master), jnp.sum(down_master * down_mas...  3.99 us
  transfers between devices with their start and end apart: 11, of which 7 were waited for; matrix products, arithmetic and copies ran while one was open for 0% of the time, Pallas kernels for 0%

profile of v6, /device:TPU:1, one launch (start us, length us, event | category | flops | bytes accessed | tf_op | source)
XLA Modules:
  0.0 191.7 jit_solution(11340121978922144894)
XLA Ops:
  7.2 0.0 all-gather.3.cloned.1.call-start
  7.2 0.5 broadcast.82
  7.7 1.3 reduce.3
  9.1 0.1 reshape.66
  9.2 2.6 %reshape_squeeze.7 = f32[24,32,344]{2,1,0:T(8,128)S(1)} reshape(f32[1,24,11008]{2,1,0:T(8,128)} %param.12) | data formatting | bytes 2113536 | tf_op jit(solution)/shard_map/reshape;squeeze | solution.py:118
  11.7 0.1 pad.20
  11.8 0.5 reshape.64
  12.3 0.0 copy-start
  12.4 0.1 copy.29
  12.5 1.1 copy-done
  13.6 0.2 copy.34
  13.8 0.1 pad.35.clone
  13.8 0.2 fusion
  14.1 1.4 copy.30
  15.4 39.7 %all_to_all.10 = f32[32,144,128]{2,1,0:T(8,128)S(1)} all-to-all(f32[32,144,128]{2,1,0:T(8,128)S(1)} %copy.30), channel_id=1, replica_groups=mesh['wide'=32,'narrow'=8] {'wide'}, dimensions={0} | all-to-all | bytes 4718592 | tf_op jit(solution)/shard_map/all_to_all | solution.py:132
  55.2 0.1 reduce_sum.63
  55.4 0.5 copy-done.4
  55.9 0.0 copy-done.9
  55.9 0.0 copy-done.10
  56.0 0.6 multiply_reduce_fusion.2
  56.6 0.0 copy-start.6
  56.6 1.1 multiply_reduce_fusion.4
  57.8 0.6 multiply_reduce_fusion
  58.4 4.0 %stack.27 = f32[8]{0:T(128)S(1)} concatenate(f32[1]{0:T(128)} %bitcast.3, f32[1]{0:T(128)} %bitcast.4, f32[1]{0:T(128)} %bitcast.5, f32[1]{0:T(128)} %bitcast.6, f32[1]{0:T(128)} %bitcast.7, f32[1]{0:T(128)} %bitcast.9, f32[2]{0:T(128)S(1)} %broadcast.52), dimensions={0} | concatenate | bytes 64 | tf_op jit(solution)/shard_map/stack | solution.py:147
  62.4 0.2 collective-permute-start
  62.6 1.0 collective-permute-done
  63.6 1.1 collective-permute-start.3
  64.7 2.7 %collective-permute-start.2 = (f32[8]{0:T(128)S(1)}, f32[8]{0:T(128)S(1)}, u32[]{:S(2)}, u32[]{:S(2)}) collective-permute-start(f32[8]{0:T(128)S(1)} %add.108), channel_id=1, source_target_pairs={{0,32},{8,40},{16,48},{24,56},{32,0},{40,8},{48,16},{56,24},{64,96... | collective-permute-start | bytes 104 | tf_op jit(solution)/shard_map/ppermute | solution.py:35
  67.5 1.2 collective-permute-done.2
  68.7 0.9 collective-permute-start.6
  69.6 3.0 %collective-permute-start.5 = (f32[8]{0:T(128)S(1)}, f32[8]{0:T(128)S(1)}, u32[]{:S(2)}, u32[]{:S(2)}) collective-permute-start(f32[8]{0:T(128)S(1)} %add_add_fusion.1), channel_id=1, source_target_pairs={{0,128},{8,136},{16,144},{24,152},{32,160},{40,168},{48,176},{56,1... | collective-permute-start | bytes 104 | tf_op jit(solution)/shard_map/ppermute | solution.py:35
  72.5 1.0 collective-permute-done.5
  73.5 1.6 collective-permute-start.7
  75.1 1.0 collective-permute-done.7
  76.1 3.0 %collective-permute-start.8 = (f32[8]{0:T(128)S(1)}, f32[8]{0:T(128)S(1)}, u32[]{:S(2)}, u32[]{:S(2)}) collective-permute-start(f32[8]{0:T(128)S(1)} %add.115), channel_id=1, source_target_pairs={{0,2},{1,3},{2,0},{3,1},{4,6},{5,7},{6,4},{7,5},{8,10},{9,11},{10,... | collective-permute-start | bytes 104 | tf_op jit(solution)/shard_map/ppermute | solution.py:35
  79.1 1.0 collective-permute-done.8
  80.0 6.1 %collective-permute-start.9 = (f32[8]{0:T(128)S(1)}, f32[8]{0:T(128)S(1)}, u32[]{:S(2)}, u32[]{:S(2)}) collective-permute-start(f32[8]{0:T(128)S(1)} %add.116), channel_id=1, source_target_pairs={{0,4},{1,5},{2,6},{3,7},{4,0},{5,1},{6,2},{7,3},{8,12},{9,13},{10,... | collective-permute-start | bytes 104 | tf_op jit(solution)/shard_map/ppermute | solution.py:35
  86.1 1.0 collective-permute-done.9
  87.1 0.6 fusion.20
  89.1 0.6 fusion.12
  92.6 0.5 fusion.14
  93.1 0.6 fusion.13
  93.8 16.2 %all_to_all.11 = bf16[8,48,384]{2,1,0:T(8,128)(2,1)} all-to-all(bf16[8,48,384]{2,1,0:T(8,128)(2,1)S(1)} %broadcast_in_dim.13), channel_id=1, replica_groups=mesh['wide'=32,'narrow'=8] {'narrow'}, dimensions={0} | all-to-all | bytes 589824 | tf_op jit(solution)/shard_map/all_to_all | solution.py:175
  110.1 0.0 all-gather.3.cloned.1.call-update
  110.1 64.9 %all-gather.3.cloned.1.call-done = bf16[256,48,384]{2,1,0:T(8,128)(2,1)} async-done(((bf16[8,48,384]{2,1,0:T(8,128)(2,1)}), bf16[256,48,384]{2,1,0:T(8,128)(2,1)}) %all-gather.3.cloned.1.call-update) | async-done | bytes 9437200 | tf_op jit(solution)/shard_map/all_gather | solution.py:178
  175.0 8.0 %shard_map.211 = (bf16[192,11008]{1,0:T(8,128)(2,1)}, bf16[512,4096]{1,0:T(8,128)(2,1)}) custom-call(bf16[32,8,48,384]{3,2,1,0:T(8,128)(2,1)} %bitcast.32), custom_call_target="tpu_custom_call" | custom-call | bytes 17858560 | tf_op jit(solution)/shard_map/pallas_call | solution.py:76
  183.0 1.1 slice.73
  184.2 0.7 reshape.69
  (44 shorter events, 0.2 us)
Async XLA Ops:
  7.2 167.9 %all-gather.3.cloned.1.call-start = ((), (), s32[]{:S(2)}) async-start(), calls=%async_computation.2 | async-start | bytes 9732096 | tf_op jit(solution)/shard_map/all_gather | solution.py:178
  12.3 1.2 copy-start
  55.2 0.8 copy-start.4
  55.2 0.8 copy-start.9
  55.2 0.8 copy-start.10
  55.2 1.4 copy-start.11
  55.2 1.4 copy-start.12
  55.2 1.4 copy-start.13
  55.2 2.6 %copy-start.1 = (f32[24,344]{1,0:T(8,128)S(1)}, f32[24,344]{1,0:T(8,128)}, u32[]{:S(2)}) copy-start(f32[24,344]{1,0:T(8,128)} %param.15) | copy-start | bytes 99076
  55.2 2.5 %copy-start.7 = (f32[24,344]{1,0:T(8,128)S(1)}, f32[24,344]{1,0:T(8,128)}, u32[]{:S(2)}) copy-start(f32[24,344]{1,0:T(8,128)} %param.21) | copy-start | bytes 99076
  55.2 2.5 %copy-start.8 = (f32[24,344]{1,0:T(8,128)S(1)}, f32[24,344]{1,0:T(8,128)}, u32[]{:S(2)}) copy-start(f32[24,344]{1,0:T(8,128)} %param.18) | copy-start | bytes 99076
  56.6 126.4 %copy-start.5 = (f32[64,128]{1,0:T(8,128)}, f32[64,128]{1,0:T(8,128)S(1)}, u32[]{:S(2)}) copy-start(f32[64,128]{1,0:T(8,128)S(1)} %get-tuple-element.30) | copy-start | bytes 98308
  56.6 126.4 %copy-start.6 = (f32[64,128]{1,0:T(8,128)}, f32[64,128]{1,0:T(8,128)S(1)}, u32[]{:S(2)}) copy-start(f32[64,128]{1,0:T(8,128)S(1)} %get-tuple-element.31) | copy-start | bytes 98308
  58.4 124.6 %copy-start.2 = (f32[24,344]{1,0:T(8,128)}, f32[24,344]{1,0:T(8,128)S(1)}, u32[]{:S(2)}) copy-start(f32[24,344]{1,0:T(8,128)S(1)} %get-tuple-element.32) | copy-start | bytes 99076
  58.4 124.6 %copy-start.3 = (f32[24,344]{1,0:T(8,128)}, f32[24,344]{1,0:T(8,128)S(1)}, u32[]{:S(2)}) copy-start(f32[24,344]{1,0:T(8,128)S(1)} %get-tuple-element.33) | copy-start | bytes 99076
  62.4 1.2 collective-permute-start
  63.6 3.9 %collective-permute-start.3 = (f32[8]{0:T(128)S(1)}, f32[8]{0:T(128)S(1)}, u32[]{:S(2)}, u32[]{:S(2)}) collective-permute-start(f32[8]{0:T(128)S(1)} %add.108), channel_id=1, source_target_pairs={{0,48},{8,56},{16,32},{24,40},{32,16},{40,24},{48,0},{56,8},{64,11... | collective-permute-start | bytes 104 | tf_op jit(solution)/shard_map/ppermute | solution.py:35
  64.7 2.7 %collective-permute-start.1 = (f32[8]{0:T(128)S(1)}, f32[8]{0:T(128)S(1)}, u32[]{:S(2)}, u32[]{:S(2)}) collective-permute-start(f32[8]{0:T(128)S(1)} %add.108), channel_id=1, source_target_pairs={{0,16},{8,24},{16,0},{24,8},{32,48},{40,56},{48,32},{56,40},{64,80... | collective-permute-start | bytes 104 | tf_op jit(solution)/shard_map/ppermute | solution.py:35
  64.7 3.9 %collective-permute-start.2 = (f32[8]{0:T(128)S(1)}, f32[8]{0:T(128)S(1)}, u32[]{:S(2)}, u32[]{:S(2)}) collective-permute-start(f32[8]{0:T(128)S(1)} %add.108), channel_id=1, source_target_pairs={{0,32},{8,40},{16,48},{24,56},{32,0},{40,8},{48,16},{56,24},{64,96... | collective-permute-start | bytes 104 | tf_op jit(solution)/shard_map/ppermute | solution.py:35
  68.7 3.9 %collective-permute-start.6 = (f32[8]{0:T(128)S(1)}, f32[8]{0:T(128)S(1)}, u32[]{:S(2)}, u32[]{:S(2)}) collective-permute-start(f32[8]{0:T(128)S(1)} %add_add_fusion.1), channel_id=1, source_target_pairs={{0,192},{8,200},{16,208},{24,216},{32,224},{40,232},{48,240},{56,2... | collective-permute-start | bytes 104 | tf_op jit(solution)/shard_map/ppermute | solution.py:35
  69.5 3.0 %collective-permute-start.4 = (f32[8]{0:T(128)S(1)}, f32[8]{0:T(128)S(1)}, u32[]{:S(2)}, u32[]{:S(2)}) collective-permute-start(f32[8]{0:T(128)S(1)} %add_add_fusion.1), channel_id=1, source_target_pairs={{0,64},{8,72},{16,80},{24,88},{32,96},{40,104},{48,112},{56,120},{... | collective-permute-start | bytes 104 | tf_op jit(solution)/shard_map/ppermute | solution.py:35
  69.6 3.9 %collective-permute-start.5 = (f32[8]{0:T(128)S(1)}, f32[8]{0:T(128)S(1)}, u32[]{:S(2)}, u32[]{:S(2)}) collective-permute-start(f32[8]{0:T(128)S(1)} %add_add_fusion.1), channel_id=1, source_target_pairs={{0,128},{8,136},{16,144},{24,152},{32,160},{40,168},{48,176},{56,1... | collective-permute-start | bytes 104 | tf_op jit(solution)/shard_map/ppermute | solution.py:35
  73.5 2.6 %collective-permute-start.7 = (f32[8]{0:T(128)S(1)}, f32[8]{0:T(128)S(1)}, u32[]{:S(2)}, u32[]{:S(2)}) collective-permute-start(f32[8]{0:T(128)S(1)} %add_add_fusion), channel_id=1, source_target_pairs={{0,1},{1,0},{2,3},{3,2},{4,5},{5,4},{6,7},{7,6},{8,9},{9,8},{10,11... | collective-permute-start | bytes 104 | tf_op jit(solution)/shard_map/ppermute | solution.py:35
  76.1 3.9 %collective-permute-start.8 = (f32[8]{0:T(128)S(1)}, f32[8]{0:T(128)S(1)}, u32[]{:S(2)}, u32[]{:S(2)}) collective-permute-start(f32[8]{0:T(128)S(1)} %add.115), channel_id=1, source_target_pairs={{0,2},{1,3},{2,0},{3,1},{4,6},{5,7},{6,4},{7,5},{8,10},{9,11},{10,... | collective-permute-start | bytes 104 | tf_op jit(solution)/shard_map/ppermute | solution.py:35
  80.0 7.1 %collective-permute-start.9 = (f32[8]{0:T(128)S(1)}, f32[8]{0:T(128)S(1)}, u32[]{:S(2)}, u32[]{:S(2)}) collective-permute-start(f32[8]{0:T(128)S(1)} %add.116), channel_id=1, source_target_pairs={{0,4},{1,5},{2,6},{3,7},{4,0},{5,1},{6,2},{7,3},{8,12},{9,13},{10,... | collective-permute-start | bytes 104 | tf_op jit(solution)/shard_map/ppermute | solution.py:35
Sparse Core Ops, SparseCore 0:
  110.2 64.7 all-gather.2

commit v7 on v6

--- a/solution.py
+++ b/solution.py
@@ -42,10 +42,6 @@
     x = group_sum(x, "wide", (1,))
     x = group_sum(x, "wide", (2, 4, 6))
     x = group_sum(x, "wide", (8, 16, 24))
-    step = 1
-    while step < lax.axis_size("narrow"):
-        x = group_sum(x, "narrow", (step,))
-        step *= 2
     return x
 
 
@@ -156,24 +152,48 @@
             jnp.float32(0.0),
         ]
     )
-    sums = mesh_sum(partial)
+
+    def as_rows(x):
+        return jnp.pad(x, ((0, 0), (0, up_pad - up_cols))).reshape(up_rows * up_tiles, LANES)
+
+    tail = jnp.concatenate(
+        [gain_master, gain_update, partial, jnp.zeros((LANES - 2 * gain_cols - 8,), jnp.float32)]
+    ).reshape(1, LANES)
+    mine = jnp.concatenate(
+        [as_rows(up_master), as_rows(up_update), down_master, down_update, tail]
+    )
+    got = lax.all_to_all(
+        jnp.broadcast_to(mine[None], (n_narrow,) + mine.shape), "narrow", 0, 0, tiled=True
+    )
+    up_span = up_rows * up_tiles
+    up_master_all = got[:, :up_span].reshape(n_narrow, up_rows, up_pad)
+    up_update_all = got[:, up_span : 2 * up_span].reshape(n_narrow, up_rows, up_pad)
+    at = 2 * up_span
+    down_master_all = got[:, at : at + down_rows]
+    down_update_all = got[:, at + down_rows : at + 2 * down_rows]
+    tail_all = got[:, at + 2 * down_rows]
+    gain_master_all = tail_all[:, :gain_cols]
+    gain_update_all = tail_all[:, gain_cols : 2 * gain_cols]
+    narrow_sum = tail_all[0, 2 * gain_cols : 2 * gain_cols + 8]
+    for k in range(1, n_narrow):
+        narrow_sum = narrow_sum + tail_all[k, 2 * gain_cols : 2 * gain_cols + 8]
+    sums = mesh_sum(narrow_sum)
     up_master_new = finish(up_master, up_update, sums[0], sums[3])
     down_master_new = finish(down_master, down_update, sums[1], sums[4])
     gain_master_new = finish(gain_master, gain_update, sums[2], sums[5])
 
-    up_low = jnp.pad(up_master_new.astype(jnp.bfloat16), ((0, 0), (0, up_pad - up_cols)))
-    down_low = down_master_new.astype(jnp.bfloat16)
-    gain_low = jnp.pad(gain_master_new.astype(jnp.bfloat16), (0, LANES - gain_cols))
-    gain_low = jnp.pad(gain_low.reshape(1, LANES), ((0, 7), (0, 0)))
-    low = jnp.concatenate(
+    up_low = finish(up_master_all, up_update_all, sums[0], sums[3]).astype(jnp.bfloat16)
+    down_low = finish(down_master_all, down_update_all, sums[1], sums[4]).astype(jnp.bfloat16)
+    gain_low = finish(gain_master_all, gain_update_all, sums[2], sums[5]).astype(jnp.bfloat16)
+    gain_low = jnp.pad(gain_low, ((0, 0), (0, LANES - gain_cols)))
+    gain_low = jnp.pad(gain_low[:, None, :], ((0, 0), (0, 7), (0, 0)))
+    rows = jnp.concatenate(
         [
             up_low,
-            jnp.concatenate([down_low[0:16], down_low[16:32], down_low[32:48]], axis=1),
-            jnp.concatenate([down_low[48:56], down_low[56:64], gain_low], axis=1),
-        ]
-    )
-    rows = lax.all_to_all(
-        jnp.broadcast_to(low[None], (n_narrow,) + low.shape), "narrow", 0, 0, tiled=True
+            jnp.concatenate([down_low[:, 0:16], down_low[:, 16:32], down_low[:, 32:48]], axis=2),
+            jnp.concatenate([down_low[:, 48:56], down_low[:, 56:64], gain_low], axis=2),
+        ],
+        axis=1,
     )
     whole = lax.all_gather(rows[None], "wide", axis=0, tiled=True)
     up_weights, down_weights = unpack(whole, up_master.shape, down_master.shape)

time: 192 us -> 199 us (1.036)
  waiting for transfers between devices: 71 us -> 92.8 us
  blocking collectives: 56 us -> 36.1 us
  other arithmetic: 5.94 us -> 8.14 us
    all_to_all x0 -> x1, waiting for transfers between devices: none -> 31.3 us  [body(): received = lax.all_to_all(packed, 'wide', 0, 0, tiled=True)]
    all_to_all x2 -> x1, blocking collectives: 56 us -> 36.1 us  [body(): lax.all_to_all(jnp.broadcast_to(mine[None], (n_narrow,) + mine.shape), 'n...]
    all_to_all x0 -> x1, starting transfers between devices: none -> 8.71 us  [body(): received = lax.all_to_all(packed, 'wide', 0, 0, tiled=True)]
    all_gather x1, waiting for transfers between devices: 64.9 us -> 57.6 us  [body(): whole = lax.all_gather(rows[None], 'wide', axis=0, tiled=True)]
    ppermute x10 -> x7, starting transfers between devices: 18.6 us -> 11.5 us  [group_sum(): lax.ppermute(x, axis, [(i, i ^ m) for i in range(size)])]
    concatenate x0 -> x2, local copies, waits for them, and re-layouts: none -> 3.99 us  [the longest x1 3.96 us: body(): jnp.concatenate([gain_master, gain_update, partial, jnp.zeros((LANES - 2...]
    another operation x2 -> x1, local copies, waits for them, and re-layouts: 3.99 us -> 0.01 us  [the longest x1 3.99 us: body(): jnp.stack([jnp.sum(up_master * up_master), jnp.sum(down_master * down_mas...]
    ppermute x10 -> x7, waiting for transfers between devices: 6.05 us -> 3.9 us  [group_sum(): lax.ppermute(x, axis, [(i, i ^ m) for i in range(size)])]
  transfers between devices with their start and end apart: 11 -> 9, of which waited for: 7 -> 6; matrix products, arithmetic and copies ran while one was open for 0% -> 1% of each run, Pallas kernels for 0% -> 0%
where the time goes in v7:
time: 199 us
  waiting for transfers between devices  92.8 us (47%)
  blocking collectives  36.1 us (18%)
  starting transfers between devices  20.2 us (10%)
  between operations  18.6 us (9%)
  local copies, waits for them, and re-layouts  14.7 us (7%)
  other arithmetic  8.14 us (4%)
  Pallas kernels  7.96 us (4%)
    all_gather x1, waiting for transfers between devices, body(): whole = lax.all_gather(rows[None], 'wide', axis=0, tiled=True)  57.6 us
    all_to_all x1, blocking collectives, body(): lax.all_to_all(jnp.broadcast_to(mine[None], (n_narrow,) + mine.shape), 'n...  36.1 us
    all_to_all x1, waiting for transfers between devices, body(): received = lax.all_to_all(packed, 'wide', 0, 0, tiled=True)  31.3 us
    ppermute x7, starting transfers between devices, group_sum(): lax.ppermute(x, axis, [(i, i ^ m) for i in range(size)])  11.5 us
    all_to_all x1, starting transfers between devices, body(): received = lax.all_to_all(packed, 'wide', 0, 0, tiled=True)  8.71 us
    pallas_call x1, Pallas kernels, unpack(): pl.pallas_call(kernel, grid=(n_narrow // per,), in_specs=[pl.BlockSpec((n...  7.96 us
  transfers between devices with their start and end apart: 9, of which 6 were waited for; matrix products, arithmetic and copies ran while one was open for 1% of the time, Pallas kernels for 0%

profile of v7, /device:TPU:1, one launch (start us, length us, event | category | flops | bytes accessed | tf_op | source)
XLA Modules:
  0.0 198.5 jit_solution(14350982588762658650)
XLA Ops:
  7.2 0.5 broadcast.83
  7.7 1.3 reduce.3
  9.0 0.1 reshape.82
  9.1 2.6 %reshape_squeeze.7 = f32[24,32,344]{2,1,0:T(8,128)S(1)} reshape(f32[1,24,11008]{2,1,0:T(8,128)} %param.12) | data formatting | bytes 2113536 | tf_op jit(solution)/shard_map/reshape;squeeze | solution.py:114
  11.7 0.1 pad.23
  11.8 0.5 reshape.80
  12.3 0.1 copy.39
  12.5 1.1 copy-done
  13.5 0.2 copy.45
  13.7 0.1 pad.39.clone
  13.8 0.2 fusion
  14.0 2.8 %copy.40 = f32[32,144,128]{2,1,0:T(8,128)} copy(f32[32,144,128]{2,0,1:T(8,128)S(1)} %fusion) | data formatting | bytes 4718592 | tf_op jit(solution)/shard_map/concatenate | solution.py:119
  16.8 8.7 %all-to-all-start = ((f32[32,144,128]{2,1,0:T(8,128)}), f32[32,144,128]{2,1,0:T(8,128)S(1)}, u32[]{:S(2)}, u32[]{:S(2)}) async-start(f32[32,144,128]{2,1,0:T(8,128)} %copy.40), calls=%async_computation | async-start | bytes 4718592 | tf_op jit(solution)/shard_map/all_to_all | solution.py:128
  25.5 0.0 copy-start.3
  25.6 0.0 copy-start.5
  25.6 0.0 copy-start.6
  25.6 0.0 all-gather.3.cloned.1.call-start
  25.7 31.3 %all-to-all-done = f32[32,144,128]{2,1,0:T(8,128)S(1)} async-done(((f32[32,144,128]{2,1,0:T(8,128)}), f32[32,144,128]{2,1,0:T(8,128)S(1)}, u32[]{:S(2)}, u32[]{:S(2)}) %all-to-all-start) | async-done | bytes 2359328 | tf_op jit(solution)/shard_map/all_to_all | solution.py:128
  57.0 0.1 reduce_sum.63
  57.2 1.3 multiply_reduce_fusion
  58.5 1.2 multiply_reduce_fusion.2
  59.8 1.1 multiply_reduce_fusion.4
  60.9 4.0 %concatenate.19 = f32[128]{0:T(128)S(1)} concatenate(f32[16]{0:T(128)S(1)} %copy-done.7, f32[16]{0:T(128)S(1)} %get-tuple-element.17, f32[1]{0:T(128)} %bitcast.4, f32[1]{0:T(128)} %bitcast.5, f32[1]{0:T(128)} %bitcast.6, f32[1]{0:T(128)} %bitcast.7, f32[1]{0:T(128)} %bitcast.8, f32[1]{0:T(128)} %bitcast.9, f32[2]{0:T(128)S(1)} %broadcast.56, f32[88]{0:T(128)S(1)} %broadcast_in_dim.19), dimensions={0} | concatenate | bytes 1024 | tf_op jit(solution)/shard_map/concatenate | solution.py:159
  64.9 0.1 broadcast_in_dim.20
  65.0 36.1 %all_to_all.10 = f32[8,273,128]{2,1,0:T(8,128)S(1)} all-to-all(f32[8,273,128]{2,1,0:T(8,128)S(1)} %broadcast_in_dim.20), channel_id=1, replica_groups=mesh['wide'=32,'narrow'=8] {'narrow'}, dimensions={0} | all-to-all | bytes 2236416 | tf_op jit(solution)/shard_map/all_to_all | solution.py:165
  101.1 0.1 add_bitcast_fusion
  101.1 3.7 %collective-permute-start = (f32[8]{0:T(128)S(1)}, f32[8]{0:T(128)S(1)}, u32[]{:S(2)}, u32[]{:S(2)}) collective-permute-start(f32[8]{0:T(128)S(1)} %add_bitcast_fusion), channel_id=1, source_target_pairs={{0,8},{8,0},{16,24},{24,16},{32,40},{40,32},{48,56},{56,48},{64,72... | collective-permute-start | bytes 104 | tf_op jit(solution)/shard_map/ppermute | solution.py:35
  104.9 0.8 collective-permute-done
  105.7 0.1 fusion.20
  105.8 0.5 collective-permute-start.3
  106.3 3.4 %collective-permute-start.2 = (f32[8]{0:T(128)S(1)}, f32[8]{0:T(128)S(1)}, u32[]{:S(2)}, u32[]{:S(2)}) collective-permute-start(f32[8]{0:T(128)S(1)} %fusion.20), channel_id=1, source_target_pairs={{0,32},{8,40},{16,48},{24,56},{32,0},{40,8},{48,16},{56,24},{64,96... | collective-permute-start | bytes 104 | tf_op jit(solution)/shard_map/ppermute | solution.py:35
  109.7 1.0 collective-permute-done.2
  110.6 2.1 %collective-permute-start.6 = (f32[8]{0:T(128)S(1)}, f32[8]{0:T(128)S(1)}, u32[]{:S(2)}, u32[]{:S(2)}) collective-permute-start(f32[8]{0:T(128)S(1)} %add_add_fusion.1), channel_id=1, source_target_pairs={{0,192},{8,200},{16,208},{24,216},{32,224},{40,232},{48,240},{56,2... | collective-permute-start | bytes 104 | tf_op jit(solution)/shard_map/ppermute | solution.py:35
  112.7 1.8 collective-permute-start.5
  114.5 0.6 collective-permute-done.4
  115.1 1.5 collective-permute-done.5
  116.6 0.6 fusion.19
  121.6 0.1 subtract_convert_fusion
  121.7 0.1 convert_element_type.24
  121.8 0.8 fusion.6
  122.5 0.0 all-gather.3.cloned.1.call-update
  122.5 0.5 multiply_subtract_fusion.2
  123.1 0.6 multiply_subtract_fusion.1
  123.7 0.6 multiply_subtract_fusion
  124.3 57.6 %all-gather.3.cloned.1.call-done = bf16[256,48,384]{2,1,0:T(8,128)(2,1)} async-done(((bf16[8,48,384]{2,1,0:T(8,128)(2,1)}), bf16[256,48,384]{2,1,0:T(8,128)(2,1)}) %all-gather.3.cloned.1.call-update) | async-done | bytes 9437200 | tf_op jit(solution)/shard_map/all_gather | solution.py:198
  181.9 8.0 %shard_map.211 = (bf16[192,11008]{1,0:T(8,128)(2,1)}, bf16[512,4096]{1,0:T(8,128)(2,1)}) custom-call(bf16[32,8,48,384]{3,2,1,0:T(8,128)(2,1)} %bitcast.38), custom_call_target="tpu_custom_call" | custom-call | bytes 17858560 | tf_op jit(solution)/shard_map/pallas_call | solution.py:72
  189.8 1.1 slice.144
  191.0 0.7 reshape.87
  (44 shorter events, 0.3 us)
Async XLA Ops:
  12.3 1.2 copy-start
  16.8 8.9 %copy-start.1 = (f32[24,344]{1,0:T(8,128)S(1)}, f32[24,344]{1,0:T(8,128)}, u32[]{:S(2)}) copy-start(f32[24,344]{1,0:T(8,128)} %param.15) | copy-start | bytes 99076
  16.8 40.2 %all-to-all-start = ((f32[32,144,128]{2,1,0:T(8,128)}), f32[32,144,128]{2,1,0:T(8,128)S(1)}, u32[]{:S(2)}, u32[]{:S(2)}) async-start(f32[32,144,128]{2,1,0:T(8,128)} %copy.40), calls=%async_computation | async-start | bytes 4718592 | tf_op jit(solution)/shard_map/all_to_all | solution.py:128
  25.5 31.7 %copy-start.3 = (f32[24,344]{1,0:T(8,128)S(1)}, f32[24,344]{1,0:T(8,128)}, u32[]{:S(2)}) copy-start(f32[24,344]{1,0:T(8,128)} %param.21) | copy-start | bytes 99076
  25.5 31.7 %copy-start.4 = (f32[24,344]{1,0:T(8,128)S(1)}, f32[24,344]{1,0:T(8,128)}, u32[]{:S(2)}) copy-start(f32[24,344]{1,0:T(8,128)} %param.18) | copy-start | bytes 99076
  25.5 32.9 %copy-start.2 = (f32[64,128]{1,0:T(8,128)S(1)}, f32[64,128]{1,0:T(8,128)}, u32[]{:S(2)}) copy-start(f32[64,128]{1,0:T(8,128)} %param.16) | copy-start | bytes 98308
  25.6 32.9 %copy-start.5 = (f32[64,128]{1,0:T(8,128)S(1)}, f32[64,128]{1,0:T(8,128)}, u32[]{:S(2)}) copy-start(f32[64,128]{1,0:T(8,128)} %param.19) | copy-start | bytes 98308
  25.6 32.9 %copy-start.6 = (f32[64,128]{1,0:T(8,128)S(1)}, f32[64,128]{1,0:T(8,128)}, u32[]{:S(2)}) copy-start(f32[64,128]{1,0:T(8,128)} %param.22) | copy-start | bytes 98308
  25.6 34.2 %copy-start.7 = (f32[16]{0:T(128)S(1)}, f32[16]{0:T(128)}, u32[]{:S(2)}) copy-start(f32[16]{0:T(128)} %param.17) | copy-start | bytes 196
  25.6 34.2 %copy-start.8 = (f32[16]{0:T(128)S(1)}, f32[16]{0:T(128)}, u32[]{:S(2)}) copy-start(f32[16]{0:T(128)} %param.20) | copy-start | bytes 196
  25.6 34.2 %copy-start.9 = (f32[16]{0:T(128)S(1)}, f32[16]{0:T(128)}, u32[]{:S(2)}) copy-start(f32[16]{0:T(128)} %param.23) | copy-start | bytes 196
  25.6 156.3 %all-gather.3.cloned.1.call-start = ((), (), s32[]{:S(2)}) async-start(), calls=%async_computation.2 | async-start | bytes 9732096 | tf_op jit(solution)/shard_map/all_gather | solution.py:198
  101.1 4.6 %collective-permute-start = (f32[8]{0:T(128)S(1)}, f32[8]{0:T(128)S(1)}, u32[]{:S(2)}, u32[]{:S(2)}) collective-permute-start(f32[8]{0:T(128)S(1)} %add_bitcast_fusion), channel_id=1, source_target_pairs={{0,8},{8,0},{16,24},{24,16},{32,40},{40,32},{48,56},{56,48},{64,72... | collective-permute-start | bytes 104 | tf_op jit(solution)/shard_map/ppermute | solution.py:35
  105.8 3.9 %collective-permute-start.3 = (f32[8]{0:T(128)S(1)}, f32[8]{0:T(128)S(1)}, u32[]{:S(2)}, u32[]{:S(2)}) collective-permute-start(f32[8]{0:T(128)S(1)} %fusion.20), channel_id=1, source_target_pairs={{0,48},{8,56},{16,32},{24,40},{32,16},{40,24},{48,0},{56,8},{64,11... | collective-permute-start | bytes 104 | tf_op jit(solution)/shard_map/ppermute | solution.py:35
  106.3 3.4 %collective-permute-start.1 = (f32[8]{0:T(128)S(1)}, f32[8]{0:T(128)S(1)}, u32[]{:S(2)}, u32[]{:S(2)}) collective-permute-start(f32[8]{0:T(128)S(1)} %fusion.20), channel_id=1, source_target_pairs={{0,16},{8,24},{16,0},{24,8},{32,48},{40,56},{48,32},{56,40},{64,80... | collective-permute-start | bytes 104 | tf_op jit(solution)/shard_map/ppermute | solution.py:35
  106.3 4.4 %collective-permute-start.2 = (f32[8]{0:T(128)S(1)}, f32[8]{0:T(128)S(1)}, u32[]{:S(2)}, u32[]{:S(2)}) collective-permute-start(f32[8]{0:T(128)S(1)} %fusion.20), channel_id=1, source_target_pairs={{0,32},{8,40},{16,48},{24,56},{32,0},{40,8},{48,16},{56,24},{64,96... | collective-permute-start | bytes 104 | tf_op jit(solution)/shard_map/ppermute | solution.py:35
  110.6 3.9 %collective-permute-start.6 = (f32[8]{0:T(128)S(1)}, f32[8]{0:T(128)S(1)}, u32[]{:S(2)}, u32[]{:S(2)}) collective-permute-start(f32[8]{0:T(128)S(1)} %add_add_fusion.1), channel_id=1, source_target_pairs={{0,192},{8,200},{16,208},{24,216},{32,224},{40,232},{48,240},{56,2... | collective-permute-start | bytes 104 | tf_op jit(solution)/shard_map/ppermute | solution.py:35
  112.7 2.4 %collective-permute-start.4 = (f32[8]{0:T(128)S(1)}, f32[8]{0:T(128)S(1)}, u32[]{:S(2)}, u32[]{:S(2)}) collective-permute-start(f32[8]{0:T(128)S(1)} %add_add_fusion.1), channel_id=1, source_target_pairs={{0,64},{8,72},{16,80},{24,88},{32,96},{40,104},{48,112},{56,120},{... | collective-permute-start | bytes 104 | tf_op jit(solution)/shard_map/ppermute | solution.py:35
  112.7 3.9 %collective-permute-start.5 = (f32[8]{0:T(128)S(1)}, f32[8]{0:T(128)S(1)}, u32[]{:S(2)}, u32[]{:S(2)}) collective-permute-start(f32[8]{0:T(128)S(1)} %add_add_fusion.1), channel_id=1, source_target_pairs={{0,128},{8,136},{16,144},{24,152},{32,160},{40,168},{48,176},{56,1... | collective-permute-start | bytes 104 | tf_op jit(solution)/shard_map/ppermute | solution.py:35
Sparse Core Ops, SparseCore 0:
  122.7 59.1 all-gather.2

commit v8 on v6

--- a/solution.py
+++ b/solution.py
@@ -42,11 +42,43 @@
     x = group_sum(x, "wide", (1,))
     x = group_sum(x, "wide", (2, 4, 6))
     x = group_sum(x, "wide", (8, 16, 24))
-    step = 1
-    while step < lax.axis_size("narrow"):
-        x = group_sum(x, "narrow", (step,))
-        step *= 2
-    return x
+    n_narrow = lax.axis_size("narrow")
+    got = lax.all_to_all(jnp.broadcast_to(x[None], (n_narrow,) + x.shape), "narrow", 0, 0, tiled=True)
+    total = got[0]
+    for k in range(1, n_narrow):
+        total = total + got[k]
+    return total
+
+
+def pack(up_g, down_g, gain_g, n_wide, height):
+    up_rows, up_cols = up_g.shape[0], up_g.shape[1] // n_wide
+    down_rows, down_cols = down_g.shape[0], down_g.shape[1] // n_wide
+    gain_cols = gain_g.shape[1] // n_wide
+    up_tiles = -(-up_cols // LANES)
+    up_at = down_rows
+    gain_at = up_at + up_rows * up_tiles
+    last = up_at + up_rows * (up_tiles - 1)
+
+    def kernel(up_ref, down_ref, gain_ref, out_ref):
+        for w in range(n_wide):
+            out_ref[w, last:height, :] = jnp.zeros((height - last, LANES), jnp.float32)
+            out_ref[w, :down_rows, :] = down_ref[:, down_cols * w : down_cols * (w + 1)]
+            for k in range(up_tiles):
+                width = min(LANES, up_cols - LANES * k)
+                start = up_cols * w + LANES * k
+                out_ref[w, up_at + up_rows * k : up_at + up_rows * (k + 1), :width] = up_ref[
+                    :, start : start + width
+                ]
+            out_ref[w, gain_at : gain_at + 1, :gain_cols] = gain_ref[:, gain_cols * w : gain_cols * (w + 1)]
+
+    moved = (up_g.size + down_g.size + gain_g.size + n_wide * height * LANES) * 4
+    return pl.pallas_call(
+        kernel,
+        in_specs=[pl.BlockSpec(memory_space=pltpu.VMEM)] * 3,
+        out_specs=pl.BlockSpec(memory_space=pltpu.VMEM),
+        out_shape=jax.ShapeDtypeStruct((n_wide, height, LANES), jnp.float32),
+        cost_estimate=pl.CostEstimate(flops=0, transcendentals=0, bytes_accessed=moved),
+    )(up_g, down_g, gain_g)
 
 
 def unpack(whole, up_shape, down_shape):
@@ -114,25 +146,12 @@
     gain_at = up_at + up_rows * up_tiles
     height = -(-(gain_at + 1) // 16) * 16
 
-    down_part = down_grads[0].reshape(down_rows, n_wide, down_cols).transpose(1, 0, 2)
-    up_part = up_grads[0].reshape(up_rows, n_wide, up_cols)
-    up_part = jnp.pad(up_part, ((0, 0), (0, 0), (0, up_pad - up_cols)))
-    up_part = up_part.reshape(up_rows, n_wide, up_tiles, LANES).transpose(1, 0, 2, 3)
-    up_part = up_part.reshape(n_wide, up_rows * up_tiles, LANES)
-    gain_part = jnp.pad(gain_grads.reshape(n_wide, 1, gain_cols), ((0, 0), (0, 0), (0, LANES - gain_cols)))
-    packed = jnp.concatenate(
-        [
-            down_part,
-            up_part,
-            gain_part,
-            jnp.zeros((n_wide, height - gain_at - 1, LANES), jnp.float32),
-        ],
-        axis=1,
-    )
+    packed = pack(up_grads[0], down_grads[0], gain_grads, n_wide, height)
     received = lax.all_to_all(packed, "wide", 0, 0, tiled=True)
     summed = jnp.sum(received, axis=0)
     down_sum = summed[:down_rows]
-    up_sum = summed[up_at:gain_at].reshape(up_rows, up_pad)[:, :up_cols]
+    up_sum = summed[up_at:gain_at].reshape(up_tiles, up_rows, LANES).transpose(1, 0, 2)
+    up_sum = up_sum.reshape(up_rows, up_pad)[:, :up_cols]
     gain_sum = summed[gain_at, :gain_cols]
 
     up_first_new, up_second_new, up_update = moments(

time: 192 us -> 183 us (0.953)
  blocking collectives: 56 us -> 67.4 us
  starting transfers between devices: 18.7 us -> 7.92 us
  local copies, waits for them, and re-layouts: 13.7 us -> 6.57 us
  waiting for transfers between devices: 71 us -> 65.9 us
  Pallas kernels: 7.96 us -> 11.5 us
    all_to_all x0 -> x1, blocking collectives: none -> 14.5 us  [mesh_sum(): lax.all_to_all(jnp.broadcast_to(x[None], (n_narrow,) + x.shape), 'narrow'...]
    ppermute x10 -> x7, starting transfers between devices: 18.6 us -> 7.89 us  [group_sum(): lax.ppermute(x, axis, [(i, i ^ m) for i in range(size)])]
    pallas_call x0 -> x1, Pallas kernels: none -> 3.59 us  [pack(): pl.pallas_call(kernel, in_specs=[pl.BlockSpec(memory_space=pltpu.VMEM)] *...]
    all_to_all x1, blocking collectives: 16.2 us -> 12.8 us  [body(): lax.all_to_all(jnp.broadcast_to(low[None], (n_narrow,) + low.shape), 'nar...]
    ppermute x10 -> x7, waiting for transfers between devices: 6.05 us -> 3.18 us  [group_sum(): lax.ppermute(x, axis, [(i, i ^ m) for i in range(size)])]
    another operation x2 -> x1, local copies, waits for them, and re-layouts: 2.56 us -> 0.01 us  [the longest x1 2.56 us: body(): up_part = up_grads[0].reshape(up_rows, n_wide, up_cols)]
    unnamed x30 -> x27, local copies, waits for them, and re-layouts: 2.39 us -> 0.07 us
    all_gather x1, waiting for transfers between devices: 64.9 us -> 62.7 us  [body(): whole = lax.all_gather(rows[None], 'wide', axis=0, tiled=True)]
  transfers between devices with their start and end apart: 11 -> 8, of which waited for: 7 -> 4; matrix products, arithmetic and copies ran while one was open for 0% -> 0% of each run, Pallas kernels for 0% -> 0%
where the time goes in v8:
time: 183 us; the launch traced here: 182 us
  blocking collectives  67.4 us (37%)
  waiting for transfers between devices  65.9 us (36%)
  between operations  18.5 us (10%)
  Pallas kernels  11.5 us (6%)
  starting transfers between devices  7.92 us (4%)
  local copies, waits for them, and re-layouts  6.57 us (4%)
  other arithmetic  4.37 us (2%)
    all_gather x1, waiting for transfers between devices, body(): whole = lax.all_gather(rows[None], 'wide', axis=0, tiled=True)  62.7 us
    all_to_all x1, blocking collectives, body(): received = lax.all_to_all(packed, 'wide', 0, 0, tiled=True)  40.1 us
    all_to_all x1, blocking collectives, mesh_sum(): lax.all_to_all(jnp.broadcast_to(x[None], (n_narrow,) + x.shape), 'narrow'...  14.5 us
    all_to_all x1, blocking collectives, body(): lax.all_to_all(jnp.broadcast_to(low[None], (n_narrow,) + low.shape), 'nar...  12.8 us
    pallas_call x1, Pallas kernels, unpack(): pl.pallas_call(kernel, grid=(n_narrow // per,), in_specs=[pl.BlockSpec((n...  7.96 us
    ppermute x7, starting transfers between devices, group_sum(): lax.ppermute(x, axis, [(i, i ^ m) for i in range(size)])  7.89 us
    another operation x1, local copies, waits for them, and re-layouts, body(): jnp.stack([jnp.sum(up_master * up_master), jnp.sum(down_master * down_mas...  3.99 us
  transfers between devices with their start and end apart: 8, of which 4 were waited for; matrix products, arithmetic and copies ran while one was open for 0% of the time, Pallas kernels for 0%

profile of v8, /device:TPU:1, one launch (start us, length us, event | category | flops | bytes accessed | tf_op | source)
XLA Modules:
  0.0 182.1 jit_solution(9535254714645996728)
XLA Ops:
  7.2 0.0 all-gather.3.cloned.1.call-start
  7.2 3.6 %shard_map.211 = f32[32,144,128]{2,1,0:T(8,128)} custom-call(f32[24,11008]{1,0:T(8,128)} %bitcast.35, f32[64,4096]{1,0:T(8,128)} %bitcast.36, f32[1,512]{1,0:T(1,128)} %gain_ref.1), custom_call_target="tpu_custom_call" | custom-call | bytes 4466688 | tf_op jit(solution)/shard_map/pallas_call | solution.py:75
  10.8 0.0 copy-start.11
  10.8 0.0 copy-start.12
  10.8 0.0 copy-start
  10.9 0.0 copy-start.6
  10.9 0.0 copy-start.7
  10.9 40.1 %all_to_all.16 = f32[32,144,128]{2,1,0:T(8,128)S(1)} all-to-all(f32[32,144,128]{2,1,0:T(8,128)} %shard_map.211), channel_id=1, replica_groups=mesh['wide'=32,'narrow'=8] {'wide'}, dimensions={0} | all-to-all | bytes 4718592 | tf_op jit(solution)/shard_map/all_to_all | solution.py:150
  50.9 0.1 reduce_sum.63
  51.1 0.0 copy-done.3
  51.1 0.0 copy-done.8
  51.1 0.0 copy-done.9
  51.1 0.6 multiply_reduce_fusion.2
  51.8 0.0 copy-done.10
  51.8 0.0 copy-done.11
  51.8 0.0 copy-done.12
  51.8 0.0 copy-start.5
  51.8 1.1 multiply_reduce_fusion.4
  52.9 0.0 copy-done
  52.9 0.0 copy-done.6
  53.0 0.0 copy-done.7
  53.0 0.6 multiply_reduce_fusion
  53.6 4.0 %stack.27 = f32[8]{0:T(128)S(1)} concatenate(f32[1]{0:T(128)} %bitcast.4, f32[1]{0:T(128)} %bitcast.5, f32[1]{0:T(128)} %bitcast.6, f32[1]{0:T(128)} %bitcast.7, f32[1]{0:T(128)} %bitcast.8, f32[1]{0:T(128)} %bitcast.10, f32[2]{0:T(128)S(1)} %broadcast.51), dimensions={0} | concatenate | bytes 64 | tf_op jit(solution)/shard_map/stack | solution.py:166
  57.6 0.2 collective-permute-start
  57.8 1.0 collective-permute-done
  58.8 1.1 collective-permute-start.3
  59.9 0.0 collective-permute-start.1
  59.9 2.7 %collective-permute-start.2 = (f32[8]{0:T(128)S(1)}, f32[8]{0:T(128)S(1)}, u32[]{:S(2)}, u32[]{:S(2)}) collective-permute-start(f32[8]{0:T(128)S(1)} %add.122), channel_id=1, source_target_pairs={{0,32},{8,40},{16,48},{24,56},{32,0},{40,8},{48,16},{56,24},{64,96... | collective-permute-start | bytes 104 | tf_op jit(solution)/shard_map/ppermute | solution.py:35
  62.6 0.0 collective-permute-done.3
  62.6 0.0 collective-permute-done.1
  62.6 1.2 collective-permute-done.2
  63.9 0.9 collective-permute-start.6
  64.7 0.0 collective-permute-start.4
  64.7 3.0 %collective-permute-start.5 = (f32[8]{0:T(128)S(1)}, f32[8]{0:T(128)S(1)}, u32[]{:S(2)}, u32[]{:S(2)}) collective-permute-start(f32[8]{0:T(128)S(1)} %add_add_fusion.1), channel_id=1, source_target_pairs={{0,128},{8,136},{16,144},{24,152},{32,160},{40,168},{48,176},{56,1... | collective-permute-start | bytes 104 | tf_op jit(solution)/shard_map/ppermute | solution.py:35
  67.7 0.0 collective-permute-done.6
  67.7 0.0 collective-permute-done.4
  67.7 1.0 collective-permute-done.5
  68.7 14.5 %all_to_all.17 = f32[8,1,8]{2,1,0:T(1,128)S(1)} all-to-all(f32[8,1,8]{2,1,0:T(1,128)S(1)} %broadcast_in_dim.6), channel_id=1, replica_groups=mesh['wide'=32,'narrow'=8] {'narrow'}, dimensions={0} | all-to-all | bytes 512 | tf_op jit(solution)/shard_map/all_to_all | solution.py:46
  83.2 0.6 fusion.18
  85.3 0.6 fusion.10
  88.8 0.5 fusion.12
  89.3 0.6 fusion.11
  90.0 12.8 %all_to_all.18 = bf16[8,48,384]{2,1,0:T(8,128)(2,1)} all-to-all(bf16[8,48,384]{2,1,0:T(8,128)(2,1)S(1)} %broadcast_in_dim.7), channel_id=1, replica_groups=mesh['wide'=32,'narrow'=8] {'narrow'}, dimensions={0} | all-to-all | bytes 589824 | tf_op jit(solution)/shard_map/all_to_all | solution.py:194
  102.7 0.0 all-gather.3.cloned.1.call-update
  102.7 62.7 %all-gather.3.cloned.1.call-done = bf16[256,48,384]{2,1,0:T(8,128)(2,1)} async-done(((bf16[8,48,384]{2,1,0:T(8,128)(2,1)}), bf16[256,48,384]{2,1,0:T(8,128)(2,1)}) %all-gather.3.cloned.1.call-update) | async-done | bytes 9437200 | tf_op jit(solution)/shard_map/all_gather | solution.py:197
  165.4 8.0 %shard_map.212 = (bf16[192,11008]{1,0:T(8,128)(2,1)}, bf16[512,4096]{1,0:T(8,128)(2,1)}) custom-call(bf16[32,8,48,384]{3,2,1,0:T(8,128)(2,1)} %bitcast.33), custom_call_target="tpu_custom_call" | custom-call | bytes 17858560 | tf_op jit(solution)/shard_map/pallas_call | solution.py:108
  173.4 1.1 slice.127
  174.5 0.7 reshape.87
  (26 shorter events, 0.1 us)
Async XLA Ops:
  7.2 158.2 %all-gather.3.cloned.1.call-start = ((), (), s32[]{:S(2)}) async-start(), calls=%async_computation.3 | async-start | bytes 9732096 | tf_op jit(solution)/shard_map/all_gather | solution.py:197
  10.8 40.3 %copy-start.3 = (f32[64,128]{1,0:T(8,128)S(1)}, f32[64,128]{1,0:T(8,128)}, u32[]{:S(2)}) copy-start(f32[64,128]{1,0:T(8,128)} %param.16) | copy-start | bytes 98308
  10.8 40.3 %copy-start.8 = (f32[64,128]{1,0:T(8,128)S(1)}, f32[64,128]{1,0:T(8,128)}, u32[]{:S(2)}) copy-start(f32[64,128]{1,0:T(8,128)} %param.19) | copy-start | bytes 98308
  10.8 40.3 %copy-start.9 = (f32[64,128]{1,0:T(8,128)S(1)}, f32[64,128]{1,0:T(8,128)}, u32[]{:S(2)}) copy-start(f32[64,128]{1,0:T(8,128)} %param.22) | copy-start | bytes 98308
  10.8 41.0 %copy-start.10 = (f32[16]{0:T(128)S(1)}, f32[16]{0:T(128)}, u32[]{:S(2)}) copy-start(f32[16]{0:T(128)} %param.17) | copy-start | bytes 196
  10.8 41.0 %copy-start.11 = (f32[16]{0:T(128)S(1)}, f32[16]{0:T(128)}, u32[]{:S(2)}) copy-start(f32[16]{0:T(128)} %param.20) | copy-start | bytes 196
  10.8 41.0 %copy-start.12 = (f32[16]{0:T(128)S(1)}, f32[16]{0:T(128)}, u32[]{:S(2)}) copy-start(f32[16]{0:T(128)} %param.23) | copy-start | bytes 196
  10.8 42.1 %copy-start = (f32[24,344]{1,0:T(8,128)S(1)}, f32[24,344]{1,0:T(8,128)}, u32[]{:S(2)}) copy-start(f32[24,344]{1,0:T(8,128)} %param.15) | copy-start | bytes 99076
  10.9 42.1 %copy-start.6 = (f32[24,344]{1,0:T(8,128)S(1)}, f32[24,344]{1,0:T(8,128)}, u32[]{:S(2)}) copy-start(f32[24,344]{1,0:T(8,128)} %param.21) | copy-start | bytes 99076
  10.9 42.1 %copy-start.7 = (f32[24,344]{1,0:T(8,128)S(1)}, f32[24,344]{1,0:T(8,128)}, u32[]{:S(2)}) copy-start(f32[24,344]{1,0:T(8,128)} %param.18) | copy-start | bytes 99076
  51.8 121.6 %copy-start.4 = (f32[64,128]{1,0:T(8,128)}, f32[64,128]{1,0:T(8,128)S(1)}, u32[]{:S(2)}) copy-start(f32[64,128]{1,0:T(8,128)S(1)} %get-tuple-element.30) | copy-start | bytes 98308
  51.8 121.6 %copy-start.5 = (f32[64,128]{1,0:T(8,128)}, f32[64,128]{1,0:T(8,128)S(1)}, u32[]{:S(2)}) copy-start(f32[64,128]{1,0:T(8,128)S(1)} %get-tuple-element.31) | copy-start | bytes 98308
  53.6 119.8 %copy-start.1 = (f32[24,344]{1,0:T(8,128)}, f32[24,344]{1,0:T(8,128)S(1)}, u32[]{:S(2)}) copy-start(f32[24,344]{1,0:T(8,128)S(1)} %get-tuple-element.32) | copy-start | bytes 99076
  53.6 119.8 %copy-start.2 = (f32[24,344]{1,0:T(8,128)}, f32[24,344]{1,0:T(8,128)S(1)}, u32[]{:S(2)}) copy-start(f32[24,344]{1,0:T(8,128)S(1)} %get-tuple-element.33) | copy-start | bytes 99076
  57.6 1.2 collective-permute-start
  58.8 3.9 %collective-permute-start.3 = (f32[8]{0:T(128)S(1)}, f32[8]{0:T(128)S(1)}, u32[]{:S(2)}, u32[]{:S(2)}) collective-permute-start(f32[8]{0:T(128)S(1)} %add.122), channel_id=1, source_target_pairs={{0,48},{8,56},{16,32},{24,40},{32,16},{40,24},{48,0},{56,8},{64,11... | collective-permute-start | bytes 104 | tf_op jit(solution)/shard_map/ppermute | solution.py:35
  59.9 2.7 %collective-permute-start.1 = (f32[8]{0:T(128)S(1)}, f32[8]{0:T(128)S(1)}, u32[]{:S(2)}, u32[]{:S(2)}) collective-permute-start(f32[8]{0:T(128)S(1)} %add.122), channel_id=1, source_target_pairs={{0,16},{8,24},{16,0},{24,8},{32,48},{40,56},{48,32},{56,40},{64,80... | collective-permute-start | bytes 104 | tf_op jit(solution)/shard_map/ppermute | solution.py:35
  59.9 3.9 %collective-permute-start.2 = (f32[8]{0:T(128)S(1)}, f32[8]{0:T(128)S(1)}, u32[]{:S(2)}, u32[]{:S(2)}) collective-permute-start(f32[8]{0:T(128)S(1)} %add.122), channel_id=1, source_target_pairs={{0,32},{8,40},{16,48},{24,56},{32,0},{40,8},{48,16},{56,24},{64,96... | collective-permute-start | bytes 104 | tf_op jit(solution)/shard_map/ppermute | solution.py:35
  63.9 3.9 %collective-permute-start.6 = (f32[8]{0:T(128)S(1)}, f32[8]{0:T(128)S(1)}, u32[]{:S(2)}, u32[]{:S(2)}) collective-permute-start(f32[8]{0:T(128)S(1)} %add_add_fusion.1), channel_id=1, source_target_pairs={{0,192},{8,200},{16,208},{24,216},{32,224},{40,232},{48,240},{56,2... | collective-permute-start | bytes 104 | tf_op jit(solution)/shard_map/ppermute | solution.py:35
  64.7 3.0 %collective-permute-start.4 = (f32[8]{0:T(128)S(1)}, f32[8]{0:T(128)S(1)}, u32[]{:S(2)}, u32[]{:S(2)}) collective-permute-start(f32[8]{0:T(128)S(1)} %add_add_fusion.1), channel_id=1, source_target_pairs={{0,64},{8,72},{16,80},{24,88},{32,96},{40,104},{48,112},{56,120},{... | collective-permute-start | bytes 104 | tf_op jit(solution)/shard_map/ppermute | solution.py:35
  64.7 3.9 %collective-permute-start.5 = (f32[8]{0:T(128)S(1)}, f32[8]{0:T(128)S(1)}, u32[]{:S(2)}, u32[]{:S(2)}) collective-permute-start(f32[8]{0:T(128)S(1)} %add_add_fusion.1), channel_id=1, source_target_pairs={{0,128},{8,136},{16,144},{24,152},{32,160},{40,168},{48,176},{56,1... | collective-permute-start | bytes 104 | tf_op jit(solution)/shard_map/ppermute | solution.py:35
Sparse Core Ops, SparseCore 0:
  102.9 62.4 all-gather.2

commit v9 on v8

--- a/solution.py
+++ b/solution.py
@@ -42,12 +42,8 @@
     x = group_sum(x, "wide", (1,))
     x = group_sum(x, "wide", (2, 4, 6))
     x = group_sum(x, "wide", (8, 16, 24))
-    n_narrow = lax.axis_size("narrow")
-    got = lax.all_to_all(jnp.broadcast_to(x[None], (n_narrow,) + x.shape), "narrow", 0, 0, tiled=True)
-    total = got[0]
-    for k in range(1, n_narrow):
-        total = total + got[k]
-    return total
+    x = group_sum(x, "narrow", (1,))
+    return group_sum(x, "narrow", (2, 4, 6))
 
 
 def pack(up_g, down_g, gain_g, n_wide, height):
@@ -163,16 +159,18 @@
     gain_first_new, gain_second_new, gain_update = moments(
         gain_sum, gain_master, gain_first, gain_second, 0.0
     )
-    partial = jnp.stack(
+    def square_sum(x):
+        return jnp.sum(x * x, keepdims=True).reshape(1)
+
+    partial = jnp.concatenate(
         [
-            jnp.sum(up_master * up_master),
-            jnp.sum(down_master * down_master),
-            jnp.sum(gain_master * gain_master),
-            jnp.sum(up_update * up_update),
-            jnp.sum(down_update * down_update),
-            jnp.sum(gain_update * gain_update),
-            jnp.float32(0.0),
-            jnp.float32(0.0),
+            square_sum(up_master),
+            square_sum(down_master),
+            square_sum(gain_master),
+            square_sum(up_update),
+            square_sum(down_update),
+            square_sum(gain_update),
+            jnp.zeros((2,), jnp.float32),
         ]
     )
     sums = mesh_sum(partial)

time: 183 us -> 185 us (1.011)
  blocking collectives: 67.4 us -> 52.8 us
  starting transfers between devices: 7.92 us -> 17.5 us
  waiting for transfers between devices: 65.9 us -> 73.7 us
    all_to_all x1 -> x0, blocking collectives: 14.5 us -> none  [mesh_sum(): lax.all_to_all(jnp.broadcast_to(x[None], (n_narrow,) + x.shape), 'narrow'...]
    ppermute x7 -> x11, starting transfers between devices: 7.89 us -> 17.5 us  [group_sum(): lax.ppermute(x, axis, [(i, i ^ m) for i in range(size)])]
    ppermute x7 -> x11, waiting for transfers between devices: 3.18 us -> 9.55 us  [group_sum(): lax.ppermute(x, axis, [(i, i ^ m) for i in range(size)])]
    another operation x2 -> x1, local copies, waits for them, and re-layouts: 3.99 us -> 0.01 us  [the longest x1 3.99 us: body(): jnp.stack([jnp.sum(up_master * up_master), jnp.sum(down_master * down_mas...]
    concatenate x0 -> x1, local copies, waits for them, and re-layouts: none -> 3.99 us  [body(): jnp.concatenate([square_sum(up_master), square_sum(down_master), square_s...]
  transfers between devices with their start and end apart: 8 -> 12, of which waited for: 4 -> 7; matrix products, arithmetic and copies ran while one was open for 0% -> 0% of each run, Pallas kernels for 0% -> 0%
where the time goes in v9:
time: 185 us
  waiting for transfers between devices  73.7 us (40%)
  blocking collectives  52.8 us (29%)
  between operations  18.5 us (10%)
  starting transfers between devices  17.5 us (9%)
  Pallas kernels  11.5 us (6%)
  local copies, waits for them, and re-layouts  6.56 us (4%)
  other arithmetic  4.37 us (2%)
    all_gather x1, waiting for transfers between devices, body(): whole = lax.all_gather(rows[None], 'wide', axis=0, tiled=True)  64.1 us
    all_to_all x1, blocking collectives, body(): received = lax.all_to_all(packed, 'wide', 0, 0, tiled=True)  40.1 us
    ppermute x11, starting transfers between devices, group_sum(): lax.ppermute(x, axis, [(i, i ^ m) for i in range(size)])  17.5 us
    all_to_all x1, blocking collectives, body(): lax.all_to_all(jnp.broadcast_to(low[None], (n_narrow,) + low.shape), 'nar...  12.8 us
    ppermute x11, waiting for transfers between devices, group_sum(): lax.ppermute(x, axis, [(i, i ^ m) for i in range(size)])  9.55 us
    pallas_call x1, Pallas kernels, unpack(): pl.pallas_call(kernel, grid=(n_narrow // per,), in_specs=[pl.BlockSpec((n...  7.96 us
    concatenate x1, local copies, waits for them, and re-layouts, body(): jnp.concatenate([square_sum(up_master), square_sum(down_master), square_s...  3.99 us
  transfers between devices with their start and end apart: 12, of which 7 were waited for; matrix products, arithmetic and copies ran while one was open for 0% of the time, Pallas kernels for 0%

profile of v9, /device:TPU:1, one launch (start us, length us, event | category | flops | bytes accessed | tf_op | source)
XLA Modules:
  0.0 184.9 jit_solution(9347564983961343602)
XLA Ops:
  7.2 0.0 all-gather.3.cloned.1.call-start
  7.2 3.6 %shard_map.211 = f32[32,144,128]{2,1,0:T(8,128)} custom-call(f32[24,11008]{1,0:T(8,128)} %bitcast.35, f32[64,4096]{1,0:T(8,128)} %bitcast.36, f32[1,512]{1,0:T(1,128)} %gain_ref.1), custom_call_target="tpu_custom_call" | custom-call | bytes 4466688 | tf_op jit(solution)/shard_map/pallas_call | solution.py:71
  10.8 0.0 copy-start.11
  10.8 0.0 copy-start.12
  10.8 0.0 copy-start
  10.9 0.0 copy-start.6
  10.9 0.0 copy-start.7
  10.9 40.1 %all_to_all.10 = f32[32,144,128]{2,1,0:T(8,128)S(1)} all-to-all(f32[32,144,128]{2,1,0:T(8,128)} %shard_map.211), channel_id=1, replica_groups=mesh['wide'=32,'narrow'=8] {'wide'}, dimensions={0} | all-to-all | bytes 4718592 | tf_op jit(solution)/shard_map/all_to_all | solution.py:146
  50.9 0.1 reduce_sum.63
  51.1 0.0 copy-done.3
  51.1 0.0 copy-done.8
  51.1 0.6 multiply_reduce_fusion.2
  51.8 0.0 copy-start.5
  51.8 1.1 multiply_reduce_fusion.4
  53.0 0.6 multiply_reduce_fusion
  53.6 4.0 %concatenate.12 = f32[8]{0:T(128)S(1)} concatenate(f32[1]{0:T(128)} %bitcast.4, f32[1]{0:T(128)} %bitcast.5, f32[1]{0:T(128)} %bitcast.6, f32[1]{0:T(128)} %bitcast.7, f32[1]{0:T(128)} %bitcast.8, f32[1]{0:T(128)} %bitcast.10, f32[2]{0:T(128)S(1)} %broadcast.48), dimensions={0} | concatenate | bytes 64 | tf_op jit(solution)/shard_map/concatenate | solution.py:165
  57.6 0.2 collective-permute-start
  57.8 1.0 collective-permute-done
  58.8 1.1 collective-permute-start.3
  59.9 0.0 collective-permute-start.1
  59.9 2.7 %collective-permute-start.2 = (f32[8]{0:T(128)S(1)}, f32[8]{0:T(128)S(1)}, u32[]{:S(2)}, u32[]{:S(2)}) collective-permute-start(f32[8]{0:T(128)S(1)} %add.107), channel_id=1, source_target_pairs={{0,32},{8,40},{16,48},{24,56},{32,0},{40,8},{48,16},{56,24},{64,96... | collective-permute-start | bytes 104 | tf_op jit(solution)/shard_map/ppermute | solution.py:35
  62.6 0.0 collective-permute-done.3
  62.6 0.0 collective-permute-done.1
  62.6 1.2 collective-permute-done.2
  63.9 0.9 collective-permute-start.6
  64.7 0.0 collective-permute-start.4
  64.7 3.0 %collective-permute-start.5 = (f32[8]{0:T(128)S(1)}, f32[8]{0:T(128)S(1)}, u32[]{:S(2)}, u32[]{:S(2)}) collective-permute-start(f32[8]{0:T(128)S(1)} %add_add_fusion.2), channel_id=1, source_target_pairs={{0,128},{8,136},{16,144},{24,152},{32,160},{40,168},{48,176},{56,1... | collective-permute-start | bytes 104 | tf_op jit(solution)/shard_map/ppermute | solution.py:35
  67.7 0.0 collective-permute-done.6
  67.7 0.0 collective-permute-done.4
  67.7 1.0 collective-permute-done.5
  68.7 1.6 collective-permute-start.7
  70.3 1.0 collective-permute-done.7
  71.3 5.8 %collective-permute-start.10 = (f32[8]{0:T(128)S(1)}, f32[8]{0:T(128)S(1)}, u32[]{:S(2)}, u32[]{:S(2)}) collective-permute-start(f32[8]{0:T(128)S(1)} %add.114), channel_id=1, source_target_pairs={{0,6},{1,7},{2,4},{3,5},{4,2},{5,3},{6,0},{7,1},{8,14},{9,15},{10,... | collective-permute-start | bytes 104 | tf_op jit(solution)/shard_map/ppermute | solution.py:35
  77.1 1.2 collective-permute-start.8
  78.3 0.9 collective-permute-start.9
  79.2 0.0 collective-permute-done.10
  79.2 1.2 collective-permute-done.8
  80.4 4.2 %collective-permute-done.9 = f32[8]{0:T(128)S(1)} collective-permute-done((f32[8]{0:T(128)S(1)}, f32[8]{0:T(128)S(1)}, u32[]{:S(2)}, u32[]{:S(2)}) %collective-permute-start.9) | collective-permute-done | bytes 64 | tf_op jit(solution)/shard_map/ppermute | solution.py:35
  84.6 0.6 fusion.18
  86.7 0.6 fusion.10
  90.1 0.5 fusion.12
  90.7 0.6 fusion.11
  91.4 12.8 %all_to_all.11 = bf16[8,48,384]{2,1,0:T(8,128)(2,1)} all-to-all(bf16[8,48,384]{2,1,0:T(8,128)(2,1)S(1)} %broadcast_in_dim.17), channel_id=1, replica_groups=mesh['wide'=32,'narrow'=8] {'narrow'}, dimensions={0} | all-to-all | bytes 589824 | tf_op jit(solution)/shard_map/all_to_all | solution.py:192
  104.1 0.0 all-gather.3.cloned.1.call-update
  104.1 64.1 %all-gather.3.cloned.1.call-done = bf16[256,48,384]{2,1,0:T(8,128)(2,1)} async-done(((bf16[8,48,384]{2,1,0:T(8,128)(2,1)}), bf16[256,48,384]{2,1,0:T(8,128)(2,1)}) %all-gather.3.cloned.1.call-update) | async-done | bytes 9437200 | tf_op jit(solution)/shard_map/all_gather | solution.py:195
  168.3 8.0 %shard_map.212 = (bf16[192,11008]{1,0:T(8,128)(2,1)}, bf16[512,4096]{1,0:T(8,128)(2,1)}) custom-call(bf16[32,8,48,384]{3,2,1,0:T(8,128)(2,1)} %bitcast.33), custom_call_target="tpu_custom_call" | custom-call | bytes 17858560 | tf_op jit(solution)/shard_map/pallas_call | solution.py:104
  176.2 1.1 slice.73
  177.4 0.7 reshape.61
  (33 shorter events, 0.2 us)
Async XLA Ops:
  7.2 161.1 %all-gather.3.cloned.1.call-start = ((), (), s32[]{:S(2)}) async-start(), calls=%async_computation.2 | async-start | bytes 9732096 | tf_op jit(solution)/shard_map/all_gather | solution.py:195
  10.8 40.3 %copy-start.3 = (f32[64,128]{1,0:T(8,128)S(1)}, f32[64,128]{1,0:T(8,128)}, u32[]{:S(2)}) copy-start(f32[64,128]{1,0:T(8,128)} %param.16) | copy-start | bytes 98308
  10.8 40.3 %copy-start.8 = (f32[64,128]{1,0:T(8,128)S(1)}, f32[64,128]{1,0:T(8,128)}, u32[]{:S(2)}) copy-start(f32[64,128]{1,0:T(8,128)} %param.19) | copy-start | bytes 98308
  10.8 40.3 %copy-start.9 = (f32[64,128]{1,0:T(8,128)S(1)}, f32[64,128]{1,0:T(8,128)}, u32[]{:S(2)}) copy-start(f32[64,128]{1,0:T(8,128)} %param.22) | copy-start | bytes 98308
  10.8 41.0 %copy-start.10 = (f32[16]{0:T(128)S(1)}, f32[16]{0:T(128)}, u32[]{:S(2)}) copy-start(f32[16]{0:T(128)} %param.17) | copy-start | bytes 196
  10.8 41.0 %copy-start.11 = (f32[16]{0:T(128)S(1)}, f32[16]{0:T(128)}, u32[]{:S(2)}) copy-start(f32[16]{0:T(128)} %param.20) | copy-start | bytes 196
  10.8 41.0 %copy-start.12 = (f32[16]{0:T(128)S(1)}, f32[16]{0:T(128)}, u32[]{:S(2)}) copy-start(f32[16]{0:T(128)} %param.23) | copy-start | bytes 196
  10.8 42.1 %copy-start = (f32[24,344]{1,0:T(8,128)S(1)}, f32[24,344]{1,0:T(8,128)}, u32[]{:S(2)}) copy-start(f32[24,344]{1,0:T(8,128)} %param.15) | copy-start | bytes 99076
  10.9 42.1 %copy-start.6 = (f32[24,344]{1,0:T(8,128)S(1)}, f32[24,344]{1,0:T(8,128)}, u32[]{:S(2)}) copy-start(f32[24,344]{1,0:T(8,128)} %param.21) | copy-start | bytes 99076
  10.9 42.1 %copy-start.7 = (f32[24,344]{1,0:T(8,128)S(1)}, f32[24,344]{1,0:T(8,128)}, u32[]{:S(2)}) copy-start(f32[24,344]{1,0:T(8,128)} %param.18) | copy-start | bytes 99076
  51.8 124.4 %copy-start.4 = (f32[64,128]{1,0:T(8,128)}, f32[64,128]{1,0:T(8,128)S(1)}, u32[]{:S(2)}) copy-start(f32[64,128]{1,0:T(8,128)S(1)} %get-tuple-element.30) | copy-start | bytes 98308
  51.8 124.4 %copy-start.5 = (f32[64,128]{1,0:T(8,128)}, f32[64,128]{1,0:T(8,128)S(1)}, u32[]{:S(2)}) copy-start(f32[64,128]{1,0:T(8,128)S(1)} %get-tuple-element.31) | copy-start | bytes 98308
  53.6 122.6 %copy-start.1 = (f32[24,344]{1,0:T(8,128)}, f32[24,344]{1,0:T(8,128)S(1)}, u32[]{:S(2)}) copy-start(f32[24,344]{1,0:T(8,128)S(1)} %get-tuple-element.32) | copy-start | bytes 99076
  53.6 122.6 %copy-start.2 = (f32[24,344]{1,0:T(8,128)}, f32[24,344]{1,0:T(8,128)S(1)}, u32[]{:S(2)}) copy-start(f32[24,344]{1,0:T(8,128)S(1)} %get-tuple-element.33) | copy-start | bytes 99076
  57.6 1.2 collective-permute-start
  58.8 3.9 %collective-permute-start.3 = (f32[8]{0:T(128)S(1)}, f32[8]{0:T(128)S(1)}, u32[]{:S(2)}, u32[]{:S(2)}) collective-permute-start(f32[8]{0:T(128)S(1)} %add.107), channel_id=1, source_target_pairs={{0,48},{8,56},{16,32},{24,40},{32,16},{40,24},{48,0},{56,8},{64,11... | collective-permute-start | bytes 104 | tf_op jit(solution)/shard_map/ppermute | solution.py:35
  59.9 2.7 %collective-permute-start.1 = (f32[8]{0:T(128)S(1)}, f32[8]{0:T(128)S(1)}, u32[]{:S(2)}, u32[]{:S(2)}) collective-permute-start(f32[8]{0:T(128)S(1)} %add.107), channel_id=1, source_target_pairs={{0,16},{8,24},{16,0},{24,8},{32,48},{40,56},{48,32},{56,40},{64,80... | collective-permute-start | bytes 104 | tf_op jit(solution)/shard_map/ppermute | solution.py:35
  59.9 3.9 %collective-permute-start.2 = (f32[8]{0:T(128)S(1)}, f32[8]{0:T(128)S(1)}, u32[]{:S(2)}, u32[]{:S(2)}) collective-permute-start(f32[8]{0:T(128)S(1)} %add.107), channel_id=1, source_target_pairs={{0,32},{8,40},{16,48},{24,56},{32,0},{40,8},{48,16},{56,24},{64,96... | collective-permute-start | bytes 104 | tf_op jit(solution)/shard_map/ppermute | solution.py:35
  63.9 3.9 %collective-permute-start.6 = (f32[8]{0:T(128)S(1)}, f32[8]{0:T(128)S(1)}, u32[]{:S(2)}, u32[]{:S(2)}) collective-permute-start(f32[8]{0:T(128)S(1)} %add_add_fusion.2), channel_id=1, source_target_pairs={{0,192},{8,200},{16,208},{24,216},{32,224},{40,232},{48,240},{56,2... | collective-permute-start | bytes 104 | tf_op jit(solution)/shard_map/ppermute | solution.py:35
  64.7 3.0 %collective-permute-start.4 = (f32[8]{0:T(128)S(1)}, f32[8]{0:T(128)S(1)}, u32[]{:S(2)}, u32[]{:S(2)}) collective-permute-start(f32[8]{0:T(128)S(1)} %add_add_fusion.2), channel_id=1, source_target_pairs={{0,64},{8,72},{16,80},{24,88},{32,96},{40,104},{48,112},{56,120},{... | collective-permute-start | bytes 104 | tf_op jit(solution)/shard_map/ppermute | solution.py:35
  64.7 3.9 %collective-permute-start.5 = (f32[8]{0:T(128)S(1)}, f32[8]{0:T(128)S(1)}, u32[]{:S(2)}, u32[]{:S(2)}) collective-permute-start(f32[8]{0:T(128)S(1)} %add_add_fusion.2), channel_id=1, source_target_pairs={{0,128},{8,136},{16,144},{24,152},{32,160},{40,168},{48,176},{56,1... | collective-permute-start | bytes 104 | tf_op jit(solution)/shard_map/ppermute | solution.py:35
  68.7 2.6 %collective-permute-start.7 = (f32[8]{0:T(128)S(1)}, f32[8]{0:T(128)S(1)}, u32[]{:S(2)}, u32[]{:S(2)}) collective-permute-start(f32[8]{0:T(128)S(1)} %add_add_fusion.1), channel_id=1, source_target_pairs={{0,1},{1,0},{2,3},{3,2},{4,5},{5,4},{6,7},{7,6},{8,9},{9,8},{10,11... | collective-permute-start | bytes 104 | tf_op jit(solution)/shard_map/ppermute | solution.py:35
  71.3 7.9 %collective-permute-start.10 = (f32[8]{0:T(128)S(1)}, f32[8]{0:T(128)S(1)}, u32[]{:S(2)}, u32[]{:S(2)}) collective-permute-start(f32[8]{0:T(128)S(1)} %add.114), channel_id=1, source_target_pairs={{0,6},{1,7},{2,4},{3,5},{4,2},{5,3},{6,0},{7,1},{8,14},{9,15},{10,... | collective-permute-start | bytes 104 | tf_op jit(solution)/shard_map/ppermute | solution.py:35
  77.1 3.3 %collective-permute-start.8 = (f32[8]{0:T(128)S(1)}, f32[8]{0:T(128)S(1)}, u32[]{:S(2)}, u32[]{:S(2)}) collective-permute-start(f32[8]{0:T(128)S(1)} %add.114), channel_id=1, source_target_pairs={{0,2},{1,3},{2,0},{3,1},{4,6},{5,7},{6,4},{7,5},{8,10},{9,11},{10,... | collective-permute-start | bytes 104 | tf_op jit(solution)/shard_map/ppermute | solution.py:35
  78.3 6.3 %collective-permute-start.9 = (f32[8]{0:T(128)S(1)}, f32[8]{0:T(128)S(1)}, u32[]{:S(2)}, u32[]{:S(2)}) collective-permute-start(f32[8]{0:T(128)S(1)} %add.114), channel_id=1, source_target_pairs={{0,4},{1,5},{2,6},{3,7},{4,0},{5,1},{6,2},{7,3},{8,12},{9,13},{10,... | collective-permute-start | bytes 104 | tf_op jit(solution)/shard_map/ppermute | solution.py:35
Sparse Core Ops, SparseCore 0:
  104.3 63.9 all-gather.2

commit v10 on v8

--- a/solution.py
+++ b/solution.py
@@ -39,15 +39,9 @@
 
 
 def mesh_sum(x):
-    x = group_sum(x, "wide", (1,))
-    x = group_sum(x, "wide", (2, 4, 6))
-    x = group_sum(x, "wide", (8, 16, 24))
-    n_narrow = lax.axis_size("narrow")
-    got = lax.all_to_all(jnp.broadcast_to(x[None], (n_narrow,) + x.shape), "narrow", 0, 0, tiled=True)
-    total = got[0]
-    for k in range(1, n_narrow):
-        total = total + got[k]
-    return total
+    n = lax.axis_size("wide") * lax.axis_size("narrow")
+    got = lax.all_to_all(jnp.broadcast_to(x[None], (n,) + x.shape), ("wide", "narrow"), 0, 0, tiled=True)
+    return jnp.sum(got, axis=0)
 
 
 def pack(up_g, down_g, gain_g, n_wide, height):

time: 183 us -> 175 us (0.956)
  waiting for transfers between devices: 65.9 us -> 53.9 us
  blocking collectives: 67.4 us -> 79.2 us
  starting transfers between devices: 7.92 us -> 0.04 us
    all_to_all x1, blocking collectives: 14.5 us -> 23.7 us  [mesh_sum(): lax.all_to_all(jnp.broadcast_to(x[None], (n,) + x.shape), ('wide', 'narro...]
    all_gather x1, waiting for transfers between devices: 62.7 us -> 53.8 us  [body(): whole = lax.all_gather(rows[None], 'wide', axis=0, tiled=True)]
    ppermute x7 -> x0, starting transfers between devices: 7.89 us -> none  [group_sum(): lax.ppermute(x, axis, [(i, i ^ m) for i in range(size)])]
    ppermute x7 -> x0, waiting for transfers between devices: 3.18 us -> none  [group_sum(): lax.ppermute(x, axis, [(i, i ^ m) for i in range(size)])]
    all_to_all x1, blocking collectives: 12.8 us -> 15.5 us  [body(): lax.all_to_all(jnp.broadcast_to(low[None], (n_narrow,) + low.shape), 'nar...]
  transfers between devices with their start and end apart: 8 -> 1, of which waited for: 4 -> 1; matrix products, arithmetic and copies ran while one was open for 0% -> 0% of each run, Pallas kernels for 0% -> 0%
where the time goes in v10:
time: 175 us; the launch traced here: 174 us
  blocking collectives  79.2 us (45%)
  waiting for transfers between devices  53.9 us (31%)
  between operations  18.5 us (11%)
  Pallas kernels  11.5 us (7%)
  local copies, waits for them, and re-layouts  6.64 us (4%)
  other arithmetic  4.64 us (3%)
    all_gather x1, waiting for transfers between devices, body(): whole = lax.all_gather(rows[None], 'wide', axis=0, tiled=True)  53.8 us
    all_to_all x1, blocking collectives, body(): received = lax.all_to_all(packed, 'wide', 0, 0, tiled=True)  40.1 us
    all_to_all x1, blocking collectives, mesh_sum(): lax.all_to_all(jnp.broadcast_to(x[None], (n,) + x.shape), ('wide', 'narro...  23.7 us
    all_to_all x1, blocking collectives, body(): lax.all_to_all(jnp.broadcast_to(low[None], (n_narrow,) + low.shape), 'nar...  15.5 us
    pallas_call x1, Pallas kernels, unpack(): pl.pallas_call(kernel, grid=(n_narrow // per,), in_specs=[pl.BlockSpec((n...  7.96 us
    another operation x1, local copies, waits for them, and re-layouts, body(): jnp.stack([jnp.sum(up_master * up_master), jnp.sum(down_master * down_mas...  3.99 us
    pallas_call x1, Pallas kernels, pack(): pl.pallas_call(kernel, in_specs=[pl.BlockSpec(memory_space=pltpu.VMEM)] *...  3.59 us
  transfers between devices with their start and end apart: 1, of which 1 were waited for; matrix products, arithmetic and copies ran while one was open for 0% of the time, Pallas kernels for 0%

profile of v10, /device:TPU:1, one launch (start us, length us, event | category | flops | bytes accessed | tf_op | source)
XLA Modules:
  0.0 174.4 jit_solution(16033865204280016587)
XLA Ops:
  7.2 0.0 all-gather.3.cloned.1.call-start
  7.2 3.6 %shard_map.211 = f32[32,144,128]{2,1,0:T(8,128)} custom-call(f32[24,11008]{1,0:T(8,128)} %bitcast.35, f32[64,4096]{1,0:T(8,128)} %bitcast.36, f32[1,512]{1,0:T(1,128)} %gain_ref.1), custom_call_target="tpu_custom_call" | custom-call | bytes 4466688 | tf_op jit(solution)/shard_map/pallas_call | solution.py:69
  10.8 0.0 copy-start.3
  10.8 0.0 copy-start.8
  10.8 0.0 copy-start.9
  10.8 0.0 copy-start.10
  10.8 0.0 copy-start.11
  10.8 0.0 copy-start.12
  10.8 0.0 copy-start
  10.9 0.0 copy-start.6
  10.9 0.0 copy-start.7
  10.9 40.1 %all_to_all.16 = f32[32,144,128]{2,1,0:T(8,128)S(1)} all-to-all(f32[32,144,128]{2,1,0:T(8,128)} %shard_map.211), channel_id=1, replica_groups=mesh['wide'=32,'narrow'=8] {'wide'}, dimensions={0} | all-to-all | bytes 4718592 | tf_op jit(solution)/shard_map/all_to_all | solution.py:144
  50.9 0.1 reduce_sum.72
  51.1 0.0 copy-done.3
  51.1 0.0 copy-done.8
  51.1 0.0 copy-done.9
  51.1 0.6 multiply_reduce_fusion.2
  51.8 0.0 copy-done.10
  51.8 0.0 copy-done.11
  51.8 0.0 copy-done.12
  51.8 0.0 copy-start.4
  51.8 0.0 copy-start.5
  51.8 1.1 multiply_reduce_fusion.4
  52.9 0.0 copy-done
  52.9 0.0 copy-done.6
  53.0 0.0 copy-done.7
  53.0 0.6 multiply_reduce_fusion
  53.6 0.0 copy-start.1
  53.6 0.0 copy-start.2
  53.6 4.0 %stack.27 = f32[8]{0:T(128)S(1)} concatenate(f32[1]{0:T(128)} %bitcast.4, f32[1]{0:T(128)} %bitcast.5, f32[1]{0:T(128)} %bitcast.6, f32[1]{0:T(128)} %bitcast.7, f32[1]{0:T(128)} %bitcast.8, f32[1]{0:T(128)} %bitcast.10, f32[2]{0:T(128)S(1)} %broadcast.51), dimensions={0} | concatenate | bytes 64 | tf_op jit(solution)/shard_map/stack | solution.py:160
  57.6 0.1 broadcast_in_dim.6
  57.7 23.7 %all_to_all.17 = f32[256,1,8]{2,1,0:T(1,128)S(1)} all-to-all(f32[256,1,8]{2,1,0:T(1,128)S(1)} %broadcast_in_dim.6), channel_id=1, replica_groups=mesh['wide'=32,'narrow'=8] {'wide','narrow'}, dimensions={0} | all-to-all | bytes 16384 | tf_op jit(solution)/shard_map/all_to_all | solution.py:43
  81.4 0.3 reduce_sum.79
  81.6 0.6 fusion.18
  83.7 0.6 fusion.10
  87.2 0.5 fusion.12
  87.7 0.6 fusion.11
  88.4 15.5 %all_to_all.18 = bf16[8,48,384]{2,1,0:T(8,128)(2,1)} all-to-all(bf16[8,48,384]{2,1,0:T(8,128)(2,1)S(1)} %broadcast_in_dim.7), channel_id=1, replica_groups=mesh['wide'=32,'narrow'=8] {'narrow'}, dimensions={0} | all-to-all | bytes 589824 | tf_op jit(solution)/shard_map/all_to_all | solution.py:188
  103.8 0.0 all-gather.3.cloned.1.call-update
  103.9 53.8 %all-gather.3.cloned.1.call-done = bf16[256,48,384]{2,1,0:T(8,128)(2,1)} async-done(((bf16[8,48,384]{2,1,0:T(8,128)(2,1)}), bf16[256,48,384]{2,1,0:T(8,128)(2,1)}) %all-gather.3.cloned.1.call-update) | async-done | bytes 9437200 | tf_op jit(solution)/shard_map/all_gather | solution.py:191
  157.7 8.0 %shard_map.212 = (bf16[192,11008]{1,0:T(8,128)(2,1)}, bf16[512,4096]{1,0:T(8,128)(2,1)}) custom-call(bf16[32,8,48,384]{3,2,1,0:T(8,128)(2,1)} %bitcast.33), custom_call_target="tpu_custom_call" | custom-call | bytes 17858560 | tf_op jit(solution)/shard_map/pallas_call | solution.py:102
  165.7 0.0 copy-done.4
  165.7 0.0 copy-done.5
  165.7 0.0 copy-done.1
  165.7 0.0 copy-done.2
  165.7 1.1 slice.73
  166.8 0.7 reshape.67
  (10 shorter events, 0.1 us)
Async XLA Ops:
  7.2 150.5 %all-gather.3.cloned.1.call-start = ((), (), s32[]{:S(2)}) async-start(), calls=%async_computation.3 | async-start | bytes 9732096 | tf_op jit(solution)/shard_map/all_gather | solution.py:191
  10.8 40.3 %copy-start.3 = (f32[64,128]{1,0:T(8,128)S(1)}, f32[64,128]{1,0:T(8,128)}, u32[]{:S(2)}) copy-start(f32[64,128]{1,0:T(8,128)} %param.16) | copy-start | bytes 98308
  10.8 40.3 %copy-start.8 = (f32[64,128]{1,0:T(8,128)S(1)}, f32[64,128]{1,0:T(8,128)}, u32[]{:S(2)}) copy-start(f32[64,128]{1,0:T(8,128)} %param.19) | copy-start | bytes 98308
  10.8 40.3 %copy-start.9 = (f32[64,128]{1,0:T(8,128)S(1)}, f32[64,128]{1,0:T(8,128)}, u32[]{:S(2)}) copy-start(f32[64,128]{1,0:T(8,128)} %param.22) | copy-start | bytes 98308
  10.8 41.0 %copy-start.10 = (f32[16]{0:T(128)S(1)}, f32[16]{0:T(128)}, u32[]{:S(2)}) copy-start(f32[16]{0:T(128)} %param.17) | copy-start | bytes 196
  10.8 41.0 %copy-start.11 = (f32[16]{0:T(128)S(1)}, f32[16]{0:T(128)}, u32[]{:S(2)}) copy-start(f32[16]{0:T(128)} %param.20) | copy-start | bytes 196
  10.8 41.0 %copy-start.12 = (f32[16]{0:T(128)S(1)}, f32[16]{0:T(128)}, u32[]{:S(2)}) copy-start(f32[16]{0:T(128)} %param.23) | copy-start | bytes 196
  10.8 42.1 %copy-start = (f32[24,344]{1,0:T(8,128)S(1)}, f32[24,344]{1,0:T(8,128)}, u32[]{:S(2)}) copy-start(f32[24,344]{1,0:T(8,128)} %param.15) | copy-start | bytes 99076
  10.9 42.1 %copy-start.6 = (f32[24,344]{1,0:T(8,128)S(1)}, f32[24,344]{1,0:T(8,128)}, u32[]{:S(2)}) copy-start(f32[24,344]{1,0:T(8,128)} %param.21) | copy-start | bytes 99076
  10.9 42.1 %copy-start.7 = (f32[24,344]{1,0:T(8,128)S(1)}, f32[24,344]{1,0:T(8,128)}, u32[]{:S(2)}) copy-start(f32[24,344]{1,0:T(8,128)} %param.18) | copy-start | bytes 99076
  51.8 113.9 %copy-start.4 = (f32[64,128]{1,0:T(8,128)}, f32[64,128]{1,0:T(8,128)S(1)}, u32[]{:S(2)}) copy-start(f32[64,128]{1,0:T(8,128)S(1)} %get-tuple-element.30) | copy-start | bytes 98308
  51.8 113.9 %copy-start.5 = (f32[64,128]{1,0:T(8,128)}, f32[64,128]{1,0:T(8,128)S(1)}, u32[]{:S(2)}) copy-start(f32[64,128]{1,0:T(8,128)S(1)} %get-tuple-element.31) | copy-start | bytes 98308
  53.6 112.1 %copy-start.1 = (f32[24,344]{1,0:T(8,128)}, f32[24,344]{1,0:T(8,128)S(1)}, u32[]{:S(2)}) copy-start(f32[24,344]{1,0:T(8,128)S(1)} %get-tuple-element.32) | copy-start | bytes 99076
  53.6 112.1 %copy-start.2 = (f32[24,344]{1,0:T(8,128)}, f32[24,344]{1,0:T(8,128)S(1)}, u32[]{:S(2)}) copy-start(f32[24,344]{1,0:T(8,128)S(1)} %get-tuple-element.33) | copy-start | bytes 99076
Sparse Core Ops, SparseCore 0:
  104.0 53.6 all-gather.2

commit v11 on v10

--- a/solution.py
+++ b/solution.py
@@ -40,8 +40,8 @@
 
 def mesh_sum(x):
     n = lax.axis_size("wide") * lax.axis_size("narrow")
-    got = lax.all_to_all(jnp.broadcast_to(x[None], (n,) + x.shape), ("wide", "narrow"), 0, 0, tiled=True)
-    return jnp.sum(got, axis=0)
+    got = lax.all_to_all(jnp.broadcast_to(x[:, None], x.shape + (n,)), ("wide", "narrow"), 1, 1, tiled=True)
+    return jnp.sum(got, axis=1)
 
 
 def pack(up_g, down_g, gain_g, n_wide, height):

time: 175 us -> 175 us (level)
  no operation moved by 1% of the time
where the time goes in v11:
time: 175 us; the launch traced here: 174 us
  blocking collectives  79.2 us (45%)
  waiting for transfers between devices  53.9 us (31%)
  between operations  18.5 us (11%)
  Pallas kernels  11.5 us (7%)
  local copies, waits for them, and re-layouts  6.64 us (4%)
  other arithmetic  4.64 us (3%)
    all_gather x1, waiting for transfers between devices, body(): whole = lax.all_gather(rows[None], 'wide', axis=0, tiled=True)  53.8 us
    all_to_all x1, blocking collectives, body(): received = lax.all_to_all(packed, 'wide', 0, 0, tiled=True)  40.1 us
    all_to_all x1, blocking collectives, mesh_sum(): lax.all_to_all(jnp.broadcast_to(x[:, None], x.shape + (n,)), ('wide', 'na...  23.7 us
    all_to_all x1, blocking collectives, body(): lax.all_to_all(jnp.broadcast_to(low[None], (n_narrow,) + low.shape), 'nar...  15.5 us
    pallas_call x1, Pallas kernels, unpack(): pl.pallas_call(kernel, grid=(n_narrow // per,), in_specs=[pl.BlockSpec((n...  7.96 us
    another operation x1, local copies, waits for them, and re-layouts, body(): jnp.stack([jnp.sum(up_master * up_master), jnp.sum(down_master * down_mas...  3.99 us
    pallas_call x1, Pallas kernels, pack(): pl.pallas_call(kernel, in_specs=[pl.BlockSpec(memory_space=pltpu.VMEM)] *...  3.59 us
  transfers between devices with their start and end apart: 1, of which 1 were waited for; matrix products, arithmetic and copies ran while one was open for 0% of the time, Pallas kernels for 0%

profile of v11, /device:TPU:1, one launch (start us, length us, event | category | flops | bytes accessed | tf_op | source)
XLA Modules:
  0.0 174.4 jit_solution(3316532160878402538)
XLA Ops:
  7.2 0.0 all-gather.3.cloned.1.call-start
  7.2 3.6 %shard_map.211 = f32[32,144,128]{2,1,0:T(8,128)} custom-call(f32[24,11008]{1,0:T(8,128)} %bitcast.35, f32[64,4096]{1,0:T(8,128)} %bitcast.36, f32[1,512]{1,0:T(1,128)} %gain_ref.1), custom_call_target="tpu_custom_call" | custom-call | bytes 4466688 | tf_op jit(solution)/shard_map/pallas_call | solution.py:69
  10.8 0.0 copy-start.3
  10.8 0.0 copy-start.8
  10.8 0.0 copy-start.9
  10.8 0.0 copy-start.10
  10.8 0.0 copy-start.11
  10.8 0.0 copy-start.12
  10.8 0.0 copy-start
  10.9 0.0 copy-start.6
  10.9 0.0 copy-start.7
  10.9 40.1 %all_to_all.16 = f32[32,144,128]{2,1,0:T(8,128)S(1)} all-to-all(f32[32,144,128]{2,1,0:T(8,128)} %shard_map.211), channel_id=1, replica_groups=mesh['wide'=32,'narrow'=8] {'wide'}, dimensions={0} | all-to-all | bytes 4718592 | tf_op jit(solution)/shard_map/all_to_all | solution.py:144
  50.9 0.1 reduce_sum.72
  51.1 0.0 copy-done.3
  51.1 0.0 copy-done.8
  51.1 0.0 copy-done.9
  51.1 0.6 multiply_reduce_fusion.2
  51.8 0.0 copy-done.10
  51.8 0.0 copy-done.11
  51.8 0.0 copy-done.12
  51.8 0.0 copy-start.4
  51.8 0.0 copy-start.5
  51.8 1.1 multiply_reduce_fusion.4
  52.9 0.0 copy-done
  52.9 0.0 copy-done.6
  53.0 0.0 copy-done.7
  53.0 0.6 multiply_reduce_fusion
  53.6 0.0 copy-start.1
  53.6 0.0 copy-start.2
  53.6 4.0 %stack.27 = f32[8]{0:T(128)S(1)} concatenate(f32[1]{0:T(128)} %bitcast.4, f32[1]{0:T(128)} %bitcast.5, f32[1]{0:T(128)} %bitcast.6, f32[1]{0:T(128)} %bitcast.7, f32[1]{0:T(128)} %bitcast.8, f32[1]{0:T(128)} %bitcast.10, f32[2]{0:T(128)S(1)} %broadcast.53), dimensions={0} | concatenate | bytes 64 | tf_op jit(solution)/shard_map/stack | solution.py:160
  57.6 0.1 broadcast_in_dim.6
  57.7 23.7 %all_to_all.17 = f32[8,256,1]{0,2,1:T(1,128)S(1)} all-to-all(f32[8,256,1]{0,2,1:T(1,128)S(1)} %broadcast_in_dim.6), channel_id=1, replica_groups=mesh['wide'=32,'narrow'=8] {'wide','narrow'}, dimensions={1} | all-to-all | bytes 16384 | tf_op jit(solution)/shard_map/all_to_all | solution.py:43
  81.4 0.3 reduce_sum.79
  81.6 0.6 fusion.18
  83.7 0.6 fusion.10
  87.2 0.5 fusion.12
  87.7 0.6 fusion.11
  88.4 15.5 %all_to_all.18 = bf16[8,48,384]{2,1,0:T(8,128)(2,1)} all-to-all(bf16[8,48,384]{2,1,0:T(8,128)(2,1)S(1)} %broadcast_in_dim.7), channel_id=1, replica_groups=mesh['wide'=32,'narrow'=8] {'narrow'}, dimensions={0} | all-to-all | bytes 589824 | tf_op jit(solution)/shard_map/all_to_all | solution.py:188
  103.8 0.0 all-gather.3.cloned.1.call-update
  103.9 53.8 %all-gather.3.cloned.1.call-done = bf16[256,48,384]{2,1,0:T(8,128)(2,1)} async-done(((bf16[8,48,384]{2,1,0:T(8,128)(2,1)}), bf16[256,48,384]{2,1,0:T(8,128)(2,1)}) %all-gather.3.cloned.1.call-update) | async-done | bytes 9437200 | tf_op jit(solution)/shard_map/all_gather | solution.py:191
  157.7 8.0 %shard_map.212 = (bf16[192,11008]{1,0:T(8,128)(2,1)}, bf16[512,4096]{1,0:T(8,128)(2,1)}) custom-call(bf16[32,8,48,384]{3,2,1,0:T(8,128)(2,1)} %bitcast.33), custom_call_target="tpu_custom_call" | custom-call | bytes 17858560 | tf_op jit(solution)/shard_map/pallas_call | solution.py:102
  165.7 0.0 copy-done.4
  165.7 0.0 copy-done.5
  165.7 0.0 copy-done.1
  165.7 0.0 copy-done.2
  165.7 1.1 slice.73
  166.8 0.7 reshape.68
  (10 shorter events, 0.1 us)
Async XLA Ops:
  7.2 150.5 %all-gather.3.cloned.1.call-start = ((), (), s32[]{:S(2)}) async-start(), calls=%async_computation.3 | async-start | bytes 9732096 | tf_op jit(solution)/shard_map/all_gather | solution.py:191
  10.8 40.3 %copy-start.3 = (f32[64,128]{1,0:T(8,128)S(1)}, f32[64,128]{1,0:T(8,128)}, u32[]{:S(2)}) copy-start(f32[64,128]{1,0:T(8,128)} %param.16) | copy-start | bytes 98308
  10.8 40.3 %copy-start.8 = (f32[64,128]{1,0:T(8,128)S(1)}, f32[64,128]{1,0:T(8,128)}, u32[]{:S(2)}) copy-start(f32[64,128]{1,0:T(8,128)} %param.19) | copy-start | bytes 98308
  10.8 40.3 %copy-start.9 = (f32[64,128]{1,0:T(8,128)S(1)}, f32[64,128]{1,0:T(8,128)}, u32[]{:S(2)}) copy-start(f32[64,128]{1,0:T(8,128)} %param.22) | copy-start | bytes 98308
  10.8 41.0 %copy-start.10 = (f32[16]{0:T(128)S(1)}, f32[16]{0:T(128)}, u32[]{:S(2)}) copy-start(f32[16]{0:T(128)} %param.17) | copy-start | bytes 196
  10.8 41.0 %copy-start.11 = (f32[16]{0:T(128)S(1)}, f32[16]{0:T(128)}, u32[]{:S(2)}) copy-start(f32[16]{0:T(128)} %param.20) | copy-start | bytes 196
  10.8 41.0 %copy-start.12 = (f32[16]{0:T(128)S(1)}, f32[16]{0:T(128)}, u32[]{:S(2)}) copy-start(f32[16]{0:T(128)} %param.23) | copy-start | bytes 196
  10.8 42.1 %copy-start = (f32[24,344]{1,0:T(8,128)S(1)}, f32[24,344]{1,0:T(8,128)}, u32[]{:S(2)}) copy-start(f32[24,344]{1,0:T(8,128)} %param.15) | copy-start | bytes 99076
  10.9 42.1 %copy-start.6 = (f32[24,344]{1,0:T(8,128)S(1)}, f32[24,344]{1,0:T(8,128)}, u32[]{:S(2)}) copy-start(f32[24,344]{1,0:T(8,128)} %param.21) | copy-start | bytes 99076
  10.9 42.1 %copy-start.7 = (f32[24,344]{1,0:T(8,128)S(1)}, f32[24,344]{1,0:T(8,128)}, u32[]{:S(2)}) copy-start(f32[24,344]{1,0:T(8,128)} %param.18) | copy-start | bytes 99076
  51.8 113.9 %copy-start.4 = (f32[64,128]{1,0:T(8,128)}, f32[64,128]{1,0:T(8,128)S(1)}, u32[]{:S(2)}) copy-start(f32[64,128]{1,0:T(8,128)S(1)} %get-tuple-element.30) | copy-start | bytes 98308
  51.8 113.9 %copy-start.5 = (f32[64,128]{1,0:T(8,128)}, f32[64,128]{1,0:T(8,128)S(1)}, u32[]{:S(2)}) copy-start(f32[64,128]{1,0:T(8,128)S(1)} %get-tuple-element.31) | copy-start | bytes 98308
  53.6 112.1 %copy-start.1 = (f32[24,344]{1,0:T(8,128)}, f32[24,344]{1,0:T(8,128)S(1)}, u32[]{:S(2)}) copy-start(f32[24,344]{1,0:T(8,128)S(1)} %get-tuple-element.32) | copy-start | bytes 99076
  53.6 112.1 %copy-start.2 = (f32[24,344]{1,0:T(8,128)}, f32[24,344]{1,0:T(8,128)S(1)}, u32[]{:S(2)}) copy-start(f32[24,344]{1,0:T(8,128)S(1)} %get-tuple-element.33) | copy-start | bytes 99076
Sparse Core Ops, SparseCore 0:
  104.0 53.6 all-gather.2
